TPU v7x, 512 devices: a whole 4x4x16 slice. The times are simulated.
512 devices in a mesh: dp: 8 (over z_hi, core), dom: 64 (over x, z_lo, y).
Axes of the slice: x: 4, y: 4, z: 16 (z_hi: 4, z_lo: 4; z = z_hi * 4 + z_lo), core: 2. Of those that a mesh axis runs over, the one named last changes fastest.
Arguments:
- density: bfloat16 [8, 64, 512, 256], P('dp', None, 'dom'), may hold values from -6 to 6
- upstream: bfloat16 [8, 64, 512, 256], P('dp', None, 'dom'), may hold values from -6 to 6
- spectral_weight: float32 [2048, 64], P(('dp', 'dom')), may hold values from -0.5 to 0.5
- moment_one: float32 [2048, 64], P(('dp', 'dom')), may hold values from -128 to 128
- moment_two: float32 [2048, 64], P(('dp', 'dom')), may hold values from 256 to 4096
- skip_weight: bfloat16 [64, 64], replicated, may hold values from -0.75 to 0.75
- skip_bias: float32 [64], replicated, may hold values from -3 to 3
- mode_counts: int32 [8], replicated, may hold values from 8 to 16, as said below
Outputs:
- input_grad: bfloat16 [8, 64, 512, 256], P('dp', None, 'dom')
- new_weight: float32 [2048, 64], P(('dp', 'dom'))
- new_moment_one: float32 [2048, 64], P(('dp', 'dom'))
- new_moment_two: float32 [2048, 64], P(('dp', 'dom'))
Inputs may be any that keep to these rules, and one draw needn't show every extreme that they name: `mode_counts`: some entry equals 16.
All inputs are finite; a program needn't handle non-finite values.
Results may differ from a plain program's by a relative error of at most 0.0053.
Values may be sent and summed in bfloat16 or wider, within the bound.
No kernel may reach another device: no remote copies, remote signals or barrier semaphores. Data moves between devices by JAX's collectives and lax.ppermute only.
A program may use at most 64 MiB of HBM per device.

v0:
```python
import math

import jax
import jax.numpy as jnp
from jax import lax
from jax.sharding import PartitionSpec as P

MODES = 16
STEP = 10


learn_rate = 0.01
beta_first = 0.9
beta_second = 0.95
decay_rate = 0.1
epsilon = 1e-08


def joined_along(tiles, dim):
    dims = list(tiles.shape[1:])
    dims[dim] *= tiles.shape[0]
    return jnp.moveaxis(tiles, 0, dim).reshape(dims)


def copy_for_each(shard, axis):
    copies = jnp.broadcast_to(shard, (lax.axis_size(axis), *shard.shape))
    return lax.all_to_all(copies, axis, split_axis=0, concat_axis=0, tiled=True)


def collect(shard, axis, dim):
    return joined_along(copy_for_each(shard, axis), dim)


def in_one_piece(arrays, axis, split_dim, concat_dim, along):
    both = jnp.concatenate(arrays, axis=along)
    result, at, done = (
        lax.all_to_all(both, axis, split_axis=split_dim, concat_axis=concat_dim, tiled=True),
        0,
        [],
    )
    for a in arrays:
        done.append(lax.slice_in_dim(result, at, at + a.shape[along], axis=along))
        at += a.shape[along]
    return tuple(done)


def split_up(shard, dim, length):
    dims = shard.shape
    tiles = shard.reshape(*dims[:dim], length, dims[dim] // length, *dims[dim + 1 :])
    return jnp.moveaxis(tiles, dim, 0)


def sum_at_owner(shard, axis, dim):
    tiles = split_up(shard, dim, lax.axis_size(axis))
    arrived = lax.all_to_all(tiles, axis, split_axis=0, concat_axis=0, tiled=True)
    return arrived.astype(jnp.float32).sum(axis=0)


def summed_on_arrival(shard, axis, dim):
    length = lax.axis_size(axis)
    tiles = lax.all_to_all(split_up(shard, dim, length), axis, 0, 0, tiled=True)
    return jnp.sum(tiles, axis=0)


def axis_parts(count_xdim):
    freq_list = jnp.arange(MODES, dtype=jnp.int32)
    cell_list = jnp.arange(count_xdim, dtype=jnp.int32)
    phases = (
        jnp.mod(freq_list[:, None] * cell_list[None, :], count_xdim).astype(jnp.float32)
        / count_xdim
    )
    angles = 2.0 * math.pi * phases
    scaling = 1.0 / math.sqrt(count_xdim)
    return (
        (jnp.cos(angles) * scaling).astype(jnp.bfloat16),
        (jnp.sin(angles) * scaling).astype(jnp.bfloat16),
    )


def doubling_table():
    return jnp.where(jnp.arange(MODES, dtype=jnp.int32) > 0, 2.0, 1.0).astype(jnp.float32)


def gelu_slope(values):
    cumulative = 0.5 * (1.0 + lax.erf(values * 0.7071067811865476))
    bell_curve = jnp.exp(-0.5 * values * values) * 0.3989422804014327
    return cumulative + values * bell_curve


def forward_parts(field, cosines, sines):
    real_part = jnp.einsum("scxl,fx->slcf", field, cosines, preferred_element_type=jnp.float32)
    imag_part = -jnp.einsum("scxl,fx->slcf", field, sines, preferred_element_type=jnp.float32)
    return (real_part, imag_part)


def inverse_cells(values_real, values_imag, cosines, sines):
    first = jnp.einsum("slcf,fx->scxl", values_real, cosines, preferred_element_type=jnp.float32)
    second = jnp.einsum("slcf,fx->scxl", values_imag, sines, preferred_element_type=jnp.float32)
    return (first - second).astype(jnp.bfloat16)


def on_device(
    density, upstream, spectral_weight, moment_one, moment_two, skip_weight, skip_bias, mode_counts
):
    samples, channels, slab_rows, line_count = density.shape
    count_xdim = slab_rows * lax.axis_size("dom")
    cosines, sines = axis_parts(count_xdim)
    doubling = doubling_table()
    doubling_low = doubling.astype(jnp.bfloat16)
    counts_here = lax.dynamic_slice_in_dim(mode_counts, lax.axis_index("dp") * samples, samples, 0)
    keep_modes = (jnp.arange(MODES, dtype=jnp.int32)[None, :] < counts_here[:, None]).astype(
        jnp.float32
    )
    keep_wide = keep_modes[:, None, None, :]
    weight_short = spectral_weight.astype(jnp.bfloat16)
    group_low = collect(weight_short, "dom", 0)
    weight_low = lax.all_gather(group_low, "dp", axis=0, tiled=True)
    weight_low = weight_low.reshape(2, MODES, channels, channels)
    weight_real = weight_low[0]
    weight_imag = weight_low[1]
    density_lines, upstream_lines = in_one_piece((density, upstream), "dom", 3, 2, 0)
    real_part, imag_part = forward_parts(density_lines, cosines, sines)
    spec_real = real_part.astype(jnp.bfloat16)
    spec_imag = imag_part.astype(jnp.bfloat16)
    form = "slcf,fco->slof"
    mixed_real = jnp.einsum(
        form, spec_real, weight_real, preferred_element_type=jnp.float32
    ) - jnp.einsum(form, spec_imag, weight_imag, preferred_element_type=jnp.float32)
    mixed_imag = jnp.einsum(
        form, spec_imag, weight_real, preferred_element_type=jnp.float32
    ) + jnp.einsum(form, spec_real, weight_imag, preferred_element_type=jnp.float32)
    mixed_real = (mixed_real * keep_wide).astype(jnp.bfloat16) * doubling_low
    mixed_imag = (mixed_imag * keep_wide).astype(jnp.bfloat16) * doubling_low
    back_lines = inverse_cells(mixed_real, mixed_imag, cosines, sines)
    back_rows = lax.optimization_barrier(back_lines)
    skip_part = jnp.einsum(
        "oc,scxl->soxl", skip_weight, density_lines, preferred_element_type=jnp.float32
    )
    before = back_rows.astype(jnp.float32) + skip_part + skip_bias[None, :, None, None]
    gate_lines = (upstream_lines.astype(jnp.float32) * gelu_slope(before)).astype(jnp.bfloat16)
    grad_real, grad_imag = forward_parts(gate_lines, cosines, sines)
    scale = keep_wide * doubling
    grad_real = (grad_real * scale).astype(jnp.bfloat16)
    grad_imag = (grad_imag * scale).astype(jnp.bfloat16)
    outer = "slof,slcf->fco"
    part_real = jnp.einsum(
        outer, grad_real, spec_real, preferred_element_type=jnp.float32
    ) + jnp.einsum(outer, grad_imag, spec_imag, preferred_element_type=jnp.float32)
    part_imag = jnp.einsum(
        outer, grad_imag, spec_real, preferred_element_type=jnp.float32
    ) - jnp.einsum(outer, grad_real, spec_imag, preferred_element_type=jnp.float32)
    grad_local = jnp.stack([part_real, part_imag], 0).reshape(2 * MODES * channels, channels)
    group_grad = sum_at_owner(grad_local.astype(jnp.bfloat16), "dp", 0)
    weight_grad = summed_on_arrival(group_grad, "dom", 0)
    inner = "fco,slof->slcf"
    input_real = jnp.einsum(
        inner, weight_real, grad_real, preferred_element_type=jnp.float32
    ) + jnp.einsum(inner, weight_imag, grad_imag, preferred_element_type=jnp.float32)
    input_imag = jnp.einsum(
        inner, weight_real, grad_imag, preferred_element_type=jnp.float32
    ) - jnp.einsum(inner, weight_imag, grad_real, preferred_element_type=jnp.float32)
    input_lines = inverse_cells(
        input_real.astype(jnp.bfloat16), input_imag.astype(jnp.bfloat16), cosines, sines
    )
    input_rows = lax.optimization_barrier(input_lines)
    skip_back = jnp.einsum(
        "oc,soxl->scxl", skip_weight, gate_lines, preferred_element_type=jnp.float32
    )
    grad_lines = (input_rows.astype(jnp.float32) + skip_back).astype(jnp.bfloat16)
    input_grad = lax.all_to_all(grad_lines, "dom", split_axis=2, concat_axis=3, tiled=True)
    new_moment_one = beta_first * moment_one + (1.0 - beta_first) * weight_grad
    new_moment_two = beta_second * moment_two + (1.0 - beta_second) * weight_grad * weight_grad
    first_hat = new_moment_one / (1.0 - beta_first**STEP)
    second_hat = new_moment_two / (1.0 - beta_second**STEP)
    new_weight = spectral_weight - learn_rate * (
        first_hat / (jnp.sqrt(second_hat) + epsilon) + decay_rate * spectral_weight
    )
    return (input_grad, new_weight, new_moment_one, new_moment_two)


def solution(mesh):
    placed = (
        P("dp", None, "dom", None),
        P("dp", None, "dom", None),
        P(("dp", "dom"), None),
        P(("dp", "dom"), None),
        P(("dp", "dom"), None),
        P(),
        P(),
        P(),
    )
    return jax.shard_map(
        on_device,
        mesh=mesh,
        in_specs=placed,
        out_specs=(
            P("dp", None, "dom", None),
            P(("dp", "dom"), None),
            P(("dp", "dom"), None),
            P(("dp", "dom"), None),
        ),
        check_vma=False,
    )
```

profile of v0, /device:TPU:1, one launch (start us, length us, event | category | flops | bytes accessed | tf_op | source)
XLA Modules:
  0.0 134.6 jit_solution(11157942799677007264)
XLA Ops:
  0.6 0.7 convert_element_type.173
  1.4 0.7 reshape.173
  2.1 12.6 %all-to-all-start.1 = ((bf16[64,2,128]{2,1,0:T(2,128)(2,1)}), bf16[64,2,128]{2,1,0:T(2,128)(2,1)S(1)}, u32[]{:S(2)}, u32[]{:S(2)}) async-start(bf16[64,2,128]{2,1,0:T(2,128)(2,1)} %reshape.173), calls=%async_computation.1 | async-start | bytes 65536 | tf_op jit(solution)/shard_map/all_to_all | solution.py:27
  14.6 1.5 %copy.138 = bf16[1,64,8,256]{1,2,0,3:T(8,128)(2,1)S(1)} copy(bf16[1,64,8,256]{3,2,1,0:T(8,128)(2,1)} %param.9) | data formatting | bytes 524288 | tf_op args[1]
  16.1 0.4 copy.137
  16.5 0.2 fusion.144
  16.8 1.5 %reshape.171 = bf16[64,2,2048]{2,1,0:T(2,128)(2,1)} reshape(bf16[256,2,8,64]{3,2,1,0:T(8,128)(2,1)S(1)} %fusion.144) | data formatting | bytes 1048576
  18.3 5.1 %all-to-all-done.1 = bf16[64,2,128]{2,1,0:T(2,128)(2,1)S(1)} async-done(((bf16[64,2,128]{2,1,0:T(2,128)(2,1)}), bf16[64,2,128]{2,1,0:T(2,128)(2,1)S(1)}, u32[]{:S(2)}, u32[]{:S(2)}) %all-to-all-start.1) | async-done | bytes 32800 | tf_op jit(solution)/shard_map/all_to_all | solution.py:27
  23.4 5.0 %all-to-all-start = ((bf16[64,2,2048]{2,1,0:T(2,128)(2,1)}), bf16[64,2,2048]{2,1,0:T(2,128)(2,1)S(1)}, u32[]{:S(2)}, u32[]{:S(2)}) async-start(bf16[64,2,2048]{2,1,0:T(2,128)(2,1)} %reshape.171), calls=%async_computation | async-start | bytes 1048576 | tf_op jit(solution)/shard_map/all_to_all | solution.py:37
  28.5 0.6 copy-done.5
  29.1 0.6 dynamic_slice.3
  29.7 0.6 compare_convert_fusion
  30.3 0.7 compare_select_fusion.1
  31.0 0.1 reshape.174
  31.1 27.5 %all_gather.3 = bf16[2048,64]{1,0:T(8,128)(2,1)S(1)} all-gather(bf16[256,64]{1,0:T(8,128)(2,1)S(1)} %bitcast.194), channel_id=1, replica_groups=mesh['dp'=8,'dom'=64] {'dp'}, dimensions={0}, use_global_device_ids=true | all-gather | bytes 294912 | tf_op jit(solution)/shard_map/all_gather | solution.py:117
  58.6 0.7 reshape.172
  59.4 0.2 fusion.142
  59.6 0.3 fusion.34
  59.8 0.3 fusion.35
  60.1 0.1 copy.232
  60.2 0.3 copy.151
  60.5 0.2 fusion.97
  60.7 0.2 fusion.91
  60.9 0.2 fusion.32
  61.1 0.3 fusion.67
  61.4 0.2 fusion.33
  61.6 0.3 fusion.11
  62.0 0.3 copy-done.6
  62.3 0.5 fusion.47
  62.7 0.3 fusion.29
  63.0 0.3 fusion.28
  63.3 0.2 fusion.87
  63.5 0.3 fusion.84
  63.8 0.3 fusion.77
  64.1 0.2 fusion.27
  64.3 0.3 fusion.8
  64.6 0.3 fusion.9
  64.9 0.1 pad_maximum_fusion.1
  65.0 0.9 copy.170
  65.9 6.1 %all-to-all-start.3 = ((bf16[8,256,64]{1,2,0:T(8,128)(2,1)}), bf16[8,256,64]{1,2,0:T(8,128)(2,1)S(1)}, u32[]{:S(2)}, u32[]{:S(2)}) async-start(bf16[8,256,64]{1,2,0:T(8,128)(2,1)} %copy.170), calls=%async_computation.3 | async-start | bytes 524288 | tf_op jit(solution)/shard_map/all_to_all | solution.py:55
  72.0 0.2 fusion.80
  72.2 0.3 fusion.26
  72.5 0.4 fusion.64
  72.9 0.3 fusion.10
  73.2 0.3 fusion.3
  73.5 0.3 copy.159
  73.8 1.0 reshape.175
  74.8 13.1 %all-to-all-done.3 = bf16[8,256,64]{1,2,0:T(8,128)(2,1)S(1)} async-done(((bf16[8,256,64]{1,2,0:T(8,128)(2,1)}), bf16[8,256,64]{1,2,0:T(8,128)(2,1)S(1)}, u32[]{:S(2)}, u32[]{:S(2)}) %all-to-all-start.3) | async-done | bytes 262176 | tf_op jit(solution)/shard_map/all_to_all | solution.py:55
  87.9 17.7 %all-to-all-start.2 = ((bf16[64,2,1024]{2,1,0:T(2,128)(2,1)}), bf16[64,2,1024]{2,1,0:T(2,128)(2,1)S(1)}, u32[]{:S(2)}, u32[]{:S(2)}) async-start(bf16[64,2,1024]{2,1,0:T(2,128)(2,1)} %reshape.175), calls=%async_computation.2 | async-start | bytes 524288 | tf_op jit(solution)/shard_map/all_to_all | solution.py:170
  105.6 0.1 copy.171
  105.7 0.8 reshape.177
  106.5 10.1 %all-to-all-done.2 = bf16[64,2,1024]{2,1,0:T(2,128)(2,1)S(1)} async-done(((bf16[64,2,1024]{2,1,0:T(2,128)(2,1)}), bf16[64,2,1024]{2,1,0:T(2,128)(2,1)S(1)}, u32[]{:S(2)}, u32[]{:S(2)}) %all-to-all-start.2) | async-done | bytes 262176 | tf_op jit(solution)/shard_map/all_to_all | solution.py:170
  116.6 6.2 %all-to-all-start.4 = ((f32[64,1,256]{2,1,0:T(1,128)}), f32[64,1,256]{2,1,0:T(1,128)S(1)}, u32[]{:S(2)}, u32[]{:S(2)}) async-start(f32[64,1,256]{2,1,0:T(1,128)} %reshape.177), calls=%async_computation.4 | async-start | bytes 131072 | tf_op jit(solution)/shard_map/all_to_all | solution.py:61
  122.8 0.3 reshape.176
  123.2 0.1 copy.233
  123.2 0.1 copy.161
  123.3 1.1 copy.172
  124.5 7.4 %all-to-all-done.4 = f32[64,1,256]{2,1,0:T(1,128)S(1)} async-done(((f32[64,1,256]{2,1,0:T(1,128)}), f32[64,1,256]{2,1,0:T(1,128)S(1)}, u32[]{:S(2)}, u32[]{:S(2)}) %all-to-all-start.4) | async-done | bytes 65568 | tf_op jit(solution)/shard_map/all_to_all | solution.py:61
  131.9 0.5 broadcast.102
  132.4 0.8 reduce
  133.2 0.1 reshape.178
  133.4 0.1 reduce_sum.19
  133.4 0.6 copy-done.2
  134.0 0.6 multiply_subtract_fusion
  (17 shorter events, 0.2 us)
Async XLA Ops:
  0.6 61.3 %copy-start = (bf16[64,64]{1,0:T(8,128)(2,1)S(1)}, bf16[64,64]{1,0:T(8,128)(2,1)}, u32[]{:S(2)}) copy-start(bf16[64,64]{1,0:T(8,128)(2,1)} %param.13) | copy-start | bytes 24580
  2.1 21.4 %all-to-all-start.1 = ((bf16[64,2,128]{2,1,0:T(2,128)(2,1)}), bf16[64,2,128]{2,1,0:T(2,128)(2,1)S(1)}, u32[]{:S(2)}, u32[]{:S(2)}) async-start(bf16[64,2,128]{2,1,0:T(2,128)(2,1)} %reshape.173), calls=%async_computation.1 | async-start | bytes 65536 | tf_op jit(solution)/shard_map/all_to_all | solution.py:27
  14.6 1.5 %copy-start.1 = (bf16[1,64,8,256]{3,2,1,0:T(8,128)(2,1)S(1)}, bf16[1,64,8,256]{3,2,1,0:T(8,128)(2,1)}, u32[]{:S(2)}) copy-start(bf16[1,64,8,256]{3,2,1,0:T(8,128)(2,1)} %param.8) | copy-start | bytes 786436
  23.4 35.2 %all-to-all-start = ((bf16[64,2,2048]{2,1,0:T(2,128)(2,1)}), bf16[64,2,2048]{2,1,0:T(2,128)(2,1)S(1)}, u32[]{:S(2)}, u32[]{:S(2)}) async-start(bf16[64,2,2048]{2,1,0:T(2,128)(2,1)} %reshape.171), calls=%async_computation | async-start | bytes 1048576 | tf_op jit(solution)/shard_map/all_to_all | solution.py:37
  28.4 0.7 copy-start.5
  61.6 0.7 copy-start.6
  65.9 21.9 %all-to-all-start.3 = ((bf16[8,256,64]{1,2,0:T(8,128)(2,1)}), bf16[8,256,64]{1,2,0:T(8,128)(2,1)S(1)}, u32[]{:S(2)}, u32[]{:S(2)}) async-start(bf16[8,256,64]{1,2,0:T(8,128)(2,1)} %copy.170), calls=%async_computation.3 | async-start | bytes 524288 | tf_op jit(solution)/shard_map/all_to_all | solution.py:55
  87.9 28.8 %all-to-all-start.2 = ((bf16[64,2,1024]{2,1,0:T(2,128)(2,1)}), bf16[64,2,1024]{2,1,0:T(2,128)(2,1)S(1)}, u32[]{:S(2)}, u32[]{:S(2)}) async-start(bf16[64,2,1024]{2,1,0:T(2,128)(2,1)} %reshape.175), calls=%async_computation.2 | async-start | bytes 524288 | tf_op jit(solution)/shard_map/all_to_all | solution.py:170
  116.6 15.2 %all-to-all-start.4 = ((f32[64,1,256]{2,1,0:T(1,128)}), f32[64,1,256]{2,1,0:T(1,128)S(1)}, u32[]{:S(2)}, u32[]{:S(2)}) async-start(f32[64,1,256]{2,1,0:T(1,128)} %reshape.177), calls=%async_computation.4 | async-start | bytes 131072 | tf_op jit(solution)/shard_map/all_to_all | solution.py:61
  133.3 0.7 copy-start.2
  133.3 0.7 copy-start.3
  133.3 0.7 copy-start.4
where the time goes:
time: 136 us; the launch traced here: 135 us
  starting transfers between devices  47.5 us (35%)
  waiting for transfers between devices  35.7 us (26%)
  blocking collectives  27.5 us (20%)
  local copies, waits for them, and re-layouts  12.9 us (9%)
  matrix products  6 us (4%)
  other arithmetic  4.06 us (3%)
    all_gather x1, blocking collectives, on_device(): weight_low = lax.all_gather(group_low, 'dp', axis=0, tiled=True)  27.5 us
    all_to_all x1, starting transfers between devices, on_device(): lax.all_to_all(grad_lines, 'dom', split_axis=2, concat_axis=3, tiled=True)  17.7 us
    all_to_all x1, waiting for transfers between devices, sum_at_owner(): lax.all_to_all(tiles, axis, split_axis=0, concat_axis=0, tiled=True)  13.1 us
    all_to_all x1, starting transfers between devices, copy_for_each(): return lax.all_to_all(copies, axis, split_axis=0, concat_axis=0, tiled=True)  12.6 us
    all_to_all x1, waiting for transfers between devices, on_device(): lax.all_to_all(grad_lines, 'dom', split_axis=2, concat_axis=3, tiled=True)  10.1 us
    unnamed x25, local copies, waits for them, and re-layouts  9.8 us
    all_to_all x1, waiting for transfers between devices, summed_on_arrival(): tiles = lax.all_to_all(split_up(shard, dim, length), axis, 0, 0, tiled=True)  7.4 us
    all_to_all x1, starting transfers between devices, summed_on_arrival(): tiles = lax.all_to_all(split_up(shard, dim, length), axis, 0, 0, tiled=True)  6.18 us
  transfers between devices with their start and end apart: 5, of which 4 were waited for; matrix products, arithmetic and copies ran while one was open for 8% of the time, Pallas kernels for 0%

commit v1 on v0

--- a/solution.py
+++ b/solution.py
@@ -113,8 +113,7 @@
     )
     keep_wide = keep_modes[:, None, None, :]
     weight_short = spectral_weight.astype(jnp.bfloat16)
-    group_low = collect(weight_short, "dom", 0)
-    weight_low = lax.all_gather(group_low, "dp", axis=0, tiled=True)
+    weight_low = lax.all_gather(weight_short, ("dp", "dom"), axis=0, tiled=True)
     weight_low = weight_low.reshape(2, MODES, channels, channels)
     weight_real = weight_low[0]
     weight_imag = weight_low[1]
@@ -150,8 +149,7 @@
         outer, grad_imag, spec_real, preferred_element_type=jnp.float32
     ) - jnp.einsum(outer, grad_real, spec_imag, preferred_element_type=jnp.float32)
     grad_local = jnp.stack([part_real, part_imag], 0).reshape(2 * MODES * channels, channels)
-    group_grad = sum_at_owner(grad_local.astype(jnp.bfloat16), "dp", 0)
-    weight_grad = summed_on_arrival(group_grad, "dom", 0)
+    weight_grad = lax.psum_scatter(grad_local, ("dp", "dom"), scatter_dimension=0, tiled=True)
     inner = "fco,slof->slcf"
     input_real = jnp.einsum(
         inner, weight_real, grad_real, preferred_element_type=jnp.float32

time: 136 us -> 1850 us (13.60)
  blocking collectives: 27.5 us -> 1320 us
  waiting for transfers between devices: 35.7 us -> 472 us
  starting transfers between devices: 47.5 us -> 17.2 us
    all_gather x1, blocking collectives: 27.5 us -> 1320 us  [on_device(): weight_low = lax.all_gather(weight_short, ('dp', 'dom'), axis=0, tiled=True)]
    unnamed x0 -> x2, waiting for transfers between devices: none -> 472 us
    all_to_all x3 -> x0, waiting for transfers between devices: 25.6 us -> none  [the longest x1 13.1 us: sum_at_owner(): lax.all_to_all(tiles, axis, split_axis=0, concat_axis=0, tiled=True)]
    all_to_all x3 -> x0, starting transfers between devices: 24.8 us -> none  [the longest x1 12.6 us: copy_for_each(): return lax.all_to_all(copies, axis, split_axis=0, concat_axis=0, tiled=True)]
  transfers between devices with their start and end apart: 5 -> 3, of which waited for: 4 -> 1; matrix products, arithmetic and copies ran while one was open for 8% -> 0% of each run, Pallas kernels for 0% -> 0%
where the time goes in v1:
time: 1850 us
  blocking collectives  1320 us (71%)
  waiting for transfers between devices  472 us (26%)
    all_gather x1, blocking collectives, on_device(): weight_low = lax.all_gather(weight_short, ('dp', 'dom'), axis=0, tiled=True)  1320 us
    unnamed x2, waiting for transfers between devices  472 us
  transfers between devices with their start and end apart: 3, of which 1 were waited for; matrix products, arithmetic and copies ran while one was open for 0% of the time, Pallas kernels for 0%

profile of v1, /device:TPU:1, one launch (start us, length us, event | category | flops | bytes accessed | tf_op | source)
XLA Modules:
  0.0 1845.9 jit_solution(2929761174149622552)
XLA Ops:
  7.2 0.0 copy-start
  7.2 0.0 copy-start.1
  7.2 1.5 copy.68
  8.7 0.0 copy-done.1
  8.7 0.4 copy.67
  9.1 0.2 fusion.142
  9.3 1.5 reshape.169
  10.9 12.6 all-to-all-start
  23.5 0.0 copy-start.5
  23.5 0.6 copy-done.5
  24.1 0.6 dynamic_slice.3
  24.7 0.7 compare_convert_fusion
  25.4 0.7 compare_select_fusion.1
  26.0 0.0 copy-done.2
  26.1 1322.4 %all-gather = bf16[512,4,64]{2,1,0:T(4,128)(2,1)S(1)} all-gather(bf16[1,4,64]{2,1,0:T(4,128)(2,1)S(1)} %convert_bitcast_fusion), channel_id=1, replica_groups=mesh['dp'=8,'dom'=64] {'dp','dom'}, dimensions={0}, use_global_device_ids=true | all-gather | bytes 262656 | tf_op jit(solution)/shard_map/all_gather | solution.py:116
  1348.4 0.2 fusion.141
  1348.6 0.0 all-to-all-done
  1348.6 0.7 reshape.170
  1349.3 0.1 copy.69
  1349.4 0.2 fusion.140
  1349.6 0.3 fusion.32
  1349.9 0.3 fusion.33
  1350.1 0.1 copy.160
  1350.2 0.3 copy.81
  1350.5 0.2 fusion.95
  1350.7 0.2 fusion.89
  1350.9 0.2 fusion.30
  1351.1 0.3 fusion.65
  1351.4 0.2 fusion.31
  1351.6 0.0 copy-start.6
  1351.6 0.3 fusion.9
  1352.0 0.0 copy-done
  1352.0 0.3 copy-done.6
  1352.3 0.5 fusion.45
  1352.8 0.3 fusion.27
  1353.0 0.3 fusion.26
  1353.3 0.2 fusion.78
  1353.5 0.3 fusion.75
  1353.8 0.2 fusion.85
  1354.1 0.3 fusion.25
  1354.3 0.4 fusion.62
  1354.7 0.2 fusion.24
  1354.9 0.4 fusion.8
  1355.3 0.3 fusion.5
  1355.6 0.3 copy.89
  1355.9 1.0 reshape.171
  1356.9 4.6 all-to-all-start.1
  1361.5 0.0 all-reduce.3.cloned.1.call-start
  1361.6 0.3 fusion
  1361.9 0.3 fusion.82
  1362.1 0.3 fusion.1
  1362.4 1.1 pad_maximum_fusion.1
  1363.5 0.0 all-reduce.3.cloned.1.call-update
  1363.6 0.0 copy-start.3
  1363.6 0.0 copy-start.4
  1363.6 472.5 %all-reduce.3.cloned.1.call-done = f32[2048,64]{1,0:T(8,128)} async-done(((f32[2048,64]{1,0:T(8,128)}), f32[2048,64]{1,0:T(8,128)}) %all-reduce.3.cloned.1.call-update) | async-done | bytes 524304
  1836.1 0.0 copy-done.3
  1836.1 0.0 copy-done.4
  1836.1 1.3 multiply_subtract_fusion
  1837.4 0.0 all-to-all-done.1
  1837.4 0.3 reshape.172
  1837.7 0.1 copy.161
  1837.8 0.1 copy.91
  1837.9 1.1 copy.100
  (3 shorter events, 0.0 us)
Async XLA Ops:
  7.2 1344.8 %copy-start = (bf16[64,64]{1,0:T(8,128)(2,1)S(1)}, bf16[64,64]{1,0:T(8,128)(2,1)}, u32[]{:S(2)}) copy-start(bf16[64,64]{1,0:T(8,128)(2,1)} %param.13) | copy-start | bytes 24580
  7.2 1.5 copy-start.1
  10.9 1337.7 %all-to-all-start = ((bf16[64,2,2048]{2,1,0:T(2,128)(2,1)}), bf16[64,2,2048]{2,1,0:T(2,128)(2,1)S(1)}, u32[]{:S(2)}, u32[]{:S(2)}) async-start(bf16[64,2,2048]{2,1,0:T(2,128)(2,1)} %reshape.169), calls=%async_computation | async-start | bytes 1048576 | tf_op jit(solution)/shard_map/all_to_all | solution.py:37
  23.5 0.7 copy-start.5
  24.7 1.3 copy-start.2
  1351.6 0.7 copy-start.6
  1356.9 480.5 %all-to-all-start.1 = ((bf16[64,2,1024]{2,1,0:T(2,128)(2,1)}), bf16[64,2,1024]{2,1,0:T(2,128)(2,1)S(1)}, u32[]{:S(2)}, u32[]{:S(2)}) async-start(bf16[64,2,1024]{2,1,0:T(2,128)(2,1)} %reshape.171), calls=%async_computation.1 | async-start | bytes 524288 | tf_op jit(solution)/shard_map/all_to_all | solution.py:168
  1361.5 474.5 %all-reduce.3.cloned.1.call-start = ((), (), s32[]{:S(2)}) async-start(), calls=%async_computation.2 | async-start | bytes 2097152
  1363.6 472.5 %copy-start.3 = (f32[4,64]{1,0:T(4,128)S(1)}, f32[4,64]{1,0:T(4,128)}, u32[]{:S(2)}) copy-start(f32[4,64]{1,0:T(4,128)} %param.11) | copy-start | bytes 3076
  1363.6 472.5 %copy-start.4 = (f32[4,64]{1,0:T(4,128)S(1)}, f32[4,64]{1,0:T(4,128)}, u32[]{:S(2)}) copy-start(f32[4,64]{1,0:T(4,128)} %param.12) | copy-start | bytes 3076
Sparse Core Ops, SparseCore 0:
  1367.8 468.1 all-reduce.2

commit v2 on v1

--- a/solution.py
+++ b/solution.py
@@ -99,11 +99,35 @@
     return (first - second).astype(jnp.bfloat16)
 
 
+def gather_over_dp(rows):
+    count = lax.axis_size("dp")
+    pairs = lambda k: [(i, (i + k) % count) for i in range(count)]
+    here = lax.axis_index("dp")
+    pieces = [rows] + [lax.ppermute(rows, "dp", pairs(k)) for k in range(1, count)]
+    stacked = jnp.stack(pieces, 0)
+    order = (here - jnp.arange(count)) % count
+    return jnp.take(stacked, order, axis=0)
+
+
+def scatter_sum_over_dp(blocks):
+    count = lax.axis_size("dp")
+    pairs = lambda k: [(i, (i + k) % count) for i in range(count)]
+    here = lax.axis_index("dp")
+    total = lax.dynamic_index_in_dim(blocks, here, 0, keepdims=False)
+    for k in range(1, count):
+        sent = lax.dynamic_index_in_dim(blocks, (here + k) % count, 0, keepdims=False)
+        total = total + lax.ppermute(sent, "dp", pairs(k))
+    return total
+
+
 def on_device(
     density, upstream, spectral_weight, moment_one, moment_two, skip_weight, skip_bias, mode_counts
 ):
     samples, channels, slab_rows, line_count = density.shape
-    count_xdim = slab_rows * lax.axis_size("dom")
+    slabs = lax.axis_size("dom")
+    groups = lax.axis_size("dp")
+    count_xdim = slab_rows * slabs
+    lines_here = line_count // slabs
     cosines, sines = axis_parts(count_xdim)
     doubling = doubling_table()
     doubling_low = doubling.astype(jnp.bfloat16)
@@ -112,12 +136,30 @@
         jnp.float32
     )
     keep_wide = keep_modes[:, None, None, :]
+    rows_here = spectral_weight.shape[0]
     weight_short = spectral_weight.astype(jnp.bfloat16)
-    weight_low = lax.all_gather(weight_short, ("dp", "dom"), axis=0, tiled=True)
-    weight_low = weight_low.reshape(2, MODES, channels, channels)
+    group_rows = gather_over_dp(weight_short).reshape(1, groups * rows_here * channels)
+
+    def to_tiles(field):
+        tiles = field.reshape(samples, channels, slab_rows, slabs, lines_here)
+        return jnp.moveaxis(tiles, 3, 0).reshape(slabs, -1)
+
+    def from_tiles(tiles):
+        field = tiles.reshape(slabs, samples, channels, slab_rows, lines_here)
+        return jnp.moveaxis(field, 0, 2).reshape(samples, channels, count_xdim, lines_here)
+
+    size = samples * channels * slab_rows * lines_here
+    outgoing = jnp.concatenate(
+        [to_tiles(density), to_tiles(upstream), jnp.broadcast_to(group_rows, (slabs, group_rows.shape[1]))],
+        axis=1,
+    )
+    arrived = lax.all_to_all(outgoing, "dom", 0, 0, tiled=True)
+    density_lines = from_tiles(arrived[:, :size])
+    upstream_lines = from_tiles(arrived[:, size : 2 * size])
+    weight_rows = arrived[:, 2 * size :].reshape(slabs, groups, rows_here, channels)
+    weight_low = jnp.moveaxis(weight_rows, 0, 1).reshape(2, MODES, channels, channels)
     weight_real = weight_low[0]
     weight_imag = weight_low[1]
-    density_lines, upstream_lines = in_one_piece((density, upstream), "dom", 3, 2, 0)
     real_part, imag_part = forward_parts(density_lines, cosines, sines)
     spec_real = real_part.astype(jnp.bfloat16)
     spec_imag = imag_part.astype(jnp.bfloat16)
@@ -148,8 +190,8 @@
     part_imag = jnp.einsum(
         outer, grad_imag, spec_real, preferred_element_type=jnp.float32
     ) - jnp.einsum(outer, grad_real, spec_imag, preferred_element_type=jnp.float32)
-    grad_local = jnp.stack([part_real, part_imag], 0).reshape(2 * MODES * channels, channels)
-    weight_grad = lax.psum_scatter(grad_local, ("dp", "dom"), scatter_dimension=0, tiled=True)
+    grad_local = jnp.stack([part_real, part_imag], 0).reshape(groups, slabs, rows_here, channels)
+    grad_tiles = jnp.moveaxis(grad_local.astype(jnp.bfloat16), 1, 0).reshape(slabs, -1)
     inner = "fco,slof->slcf"
     input_real = jnp.einsum(
         inner, weight_real, grad_real, preferred_element_type=jnp.float32
@@ -165,7 +207,15 @@
         "oc,soxl->scxl", skip_weight, gate_lines, preferred_element_type=jnp.float32
     )
     grad_lines = (input_rows.astype(jnp.float32) + skip_back).astype(jnp.bfloat16)
-    input_grad = lax.all_to_all(grad_lines, "dom", split_axis=2, concat_axis=3, tiled=True)
+    line_tiles = grad_lines.reshape(samples, channels, slabs, slab_rows, lines_here)
+    line_tiles = jnp.moveaxis(line_tiles, 2, 0).reshape(slabs, -1)
+    returned = lax.all_to_all(
+        jnp.concatenate([line_tiles, grad_tiles], axis=1), "dom", 0, 0, tiled=True
+    )
+    input_grad = returned[:, :size].reshape(slabs, samples, channels, slab_rows, lines_here)
+    input_grad = jnp.moveaxis(input_grad, 0, 3).reshape(samples, channels, slab_rows, line_count)
+    group_grad = returned[:, size:].astype(jnp.float32).reshape(slabs, groups, rows_here, channels)
+    weight_grad = scatter_sum_over_dp(group_grad.sum(axis=0))
     new_moment_one = beta_first * moment_one + (1.0 - beta_first) * weight_grad
     new_moment_two = beta_second * moment_two + (1.0 - beta_second) * weight_grad * weight_grad
     first_hat = new_moment_one / (1.0 - beta_first**STEP)

time: 1850 us -> 184 us (0.10)
  blocking collectives: 1320 us -> 0 us
  waiting for transfers between devices: 472 us -> 42.9 us
  starting transfers between devices: 17.2 us -> 94.6 us
    all_gather x1 -> x0, blocking collectives: 1320 us -> none  [on_device(): weight_low = lax.all_gather(weight_short, ('dp', 'dom'), axis=0, tiled=True)]
    unnamed x2 -> x0, waiting for transfers between devices: 472 us -> none
    ppermute x0 -> x14, starting transfers between devices: none -> 80.8 us  [the longest x7 44.8 us: gather_over_dp(): lax.ppermute(rows, 'dp', pairs(k))]
    all_to_all x2, waiting for transfers between devices: 0.01 us -> 38.2 us  [the longest x1 20.9 us: on_device(): arrived = lax.all_to_all(outgoing, 'dom', 0, 0, tiled=True)]
  transfers between devices with their start and end apart: 3 -> 16, of which waited for: 1 -> 4; matrix products, arithmetic and copies ran while one was open for 0% -> 5% of each run, Pallas kernels for 0% -> 0%
where the time goes in v2:
time: 184 us; the launch traced here: 182 us
  starting transfers between devices  94.6 us (51%)
  waiting for transfers between devices  42.9 us (23%)
  local copies, waits for them, and re-layouts  23.4 us (13%)
  other arithmetic  13.3 us (7%)
  matrix products  6.01 us (3%)
    ppermute x7, starting transfers between devices, gather_over_dp(): lax.ppermute(rows, 'dp', pairs(k))  44.8 us
    ppermute x7, starting transfers between devices, scatter_sum_over_dp(): total = total + lax.ppermute(sent, 'dp', pairs(k))  36 us
    all_to_all x1, waiting for transfers between devices, on_device(): arrived = lax.all_to_all(outgoing, 'dom', 0, 0, tiled=True)  20.9 us
    all_to_all x1, waiting for transfers between devices, on_device(): lax.all_to_all(jnp.concatenate([line_tiles, grad_tiles], axis=1), 'dom',...  17.2 us
    all_to_all x1, starting transfers between devices, on_device(): arrived = lax.all_to_all(outgoing, 'dom', 0, 0, tiled=True)  9.21 us
    unnamed x29, local copies, waits for them, and re-layouts  7.87 us
    all_to_all x2, other arithmetic, on_device(): arrived = lax.all_to_all(outgoing, 'dom', 0, 0, tiled=True)  7.34 us
    all_to_all x1, starting transfers between devices, on_device(): lax.all_to_all(jnp.concatenate([line_tiles, grad_tiles], axis=1), 'dom',...  4.63 us
  transfers between devices with their start and end apart: 16, of which 4 were waited for; matrix products, arithmetic and copies ran while one was open for 5% of the time, Pallas kernels for 0%

profile of v2, /device:TPU:1, one launch (start us, length us, event | category | flops | bytes accessed | tf_op | source)
XLA Modules:
  0.0 181.6 jit_solution(1127113478800155602)
XLA Ops:
  0.7 0.7 constant_dynamic-update-slice_fusion.7
  1.4 10.2 %collective-permute-start = (bf16[4,64]{1,0:T(4,128)(2,1)S(1)}, bf16[4,64]{1,0:T(4,128)(2,1)S(1)}, u32[]{:S(2)}, u32[]{:S(2)}) collective-permute-start(bf16[4,64]{1,0:T(4,128)(2,1)S(1)} %get-tuple-element.16), channel_id=1, source_target_pairs={{0,64},{64,128},{128,192},{192,256},{256,320},{320,384},{384,448},... | collective-permute-start | bytes 1544 | tf_op jit(solution)/shard_map/ppermute | solution.py:106
  11.6 8.8 %collective-permute-start.1 = (bf16[4,64]{1,0:T(4,128)(2,1)S(1)}, bf16[4,64]{1,0:T(4,128)(2,1)S(1)}, u32[]{:S(2)}, u32[]{:S(2)}) collective-permute-start(bf16[4,64]{1,0:T(4,128)(2,1)S(1)} %get-tuple-element.16), channel_id=1, source_target_pairs={{0,128},{64,192},{128,256},{192,320},{256,384},{320,448},{384,0},{... | collective-permute-start | bytes 1544 | tf_op jit(solution)/shard_map/ppermute | solution.py:106
  20.4 4.0 %collective-permute-start.2 = (bf16[4,64]{1,0:T(4,128)(2,1)S(1)}, bf16[4,64]{1,0:T(4,128)(2,1)S(1)}, u32[]{:S(2)}, u32[]{:S(2)}) collective-permute-start(bf16[4,64]{1,0:T(4,128)(2,1)S(1)} %get-tuple-element.16), channel_id=1, source_target_pairs={{0,192},{64,256},{128,320},{192,384},{256,448},{320,0},{384,64},{4... | collective-permute-start | bytes 1544 | tf_op jit(solution)/shard_map/ppermute | solution.py:106
  24.4 3.4 %collective-permute-start.3 = (bf16[4,64]{1,0:T(4,128)(2,1)S(1)}, bf16[4,64]{1,0:T(4,128)(2,1)S(1)}, u32[]{:S(2)}, u32[]{:S(2)}) collective-permute-start(bf16[4,64]{1,0:T(4,128)(2,1)S(1)} %get-tuple-element.16), channel_id=1, source_target_pairs={{0,256},{64,320},{128,384},{192,448},{256,0},{320,64},{384,128},{4... | collective-permute-start | bytes 1544 | tf_op jit(solution)/shard_map/ppermute | solution.py:106
  27.8 6.3 %collective-permute-start.4 = (bf16[4,64]{1,0:T(4,128)(2,1)S(1)}, bf16[4,64]{1,0:T(4,128)(2,1)S(1)}, u32[]{:S(2)}, u32[]{:S(2)}) collective-permute-start(bf16[4,64]{1,0:T(4,128)(2,1)S(1)} %get-tuple-element.16), channel_id=1, source_target_pairs={{0,320},{64,384},{128,448},{192,0},{256,64},{320,128},{384,192},{4... | collective-permute-start | bytes 1544 | tf_op jit(solution)/shard_map/ppermute | solution.py:106
  34.2 1.4 copy.73
  35.6 1.1 copy.74
  36.7 0.4 copy.75
  37.1 1.1 copy.76
  38.2 7.1 %collective-permute-start.5 = (bf16[4,64]{1,0:T(4,128)(2,1)S(1)}, bf16[4,64]{1,0:T(4,128)(2,1)S(1)}, u32[]{:S(2)}, u32[]{:S(2)}) collective-permute-start(bf16[4,64]{1,0:T(4,128)(2,1)S(1)} %get-tuple-element.16), channel_id=1, source_target_pairs={{0,384},{64,448},{128,0},{192,64},{256,128},{320,192},{384,256},{4... | collective-permute-start | bytes 1544 | tf_op jit(solution)/shard_map/ppermute | solution.py:106
  45.3 5.0 %collective-permute-start.6 = (bf16[4,64]{1,0:T(4,128)(2,1)S(1)}, bf16[4,64]{1,0:T(4,128)(2,1)S(1)}, u32[]{:S(2)}, u32[]{:S(2)}) collective-permute-start(bf16[4,64]{1,0:T(4,128)(2,1)S(1)} %get-tuple-element.16), channel_id=1, source_target_pairs={{0,448},{64,0},{128,64},{192,128},{256,192},{320,256},{384,320},{4... | collective-permute-start | bytes 1544 | tf_op jit(solution)/shard_map/ppermute | solution.py:106
  50.5 3.7 %collective-permute-done.6 = bf16[4,64]{1,0:T(4,128)(2,1)S(1)} collective-permute-done((bf16[4,64]{1,0:T(4,128)(2,1)S(1)}, bf16[4,64]{1,0:T(4,128)(2,1)S(1)}, u32[]{:S(2)}, u32[]{:S(2)}) %collective-permute-start.6) | collective-permute-done | bytes 544 | tf_op jit(solution)/shard_map/ppermute | solution.py:106
  54.1 0.6 gather_fusion
  54.9 5.1 %maximum_bitcast_fusion = bf16[64,1,6144]{0,2,1:T(8,128)(2,1)S(1)} fusion(bf16[64,2048]{0,1:T(8,128)(2,1)S(1)} %bitcast.251, bf16[64,2048]{0,1:T(8,128)(2,1)S(1)} %bitcast.250, bf16[6144]{0:T(1024)(128)(2,1)S(1)} %pad.6.clone), kind=kLoop, calls=%fused_computation.1 | loop fusion | flops 2359296 | bytes 1323008 | tf_op jit(solution)/shard_map/all_to_all | solution.py:156
  60.0 0.5 broadcast.220
  60.5 2.3 %reduce.1 = bf16[64,6144]{0,1:T(8,128)(2,1)S(1)} reduce(bf16[64,1,6144]{0,2,1:T(8,128)(2,1)S(1)} %maximum_bitcast_fusion, bf16[]{:T(256)} %broadcast.220), dimensions={1}, to_apply=%copy.77.reduce_sub_computation | reduce | bytes 1572866 | tf_op jit(solution)/shard_map/all_to_all | solution.py:156
  62.8 0.7 copy.165
  63.4 1.5 reshape.292
  64.9 9.2 %all-to-all-start = ((bf16[64,2,3072]{2,1,0:T(2,128)(2,1)}), bf16[64,2,3072]{2,1,0:T(2,128)(2,1)S(1)}, u32[]{:S(2)}, u32[]{:S(2)}) async-start(bf16[64,2,3072]{2,1,0:T(2,128)(2,1)} %reshape.292), calls=%async_computation | async-start | bytes 1572864 | tf_op jit(solution)/shard_map/all_to_all | solution.py:156
  74.1 0.6 dynamic_slice.28
  74.7 0.6 compare_convert_fusion
  75.4 0.7 compare_select_fusion.7
  76.0 20.9 %all-to-all-done = bf16[64,2,3072]{2,1,0:T(2,128)(2,1)S(1)} async-done(((bf16[64,2,3072]{2,1,0:T(2,128)(2,1)}), bf16[64,2,3072]{2,1,0:T(2,128)(2,1)S(1)}, u32[]{:S(2)}, u32[]{:S(2)}) %all-to-all-start) | async-done | bytes 786464 | tf_op jit(solution)/shard_map/all_to_all | solution.py:156
  97.0 0.6 reshape.293
  97.6 1.5 copy.78
  99.1 0.9 fusion.148
  100.0 1.8 copy.82
  101.8 0.3 fusion.35
  102.4 0.8 copy.121
  104.3 0.3 fusion.64
  104.6 0.3 fusion.11
  105.0 1.8 copy.79
  106.8 1.5 copy.93
  108.4 0.5 fusion.47
  109.1 0.3 fusion.29
  109.6 0.3 fusion.81
  110.1 0.3 fusion.74
  110.9 0.4 fusion.61
  111.3 0.3 fusion.10
  111.6 0.3 fusion.3
  111.9 0.3 copy.101
  112.2 1.0 copy.102
  113.2 0.3 fusion.9
  113.5 0.3 fusion.8
  113.9 0.3 copy.123
  114.4 1.7 reduce.2
  116.1 0.3 copy.166
  116.5 1.2 reshape.294
  117.6 4.6 %all-to-all-start.1 = ((bf16[64,2,2048]{2,1,0:T(2,128)(2,1)}), bf16[64,2,2048]{2,1,0:T(2,128)(2,1)S(1)}, u32[]{:S(2)}, u32[]{:S(2)}) async-start(bf16[64,2,2048]{2,1,0:T(2,128)(2,1)} %reshape.294), calls=%async_computation.1 | async-start | bytes 1048576 | tf_op jit(solution)/shard_map/all_to_all | solution.py:212
  122.4 17.2 %all-to-all-done.1 = bf16[64,2,2048]{2,1,0:T(2,128)(2,1)S(1)} async-done(((bf16[64,2,2048]{2,1,0:T(2,128)(2,1)}), bf16[64,2,2048]{2,1,0:T(2,128)(2,1)S(1)}, u32[]{:S(2)}, u32[]{:S(2)}) %all-to-all-start.1) | async-done | bytes 524320 | tf_op jit(solution)/shard_map/all_to_all | solution.py:212
  139.6 0.5 reshape.295
  140.2 1.1 copy.114
  141.6 6.0 %collective-permute-start.10 = (f32[4,64]{1,0:T(4,128)S(1)}, f32[4,64]{1,0:T(4,128)S(1)}, u32[]{:S(2)}, u32[]{:S(2)}) collective-permute-start(f32[4,64]{1,0:T(4,128)S(1)} %get-tuple-element.26), channel_id=1, source_target_pairs={{0,256},{64,320},{128,384},{192,448},{256,0},{320,64},{384,128},{4... | collective-permute-start | bytes 3080 | tf_op jit(solution)/shard_map/ppermute | solution.py:119
  147.6 5.8 %collective-permute-start.11 = (f32[4,64]{1,0:T(4,128)S(1)}, f32[4,64]{1,0:T(4,128)S(1)}, u32[]{:S(2)}, u32[]{:S(2)}) collective-permute-start(f32[4,64]{1,0:T(4,128)S(1)} %get-tuple-element.25), channel_id=1, source_target_pairs={{0,320},{64,384},{128,448},{192,0},{256,64},{320,128},{384,192},{4... | collective-permute-start | bytes 3080 | tf_op jit(solution)/shard_map/ppermute | solution.py:119
  153.4 6.4 %collective-permute-start.12 = (f32[4,64]{1,0:T(4,128)S(1)}, f32[4,64]{1,0:T(4,128)S(1)}, u32[]{:S(2)}, u32[]{:S(2)}) collective-permute-start(f32[4,64]{1,0:T(4,128)S(1)} %get-tuple-element.24), channel_id=1, source_target_pairs={{0,384},{64,448},{128,0},{192,64},{256,128},{320,192},{384,256},{4... | collective-permute-start | bytes 3080 | tf_op jit(solution)/shard_map/ppermute | solution.py:119
  159.8 3.5 %collective-permute-start.13 = (f32[4,64]{1,0:T(4,128)S(1)}, f32[4,64]{1,0:T(4,128)S(1)}, u32[]{:S(2)}, u32[]{:S(2)}) collective-permute-start(f32[4,64]{1,0:T(4,128)S(1)} %get-tuple-element.23), channel_id=1, source_target_pairs={{0,448},{64,0},{128,64},{192,128},{256,192},{320,256},{384,320},{4... | collective-permute-start | bytes 3080 | tf_op jit(solution)/shard_map/ppermute | solution.py:119
  163.4 6.0 %collective-permute-start.7 = (f32[4,64]{1,0:T(4,128)S(1)}, f32[4,64]{1,0:T(4,128)S(1)}, u32[]{:S(2)}, u32[]{:S(2)}) collective-permute-start(f32[4,64]{1,0:T(4,128)S(1)} %get-tuple-element.22), channel_id=1, source_target_pairs={{0,64},{64,128},{128,192},{192,256},{256,320},{320,384},{384,448},... | collective-permute-start | bytes 3080 | tf_op jit(solution)/shard_map/ppermute | solution.py:119
  169.3 2.8 %collective-permute-start.8 = (f32[4,64]{1,0:T(4,128)S(1)}, f32[4,64]{1,0:T(4,128)S(1)}, u32[]{:S(2)}, u32[]{:S(2)}) collective-permute-start(f32[4,64]{1,0:T(4,128)S(1)} %get-tuple-element.28), channel_id=1, source_target_pairs={{0,128},{64,192},{128,256},{192,320},{256,384},{320,448},{384,0},{... | collective-permute-start | bytes 3080 | tf_op jit(solution)/shard_map/ppermute | solution.py:119
  172.1 5.5 %collective-permute-start.9 = (f32[4,64]{1,0:T(4,128)S(1)}, f32[4,64]{1,0:T(4,128)S(1)}, u32[]{:S(2)}, u32[]{:S(2)}) collective-permute-start(f32[4,64]{1,0:T(4,128)S(1)} %get-tuple-element.27), channel_id=1, source_target_pairs={{0,192},{64,256},{128,320},{192,384},{256,448},{320,0},{384,64},{4... | collective-permute-start | bytes 3080 | tf_op jit(solution)/shard_map/ppermute | solution.py:119
  177.7 1.1 copy.115
  178.7 1.1 copy.116
  179.9 1.0 collective-permute-done.9
  180.9 0.6 multiply_subtract_fusion
  (58 shorter events, 3.6 us)
Async XLA Ops:
  0.6 107.7 %copy-start = (bf16[64,64]{1,0:T(8,128)(2,1)S(1)}, bf16[64,64]{1,0:T(8,128)(2,1)}, u32[]{:S(2)}) copy-start(bf16[64,64]{1,0:T(8,128)(2,1)} %param.13) | copy-start | bytes 24580
  0.6 36.1 %copy-start.1 = (bf16[1,64,8,256]{3,2,1,0:T(8,128)(2,1)S(1)}, bf16[1,64,8,256]{3,2,1,0:T(8,128)(2,1)}, u32[]{:S(2)}) copy-start(bf16[1,64,8,256]{3,2,1,0:T(8,128)(2,1)} %param.9) | copy-start | bytes 786436
  1.4 36.8 %collective-permute-start = (bf16[4,64]{1,0:T(4,128)(2,1)S(1)}, bf16[4,64]{1,0:T(4,128)(2,1)S(1)}, u32[]{:S(2)}, u32[]{:S(2)}) collective-permute-start(bf16[4,64]{1,0:T(4,128)(2,1)S(1)} %get-tuple-element.16), channel_id=1, source_target_pairs={{0,64},{64,128},{128,192},{192,256},{256,320},{320,384},{384,448},... | collective-permute-start | bytes 1544 | tf_op jit(solution)/shard_map/ppermute | solution.py:106
  11.6 33.7 %collective-permute-start.1 = (bf16[4,64]{1,0:T(4,128)(2,1)S(1)}, bf16[4,64]{1,0:T(4,128)(2,1)S(1)}, u32[]{:S(2)}, u32[]{:S(2)}) collective-permute-start(bf16[4,64]{1,0:T(4,128)(2,1)S(1)} %get-tuple-element.16), channel_id=1, source_target_pairs={{0,128},{64,192},{128,256},{192,320},{256,384},{320,448},{384,0},{... | collective-permute-start | bytes 1544 | tf_op jit(solution)/shard_map/ppermute | solution.py:106
  20.4 30.0 %collective-permute-start.2 = (bf16[4,64]{1,0:T(4,128)(2,1)S(1)}, bf16[4,64]{1,0:T(4,128)(2,1)S(1)}, u32[]{:S(2)}, u32[]{:S(2)}) collective-permute-start(bf16[4,64]{1,0:T(4,128)(2,1)S(1)} %get-tuple-element.16), channel_id=1, source_target_pairs={{0,192},{64,256},{128,320},{192,384},{256,448},{320,0},{384,64},{4... | collective-permute-start | bytes 1544 | tf_op jit(solution)/shard_map/ppermute | solution.py:106
  24.4 26.0 %collective-permute-start.3 = (bf16[4,64]{1,0:T(4,128)(2,1)S(1)}, bf16[4,64]{1,0:T(4,128)(2,1)S(1)}, u32[]{:S(2)}, u32[]{:S(2)}) collective-permute-start(bf16[4,64]{1,0:T(4,128)(2,1)S(1)} %get-tuple-element.16), channel_id=1, source_target_pairs={{0,256},{64,320},{128,384},{192,448},{256,0},{320,64},{384,128},{4... | collective-permute-start | bytes 1544 | tf_op jit(solution)/shard_map/ppermute | solution.py:106
  27.8 22.6 %collective-permute-start.4 = (bf16[4,64]{1,0:T(4,128)(2,1)S(1)}, bf16[4,64]{1,0:T(4,128)(2,1)S(1)}, u32[]{:S(2)}, u32[]{:S(2)}) collective-permute-start(bf16[4,64]{1,0:T(4,128)(2,1)S(1)} %get-tuple-element.16), channel_id=1, source_target_pairs={{0,320},{64,384},{128,448},{192,0},{256,64},{320,128},{384,192},{4... | collective-permute-start | bytes 1544 | tf_op jit(solution)/shard_map/ppermute | solution.py:106
  38.2 12.2 %collective-permute-start.5 = (bf16[4,64]{1,0:T(4,128)(2,1)S(1)}, bf16[4,64]{1,0:T(4,128)(2,1)S(1)}, u32[]{:S(2)}, u32[]{:S(2)}) collective-permute-start(bf16[4,64]{1,0:T(4,128)(2,1)S(1)} %get-tuple-element.16), channel_id=1, source_target_pairs={{0,384},{64,448},{128,0},{192,64},{256,128},{320,192},{384,256},{4... | collective-permute-start | bytes 1544 | tf_op jit(solution)/shard_map/ppermute | solution.py:106
  45.3 8.8 %collective-permute-start.6 = (bf16[4,64]{1,0:T(4,128)(2,1)S(1)}, bf16[4,64]{1,0:T(4,128)(2,1)S(1)}, u32[]{:S(2)}, u32[]{:S(2)}) collective-permute-start(bf16[4,64]{1,0:T(4,128)(2,1)S(1)} %get-tuple-element.16), channel_id=1, source_target_pairs={{0,448},{64,0},{128,64},{192,128},{256,192},{320,256},{384,320},{4... | collective-permute-start | bytes 1544 | tf_op jit(solution)/shard_map/ppermute | solution.py:106
  63.4 10.7 %copy-start.5 = (s32[8]{0:T(128)S(1)}, s32[8]{0:T(128)}, u32[]{:S(2)}) copy-start(s32[8]{0:T(128)} %param.15) | copy-start | bytes 100
  64.9 32.1 %all-to-all-start = ((bf16[64,2,3072]{2,1,0:T(2,128)(2,1)}), bf16[64,2,3072]{2,1,0:T(2,128)(2,1)S(1)}, u32[]{:S(2)}, u32[]{:S(2)}) async-start(bf16[64,2,3072]{2,1,0:T(2,128)(2,1)} %reshape.292), calls=%async_computation | async-start | bytes 1572864 | tf_op jit(solution)/shard_map/all_to_all | solution.py:156
  105.0 3.4 %copy-start.6 = (f32[64]{0:T(128)S(1)}, f32[64]{0:T(128)}, u32[]{:S(2)}) copy-start(f32[64]{0:T(128)} %param.14) | copy-start | bytes 772
  117.6 22.0 %all-to-all-start.1 = ((bf16[64,2,2048]{2,1,0:T(2,128)(2,1)}), bf16[64,2,2048]{2,1,0:T(2,128)(2,1)S(1)}, u32[]{:S(2)}, u32[]{:S(2)}) async-start(bf16[64,2,2048]{2,1,0:T(2,128)(2,1)} %reshape.294), calls=%async_computation.1 | async-start | bytes 1048576 | tf_op jit(solution)/shard_map/all_to_all | solution.py:212
  141.4 39.5 %copy-start.2 = (f32[4,64]{1,0:T(4,128)S(1)}, f32[4,64]{1,0:T(4,128)}, u32[]{:S(2)}) copy-start(f32[4,64]{1,0:T(4,128)} %param.10) | copy-start | bytes 3076
  141.5 39.5 %copy-start.3 = (f32[4,64]{1,0:T(4,128)S(1)}, f32[4,64]{1,0:T(4,128)}, u32[]{:S(2)}) copy-start(f32[4,64]{1,0:T(4,128)} %param.11) | copy-start | bytes 3076
  141.5 39.5 %copy-start.4 = (f32[4,64]{1,0:T(4,128)S(1)}, f32[4,64]{1,0:T(4,128)}, u32[]{:S(2)}) copy-start(f32[4,64]{1,0:T(4,128)} %param.12) | copy-start | bytes 3076
  141.6 27.8 %collective-permute-start.10 = (f32[4,64]{1,0:T(4,128)S(1)}, f32[4,64]{1,0:T(4,128)S(1)}, u32[]{:S(2)}, u32[]{:S(2)}) collective-permute-start(f32[4,64]{1,0:T(4,128)S(1)} %get-tuple-element.26), channel_id=1, source_target_pairs={{0,256},{64,320},{128,384},{192,448},{256,0},{320,64},{384,128},{4... | collective-permute-start | bytes 3080 | tf_op jit(solution)/shard_map/ppermute | solution.py:119
  147.6 24.5 %collective-permute-start.11 = (f32[4,64]{1,0:T(4,128)S(1)}, f32[4,64]{1,0:T(4,128)S(1)}, u32[]{:S(2)}, u32[]{:S(2)}) collective-permute-start(f32[4,64]{1,0:T(4,128)S(1)} %get-tuple-element.25), channel_id=1, source_target_pairs={{0,320},{64,384},{128,448},{192,0},{256,64},{320,128},{384,192},{4... | collective-permute-start | bytes 3080 | tf_op jit(solution)/shard_map/ppermute | solution.py:119
  153.4 26.5 %collective-permute-start.12 = (f32[4,64]{1,0:T(4,128)S(1)}, f32[4,64]{1,0:T(4,128)S(1)}, u32[]{:S(2)}, u32[]{:S(2)}) collective-permute-start(f32[4,64]{1,0:T(4,128)S(1)} %get-tuple-element.24), channel_id=1, source_target_pairs={{0,384},{64,448},{128,0},{192,64},{256,128},{320,192},{384,256},{4... | collective-permute-start | bytes 3080 | tf_op jit(solution)/shard_map/ppermute | solution.py:119
  159.8 20.0 %collective-permute-start.13 = (f32[4,64]{1,0:T(4,128)S(1)}, f32[4,64]{1,0:T(4,128)S(1)}, u32[]{:S(2)}, u32[]{:S(2)}) collective-permute-start(f32[4,64]{1,0:T(4,128)S(1)} %get-tuple-element.23), channel_id=1, source_target_pairs={{0,448},{64,0},{128,64},{192,128},{256,192},{320,256},{384,320},{4... | collective-permute-start | bytes 3080 | tf_op jit(solution)/shard_map/ppermute | solution.py:119
  163.4 16.5 %collective-permute-start.7 = (f32[4,64]{1,0:T(4,128)S(1)}, f32[4,64]{1,0:T(4,128)S(1)}, u32[]{:S(2)}, u32[]{:S(2)}) collective-permute-start(f32[4,64]{1,0:T(4,128)S(1)} %get-tuple-element.22), channel_id=1, source_target_pairs={{0,64},{64,128},{128,192},{192,256},{256,320},{320,384},{384,448},... | collective-permute-start | bytes 3080 | tf_op jit(solution)/shard_map/ppermute | solution.py:119
  169.3 10.5 %collective-permute-start.8 = (f32[4,64]{1,0:T(4,128)S(1)}, f32[4,64]{1,0:T(4,128)S(1)}, u32[]{:S(2)}, u32[]{:S(2)}) collective-permute-start(f32[4,64]{1,0:T(4,128)S(1)} %get-tuple-element.28), channel_id=1, source_target_pairs={{0,128},{64,192},{128,256},{192,320},{256,384},{320,448},{384,0},{... | collective-permute-start | bytes 3080 | tf_op jit(solution)/shard_map/ppermute | solution.py:119
  172.1 8.8 %collective-permute-start.9 = (f32[4,64]{1,0:T(4,128)S(1)}, f32[4,64]{1,0:T(4,128)S(1)}, u32[]{:S(2)}, u32[]{:S(2)}) collective-permute-start(f32[4,64]{1,0:T(4,128)S(1)} %get-tuple-element.27), channel_id=1, source_target_pairs={{0,192},{64,256},{128,320},{192,384},{256,448},{320,0},{384,64},{4... | collective-permute-start | bytes 3080 | tf_op jit(solution)/shard_map/ppermute | solution.py:119

commit v3 on v0

--- a/solution.py
+++ b/solution.py
@@ -149,9 +149,11 @@
     part_imag = jnp.einsum(
         outer, grad_imag, spec_real, preferred_element_type=jnp.float32
     ) - jnp.einsum(outer, grad_real, spec_imag, preferred_element_type=jnp.float32)
-    grad_local = jnp.stack([part_real, part_imag], 0).reshape(2 * MODES * channels, channels)
-    group_grad = sum_at_owner(grad_local.astype(jnp.bfloat16), "dp", 0)
-    weight_grad = summed_on_arrival(group_grad, "dom", 0)
+    groups = lax.axis_size("dp")
+    slabs = lax.axis_size("dom")
+    rows_here = spectral_weight.shape[0]
+    grad_local = jnp.stack([part_real, part_imag], 0).astype(jnp.bfloat16)
+    grad_tiles = jnp.moveaxis(grad_local.reshape(groups, slabs, rows_here, channels), 1, 0)
     inner = "fco,slof->slcf"
     input_real = jnp.einsum(
         inner, weight_real, grad_real, preferred_element_type=jnp.float32
@@ -167,7 +169,24 @@
         "oc,soxl->scxl", skip_weight, gate_lines, preferred_element_type=jnp.float32
     )
     grad_lines = (input_rows.astype(jnp.float32) + skip_back).astype(jnp.bfloat16)
-    input_grad = lax.all_to_all(grad_lines, "dom", split_axis=2, concat_axis=3, tiled=True)
+    lines_here = grad_lines.shape[3]
+    line_tiles = grad_lines.reshape(samples, channels, slabs, slab_rows, lines_here)
+    line_tiles = jnp.moveaxis(line_tiles, 2, 0).reshape(slabs, -1)
+    size = line_tiles.shape[1]
+    returned = lax.all_to_all(
+        jnp.concatenate([line_tiles, grad_tiles.reshape(slabs, -1)], axis=1),
+        "dom",
+        0,
+        0,
+        tiled=True,
+    )
+    input_grad = returned[:, :size].reshape(slabs, samples, channels, slab_rows, lines_here)
+    input_grad = jnp.moveaxis(input_grad, 0, 3).reshape(samples, channels, slab_rows, -1)
+    group_grad = returned[:, size:].astype(jnp.float32).reshape(slabs, groups, rows_here, channels)
+    group_grad = group_grad.sum(axis=0)
+    every_group = lax.all_gather(group_grad, "dp", axis=0, tiled=False)
+    mine = lax.dynamic_index_in_dim(every_group, lax.axis_index("dp"), 1, keepdims=False)
+    weight_grad = mine.sum(axis=0)
     new_moment_one = beta_first * moment_one + (1.0 - beta_first) * weight_grad
     new_moment_two = beta_second * moment_two + (1.0 - beta_second) * weight_grad * weight_grad
     first_hat = new_moment_one / (1.0 - beta_first**STEP)

time: 136 us -> 128 us (0.941)
  blocking collectives: 27.5 us -> 79.7 us
  waiting for transfers between devices: 35.7 us -> 5.15 us
  starting transfers between devices: 47.5 us -> 17.5 us
    all_to_all x0 -> x1, blocking collectives: none -> 31.9 us  [on_device(): lax.all_to_all(jnp.concatenate([line_tiles, grad_tiles.reshape(slabs, -1)...]
    all_to_all x3 -> x0, waiting for transfers between devices: 30.6 us -> none  [the longest x1 13.1 us: sum_at_owner(): lax.all_to_all(tiles, axis, split_axis=0, concat_axis=0, tiled=True)]
    all_to_all x3 -> x0, starting transfers between devices: 30 us -> none  [the longest x1 17.7 us: on_device(): lax.all_to_all(grad_lines, 'dom', split_axis=2, concat_axis=3, tiled=True)]
    all_gather x0 -> x1, blocking collectives: none -> 19.7 us  [on_device(): every_group = lax.all_gather(group_grad, 'dp', axis=0, tiled=False)]
    unnamed x25 -> x24, local copies, waits for them, and re-layouts: 9.8 us -> 7.24 us
    transpose x0 -> x2, local copies, waits for them, and re-layouts: none -> 2.06 us  [the longest x1 1.06 us: on_device(): jnp.moveaxis(input_grad, 0, 3).reshape(samples, channels, slab_rows, -1)]
  transfers between devices with their start and end apart: 5 -> 2, of which waited for: 4 -> 1; matrix products, arithmetic and copies ran while one was open for 8% -> 4% of each run, Pallas kernels for 0% -> 0%
where the time goes in v3:
time: 128 us; the launch traced here: 127 us
  blocking collectives  79.7 us (62%)
  starting transfers between devices  17.5 us (14%)
  local copies, waits for them, and re-layouts  12.7 us (10%)
  matrix products  6.03 us (5%)
  other arithmetic  5.35 us (4%)
  waiting for transfers between devices  5.15 us (4%)
    all_to_all x1, blocking collectives, on_device(): lax.all_to_all(jnp.concatenate([line_tiles, grad_tiles.reshape(slabs, -1)...  31.9 us
    all_gather x1, blocking collectives, on_device(): weight_low = lax.all_gather(group_low, 'dp', axis=0, tiled=True)  28 us
    all_gather x1, blocking collectives, on_device(): every_group = lax.all_gather(group_grad, 'dp', axis=0, tiled=False)  19.7 us
    all_to_all x1, starting transfers between devices, copy_for_each(): return lax.all_to_all(copies, axis, split_axis=0, concat_axis=0, tiled=True)  12.6 us
    unnamed x24, local copies, waits for them, and re-layouts  7.24 us
    all_to_all x1, waiting for transfers between devices, copy_for_each(): return lax.all_to_all(copies, axis, split_axis=0, concat_axis=0, tiled=True)  5.15 us
    all_to_all x1, starting transfers between devices, in_one_piece(): lax.all_to_all(both, axis, split_axis=split_dim, concat_axis=concat_dim,...  4.95 us
  transfers between devices with their start and end apart: 2, of which 1 were waited for; matrix products, arithmetic and copies ran while one was open for 4% of the time, Pallas kernels for 0%

profile of v3, /device:TPU:1, one launch (start us, length us, event | category | flops | bytes accessed | tf_op | source)
XLA Modules:
  0.0 127.4 jit_solution(8795758221071796739)
XLA Ops:
  0.6 0.0 copy-start
  0.7 0.7 convert_element_type.173
  1.4 0.7 reshape.193
  2.1 12.6 %all-to-all-start.1 = ((bf16[64,2,128]{2,1,0:T(2,128)(2,1)}), bf16[64,2,128]{2,1,0:T(2,128)(2,1)S(1)}, u32[]{:S(2)}, u32[]{:S(2)}) async-start(bf16[64,2,128]{2,1,0:T(2,128)(2,1)} %reshape.193), calls=%async_computation.1 | async-start | bytes 65536 | tf_op jit(solution)/shard_map/all_to_all | solution.py:27
  14.7 1.4 %copy.108 = bf16[1,64,8,256]{1,2,0,3:T(8,128)(2,1)S(1)} copy(bf16[1,64,8,256]{3,2,1,0:T(8,128)(2,1)} %param.9) | data formatting | bytes 524288 | tf_op args[1]
  16.1 0.4 copy.107
  16.5 0.2 fusion.144
  16.8 0.0 copy-start.5
  16.8 1.5 %reshape.191 = bf16[64,2,2048]{2,1,0:T(2,128)(2,1)} reshape(bf16[256,2,8,64]{3,2,1,0:T(8,128)(2,1)S(1)} %fusion.144) | data formatting | bytes 1048576
  18.3 5.2 %all-to-all-done.1 = bf16[64,2,128]{2,1,0:T(2,128)(2,1)S(1)} async-done(((bf16[64,2,128]{2,1,0:T(2,128)(2,1)}), bf16[64,2,128]{2,1,0:T(2,128)(2,1)S(1)}, u32[]{:S(2)}, u32[]{:S(2)}) %all-to-all-start.1) | async-done | bytes 32800 | tf_op jit(solution)/shard_map/all_to_all | solution.py:27
  23.5 4.9 %all-to-all-start = ((bf16[64,2,2048]{2,1,0:T(2,128)(2,1)}), bf16[64,2,2048]{2,1,0:T(2,128)(2,1)S(1)}, u32[]{:S(2)}, u32[]{:S(2)}) async-start(bf16[64,2,2048]{2,1,0:T(2,128)(2,1)} %reshape.191), calls=%async_computation | async-start | bytes 1048576 | tf_op jit(solution)/shard_map/all_to_all | solution.py:37
  28.5 0.6 dynamic_slice.7
  29.1 0.6 compare_convert_fusion
  29.7 0.7 compare_select_fusion.1
  30.4 0.1 reshape.194
  30.5 28.0 %all_gather.9 = bf16[2048,64]{1,0:T(8,128)(2,1)S(1)} all-gather(bf16[256,64]{1,0:T(8,128)(2,1)S(1)} %bitcast.202), channel_id=1, replica_groups=mesh['dp'=8,'dom'=64] {'dp'}, dimensions={0}, use_global_device_ids=true | all-gather | bytes 294912 | tf_op jit(solution)/shard_map/all_gather | solution.py:117
  58.5 0.0 all-to-all-done
  58.5 0.7 reshape.192
  59.2 0.1 copy.109
  59.3 0.2 fusion.142
  59.5 0.3 fusion.34
  59.7 0.3 fusion.35
  60.0 0.1 copy.206
  60.1 0.3 copy.121
  60.4 0.2 fusion.97
  60.6 0.2 fusion.91
  60.8 0.2 fusion.32
  61.0 0.3 fusion.67
  61.3 0.2 fusion.33
  61.5 0.3 fusion.11
  61.9 0.5 fusion.47
  62.3 0.3 fusion.28
  62.6 0.3 fusion.29
  62.9 0.3 fusion.84
  63.2 0.2 fusion.87
  63.4 0.3 fusion.77
  63.7 0.2 fusion.80
  63.9 0.3 fusion.8
  64.2 0.3 fusion.9
  64.5 0.1 pad_maximum_fusion.1
  64.6 0.3 copy.151
  65.0 0.2 fusion.27
  65.2 0.4 fusion.64
  65.6 0.2 fusion.26
  65.8 0.4 fusion.10
  66.2 0.3 fusion.3
  66.4 0.3 copy.129
  66.7 1.0 copy.130
  67.7 0.2 maximum_bitcast_fusion
  67.9 0.5 broadcast.102
  68.4 1.7 %reduce.2 = bf16[64,4096]{0,1:T(8,128)(2,1)S(1)} reduce(bf16[64,1,4096]{0,2,1:T(8,128)(2,1)S(1)} %maximum_bitcast_fusion, bf16[]{:T(256)} %broadcast.102), dimensions={1}, to_apply=%copy.141.reduce_sub_computation | reduce | bytes 1048578 | tf_op jit(solution)/shard_map/all_to_all | solution.py:176
  70.2 0.3 copy.207
  70.5 0.4 reshape.195
  70.9 31.9 %all_to_all.32 = bf16[64,2,2048]{2,1,0:T(2,128)(2,1)S(1)} all-to-all(bf16[64,2,2048]{2,1,0:T(2,128)(2,1)S(1)} %reshape.195), channel_id=1, replica_groups=mesh['dp'=8,'dom'=64] {'dom'}, dimensions={0} | all-to-all | bytes 1048576 | tf_op jit(solution)/shard_map/all_to_all | solution.py:176
  102.8 0.5 reshape.196
  103.3 1.1 copy.142
  104.4 0.2 convert_reduce_fusion
  104.7 0.0 copy-start.3
  104.7 0.0 copy-start.4
  104.7 1.1 copy.143
  105.8 1.1 copy.145
  106.9 0.1 all_gather.10
  107.0 19.7 %all_gather.11 = f32[8,8,4,64]{3,1,2,0:T(8,128)S(1)} all-gather(f32[1,8,4,64]{3,1,2,0:T(8,128)S(1)} %copy.144), channel_id=1, replica_groups=mesh['dp'=8,'dom'=64] {'dp'}, dimensions={0}, use_global_device_ids=true | all-gather | bytes 73728 | tf_op jit(solution)/shard_map/all_gather | solution.py:187
  126.8 0.6 multiply_subtract_fusion
  (16 shorter events, 0.2 us)
Async XLA Ops:
  0.6 61.2 %copy-start = (bf16[64,64]{1,0:T(8,128)(2,1)S(1)}, bf16[64,64]{1,0:T(8,128)(2,1)}, u32[]{:S(2)}) copy-start(bf16[64,64]{1,0:T(8,128)(2,1)} %param.13) | copy-start | bytes 24580
  0.6 15.5 %copy-start.1 = (bf16[1,64,8,256]{3,2,1,0:T(8,128)(2,1)S(1)}, bf16[1,64,8,256]{3,2,1,0:T(8,128)(2,1)}, u32[]{:S(2)}) copy-start(bf16[1,64,8,256]{3,2,1,0:T(8,128)(2,1)} %param.8) | copy-start | bytes 786436
  2.1 21.4 %all-to-all-start.1 = ((bf16[64,2,128]{2,1,0:T(2,128)(2,1)}), bf16[64,2,128]{2,1,0:T(2,128)(2,1)S(1)}, u32[]{:S(2)}, u32[]{:S(2)}) async-start(bf16[64,2,128]{2,1,0:T(2,128)(2,1)} %reshape.193), calls=%async_computation.1 | async-start | bytes 65536 | tf_op jit(solution)/shard_map/all_to_all | solution.py:27
  16.8 11.7 %copy-start.5 = (s32[8]{0:T(128)S(1)}, s32[8]{0:T(128)}, u32[]{:S(2)}) copy-start(s32[8]{0:T(128)} %param.15) | copy-start | bytes 100
  23.5 35.0 %all-to-all-start = ((bf16[64,2,2048]{2,1,0:T(2,128)(2,1)}), bf16[64,2,2048]{2,1,0:T(2,128)(2,1)S(1)}, u32[]{:S(2)}, u32[]{:S(2)}) async-start(bf16[64,2,2048]{2,1,0:T(2,128)(2,1)} %reshape.191), calls=%async_computation | async-start | bytes 1048576 | tf_op jit(solution)/shard_map/all_to_all | solution.py:37
  60.8 1.1 copy-start.6
  104.7 22.1 %copy-start.2 = (f32[4,64]{1,0:T(4,128)S(1)}, f32[4,64]{1,0:T(4,128)}, u32[]{:S(2)}) copy-start(f32[4,64]{1,0:T(4,128)} %param.10) | copy-start | bytes 3076
  104.7 22.1 %copy-start.3 = (f32[4,64]{1,0:T(4,128)S(1)}, f32[4,64]{1,0:T(4,128)}, u32[]{:S(2)}) copy-start(f32[4,64]{1,0:T(4,128)} %param.11) | copy-start | bytes 3076
  104.7 22.1 %copy-start.4 = (f32[4,64]{1,0:T(4,128)S(1)}, f32[4,64]{1,0:T(4,128)}, u32[]{:S(2)}) copy-start(f32[4,64]{1,0:T(4,128)} %param.12) | copy-start | bytes 3076

commit v4 on v0

--- a/solution.py
+++ b/solution.py
@@ -149,9 +149,11 @@
     part_imag = jnp.einsum(
         outer, grad_imag, spec_real, preferred_element_type=jnp.float32
     ) - jnp.einsum(outer, grad_real, spec_imag, preferred_element_type=jnp.float32)
-    grad_local = jnp.stack([part_real, part_imag], 0).reshape(2 * MODES * channels, channels)
-    group_grad = sum_at_owner(grad_local.astype(jnp.bfloat16), "dp", 0)
-    weight_grad = summed_on_arrival(group_grad, "dom", 0)
+    groups = lax.axis_size("dp")
+    slabs = lax.axis_size("dom")
+    rows_here = spectral_weight.shape[0]
+    grad_local = jnp.stack([part_real, part_imag], 0).astype(jnp.bfloat16)
+    grad_tiles = jnp.moveaxis(grad_local.reshape(groups, slabs, rows_here, channels), 1, 0)
     inner = "fco,slof->slcf"
     input_real = jnp.einsum(
         inner, weight_real, grad_real, preferred_element_type=jnp.float32
@@ -167,7 +169,14 @@
         "oc,soxl->scxl", skip_weight, gate_lines, preferred_element_type=jnp.float32
     )
     grad_lines = (input_rows.astype(jnp.float32) + skip_back).astype(jnp.bfloat16)
+    group_grad = lax.all_to_all(grad_tiles, "dom", 0, 0, tiled=True)
+    grad_lines, group_grad = lax.optimization_barrier((grad_lines, group_grad))
     input_grad = lax.all_to_all(grad_lines, "dom", split_axis=2, concat_axis=3, tiled=True)
+    group_grad = group_grad.astype(jnp.float32).sum(axis=0)
+    every_group = lax.all_gather(group_grad, "dp", axis=0, tiled=False)
+    input_grad, every_group = lax.optimization_barrier((input_grad, every_group))
+    mine = lax.dynamic_index_in_dim(every_group, lax.axis_index("dp"), 1, keepdims=False)
+    weight_grad = mine.sum(axis=0)
     new_moment_one = beta_first * moment_one + (1.0 - beta_first) * weight_grad
     new_moment_two = beta_second * moment_two + (1.0 - beta_second) * weight_grad * weight_grad
     first_hat = new_moment_one / (1.0 - beta_first**STEP)

time: 136 us -> 123 us (0.904)
  waiting for transfers between devices: 35.7 us -> 15.1 us
  blocking collectives: 27.5 us -> 47 us
  starting transfers between devices: 47.5 us -> 38.2 us
    all_gather x0 -> x1, blocking collectives: none -> 19.5 us  [on_device(): every_group = lax.all_gather(group_grad, 'dp', axis=0, tiled=False)]
    all_to_all x1, starting transfers between devices: 17.7 us -> 6 us  [on_device(): lax.all_to_all(grad_lines, 'dom', split_axis=2, concat_axis=3, tiled=True)]
    all_to_all x2 -> x1, waiting for transfers between devices: 20.5 us -> 10 us  [on_device(): group_grad = lax.all_to_all(grad_tiles, 'dom', 0, 0, tiled=True)]
    all_to_all x1, waiting for transfers between devices: 10.1 us -> 0.01 us  [on_device(): lax.all_to_all(grad_lines, 'dom', split_axis=2, concat_axis=3, tiled=True)]
    all_to_all x2 -> x1, starting transfers between devices: 12.3 us -> 14.6 us  [on_device(): group_grad = lax.all_to_all(grad_tiles, 'dom', 0, 0, tiled=True)]
    unnamed x25 -> x24, local copies, waits for them, and re-layouts: 9.8 us -> 10 us
  transfers between devices with their start and end apart: 5 -> 4, of which waited for: 4 -> 2; matrix products, arithmetic and copies ran while one was open for 8% -> 6% of each run, Pallas kernels for 0% -> 0%
where the time goes in v4:
time: 123 us
  blocking collectives  47 us (38%)
  starting transfers between devices  38.2 us (31%)
  waiting for transfers between devices  15.1 us (12%)
  local copies, waits for them, and re-layouts  12.1 us (10%)
  matrix products  6 us (5%)
  other arithmetic  3.47 us (3%)
    all_gather x1, blocking collectives, on_device(): weight_low = lax.all_gather(group_low, 'dp', axis=0, tiled=True)  27.5 us
    all_gather x1, blocking collectives, on_device(): every_group = lax.all_gather(group_grad, 'dp', axis=0, tiled=False)  19.5 us
    all_to_all x1, starting transfers between devices, on_device(): group_grad = lax.all_to_all(grad_tiles, 'dom', 0, 0, tiled=True)  14.6 us
    all_to_all x1, starting transfers between devices, copy_for_each(): return lax.all_to_all(copies, axis, split_axis=0, concat_axis=0, tiled=True)  12.6 us
    unnamed x24, local copies, waits for them, and re-layouts  10 us
    all_to_all x1, waiting for transfers between devices, on_device(): group_grad = lax.all_to_all(grad_tiles, 'dom', 0, 0, tiled=True)  10 us
    all_to_all x1, starting transfers between devices, on_device(): lax.all_to_all(grad_lines, 'dom', split_axis=2, concat_axis=3, tiled=True)  6 us
    all_to_all x1, waiting for transfers between devices, copy_for_each(): return lax.all_to_all(copies, axis, split_axis=0, concat_axis=0, tiled=True)  5.09 us
  transfers between devices with their start and end apart: 4, of which 2 were waited for; matrix products, arithmetic and copies ran while one was open for 6% of the time, Pallas kernels for 0%

profile of v4, /device:TPU:1, one launch (start us, length us, event | category | flops | bytes accessed | tf_op | source)
XLA Modules:
  0.0 122.8 jit_solution(3879859582781765975)
XLA Ops:
  0.6 0.0 copy-start
  0.6 0.7 convert_element_type.173
  1.4 0.7 reshape.169
  2.1 12.6 %all-to-all-start.1 = ((bf16[64,2,128]{2,1,0:T(2,128)(2,1)}), bf16[64,2,128]{2,1,0:T(2,128)(2,1)S(1)}, u32[]{:S(2)}, u32[]{:S(2)}) async-start(bf16[64,2,128]{2,1,0:T(2,128)(2,1)} %reshape.169), calls=%async_computation.1 | async-start | bytes 65536 | tf_op jit(solution)/shard_map/all_to_all | solution.py:27
  14.6 0.0 copy-start.1
  14.6 1.5 %copy.68 = bf16[1,64,8,256]{1,2,0,3:T(8,128)(2,1)S(1)} copy(bf16[1,64,8,256]{3,2,1,0:T(8,128)(2,1)} %param.9) | data formatting | bytes 524288 | tf_op args[1]
  16.1 0.4 copy.67
  16.5 0.2 fusion.144
  16.8 1.6 %reshape.167 = bf16[64,2,2048]{2,1,0:T(2,128)(2,1)} reshape(bf16[256,2,8,64]{3,2,1,0:T(8,128)(2,1)S(1)} %fusion.144) | data formatting | bytes 1048576
  18.3 5.1 %all-to-all-done.1 = bf16[64,2,128]{2,1,0:T(2,128)(2,1)S(1)} async-done(((bf16[64,2,128]{2,1,0:T(2,128)(2,1)}), bf16[64,2,128]{2,1,0:T(2,128)(2,1)S(1)}, u32[]{:S(2)}, u32[]{:S(2)}) %all-to-all-start.1) | async-done | bytes 32800 | tf_op jit(solution)/shard_map/all_to_all | solution.py:27
  23.4 5.0 %all-to-all-start = ((bf16[64,2,2048]{2,1,0:T(2,128)(2,1)}), bf16[64,2,2048]{2,1,0:T(2,128)(2,1)S(1)}, u32[]{:S(2)}, u32[]{:S(2)}) async-start(bf16[64,2,2048]{2,1,0:T(2,128)(2,1)} %reshape.167), calls=%async_computation | async-start | bytes 1048576 | tf_op jit(solution)/shard_map/all_to_all | solution.py:37
  28.5 0.6 copy-done.5
  29.1 0.6 dynamic_slice.7
  29.7 0.6 compare_convert_fusion
  30.4 0.7 compare_select_fusion.1
  31.0 0.1 reshape.170
  31.1 27.5 %all_gather.9 = bf16[2048,64]{1,0:T(8,128)(2,1)S(1)} all-gather(bf16[256,64]{1,0:T(8,128)(2,1)S(1)} %bitcast.197), channel_id=1, replica_groups=mesh['dp'=8,'dom'=64] {'dp'}, dimensions={0}, use_global_device_ids=true | all-gather | bytes 294912 | tf_op jit(solution)/shard_map/all_gather | solution.py:117
  58.6 0.7 reshape.168
  59.3 0.1 copy.69
  59.4 0.2 fusion.142
  59.6 0.3 fusion.34
  59.8 0.3 fusion.35
  60.1 0.1 copy.162
  60.2 0.3 copy.81
  60.5 0.2 fusion.97
  60.7 0.2 fusion.91
  60.9 0.2 fusion.32
  61.1 0.3 fusion.67
  61.4 0.2 fusion.33
  61.6 0.3 fusion.11
  62.0 0.3 copy-done.6
  62.3 0.5 fusion.47
  62.7 0.3 fusion.29
  63.0 0.3 fusion.28
  63.3 0.2 fusion.87
  63.5 0.3 fusion.84
  63.8 0.3 fusion.77
  64.1 0.2 fusion.27
  64.3 0.3 fusion.8
  64.6 0.3 fusion.9
  64.9 0.1 pad_maximum_fusion.1
  65.0 0.2 copy.164
  65.2 1.0 reshape.171
  66.2 14.6 %all-to-all-start.2 = ((bf16[64,2,1024]{2,1,0:T(2,128)(2,1)}), bf16[64,2,1024]{2,1,0:T(2,128)(2,1)S(1)}, u32[]{:S(2)}, u32[]{:S(2)}) async-start(bf16[64,2,1024]{2,1,0:T(2,128)(2,1)} %reshape.171), calls=%async_computation.2 | async-start | bytes 524288 | tf_op jit(solution)/shard_map/all_to_all | solution.py:172
  80.9 0.2 fusion.80
  81.1 0.3 fusion.26
  81.3 0.4 fusion.64
  81.7 0.3 fusion.10
  82.0 0.3 fusion.3
  82.3 10.0 %all-to-all-done.2 = bf16[64,2,1024]{2,1,0:T(2,128)(2,1)S(1)} async-done(((bf16[64,2,1024]{2,1,0:T(2,128)(2,1)}), bf16[64,2,1024]{2,1,0:T(2,128)(2,1)S(1)}, u32[]{:S(2)}, u32[]{:S(2)}) %all-to-all-start.2) | async-done | bytes 262176 | tf_op jit(solution)/shard_map/all_to_all | solution.py:172
  92.3 0.3 reshape.172
  92.7 0.3 copy.98
  93.0 1.0 reshape.173
  94.0 6.0 %all-to-all-start.3 = ((bf16[64,2,1024]{2,1,0:T(2,128)(2,1)}), bf16[64,2,1024]{2,1,0:T(2,128)(2,1)S(1)}, u32[]{:S(2)}, u32[]{:S(2)}) async-start(bf16[64,2,1024]{2,1,0:T(2,128)(2,1)} %reshape.173), calls=%async_computation.3 | async-start | bytes 524288 | tf_op jit(solution)/shard_map/all_to_all | solution.py:174
  100.0 0.3 convert_reduce_fusion
  100.3 19.5 %all-gather = f32[64,4,64]{2,1,0:T(4,128)S(1)} all-gather(f32[8,4,64]{2,1,0:T(4,128)S(1)} %convert_reduce_fusion), channel_id=2, replica_groups=mesh['dp'=8,'dom'=64] {'dp'}, dimensions={0}, use_global_device_ids=true | all-gather | bytes 73728 | tf_op jit(solution)/shard_map/all_gather | solution.py:176
  119.9 0.3 reshape.174
  120.2 0.1 copy.163
  120.3 0.1 copy.100
  120.4 1.1 copy.101
  121.5 0.7 copy-done.2
  122.2 0.0 copy-done.3
  122.2 0.0 copy-done.4
  122.2 0.6 multiply_subtract_fusion
  (13 shorter events, 0.1 us)
Async XLA Ops:
  0.6 61.3 %copy-start = (bf16[64,64]{1,0:T(8,128)(2,1)S(1)}, bf16[64,64]{1,0:T(8,128)(2,1)}, u32[]{:S(2)}) copy-start(bf16[64,64]{1,0:T(8,128)(2,1)} %param.13) | copy-start | bytes 24580
  2.1 21.4 %all-to-all-start.1 = ((bf16[64,2,128]{2,1,0:T(2,128)(2,1)}), bf16[64,2,128]{2,1,0:T(2,128)(2,1)S(1)}, u32[]{:S(2)}, u32[]{:S(2)}) async-start(bf16[64,2,128]{2,1,0:T(2,128)(2,1)} %reshape.169), calls=%async_computation.1 | async-start | bytes 65536 | tf_op jit(solution)/shard_map/all_to_all | solution.py:27
  14.6 1.5 %copy-start.1 = (bf16[1,64,8,256]{3,2,1,0:T(8,128)(2,1)S(1)}, bf16[1,64,8,256]{3,2,1,0:T(8,128)(2,1)}, u32[]{:S(2)}) copy-start(bf16[1,64,8,256]{3,2,1,0:T(8,128)(2,1)} %param.8) | copy-start | bytes 786436
  23.4 35.2 %all-to-all-start = ((bf16[64,2,2048]{2,1,0:T(2,128)(2,1)}), bf16[64,2,2048]{2,1,0:T(2,128)(2,1)S(1)}, u32[]{:S(2)}, u32[]{:S(2)}) async-start(bf16[64,2,2048]{2,1,0:T(2,128)(2,1)} %reshape.167), calls=%async_computation | async-start | bytes 1048576 | tf_op jit(solution)/shard_map/all_to_all | solution.py:37
  28.5 0.7 copy-start.5
  61.6 0.7 copy-start.6
  66.2 26.1 %all-to-all-start.2 = ((bf16[64,2,1024]{2,1,0:T(2,128)(2,1)}), bf16[64,2,1024]{2,1,0:T(2,128)(2,1)S(1)}, u32[]{:S(2)}, u32[]{:S(2)}) async-start(bf16[64,2,1024]{2,1,0:T(2,128)(2,1)} %reshape.171), calls=%async_computation.2 | async-start | bytes 524288 | tf_op jit(solution)/shard_map/all_to_all | solution.py:172
  94.0 25.8 %all-to-all-start.3 = ((bf16[64,2,1024]{2,1,0:T(2,128)(2,1)}), bf16[64,2,1024]{2,1,0:T(2,128)(2,1)S(1)}, u32[]{:S(2)}, u32[]{:S(2)}) async-start(bf16[64,2,1024]{2,1,0:T(2,128)(2,1)} %reshape.173), calls=%async_computation.3 | async-start | bytes 524288 | tf_op jit(solution)/shard_map/all_to_all | solution.py:174
  121.5 0.7 copy-start.2
  121.5 0.7 copy-start.3
  121.5 0.7 copy-start.4

commit v5 on v4

--- a/solution.py
+++ b/solution.py
@@ -111,8 +111,9 @@
     keep_modes = (jnp.arange(MODES, dtype=jnp.int32)[None, :] < counts_here[:, None]).astype(
         jnp.float32
     )
+    weight_short = spectral_weight.astype(jnp.bfloat16)
+    weight_short, keep_modes = lax.optimization_barrier((weight_short, keep_modes))
     keep_wide = keep_modes[:, None, None, :]
-    weight_short = spectral_weight.astype(jnp.bfloat16)
     group_low = collect(weight_short, "dom", 0)
     weight_low = lax.all_gather(group_low, "dp", axis=0, tiled=True)
     weight_low = weight_low.reshape(2, MODES, channels, channels)
@@ -174,7 +175,6 @@
     input_grad = lax.all_to_all(grad_lines, "dom", split_axis=2, concat_axis=3, tiled=True)
     group_grad = group_grad.astype(jnp.float32).sum(axis=0)
     every_group = lax.all_gather(group_grad, "dp", axis=0, tiled=False)
-    input_grad, every_group = lax.optimization_barrier((input_grad, every_group))
     mine = lax.dynamic_index_in_dim(every_group, lax.axis_index("dp"), 1, keepdims=False)
     weight_grad = mine.sum(axis=0)
     new_moment_one = beta_first * moment_one + (1.0 - beta_first) * weight_grad
@@ -184,7 +184,7 @@
     new_weight = spectral_weight - learn_rate * (
         first_hat / (jnp.sqrt(second_hat) + epsilon) + decay_rate * spectral_weight
     )
-    return (input_grad, new_weight, new_moment_one, new_moment_two)
+    return lax.optimization_barrier((input_grad, new_weight, new_moment_one, new_moment_two))
 
 
 def solution(mesh):

time: 123 us -> 125 us (1.016)
  blocking collectives: 47 us -> 49.9 us
    all_gather x1, blocking collectives: 27.5 us -> 30.4 us  [on_device(): weight_low = lax.all_gather(group_low, 'dp', axis=0, tiled=True)]
    unnamed x24 -> x23, local copies, waits for them, and re-layouts: 10 us -> 8.9 us
  transfers between devices with their start and end apart: 4 -> 4, of which waited for: 2 -> 2; matrix products, arithmetic and copies ran while one was open for 6% -> 5% of each run, Pallas kernels for 0% -> 0%
where the time goes in v5:
time: 125 us
  blocking collectives  49.9 us (40%)
  starting transfers between devices  37.6 us (30%)
  waiting for transfers between devices  15.1 us (12%)
  local copies, waits for them, and re-layouts  12.1 us (10%)
  matrix products  6.01 us (5%)
  other arithmetic  2.82 us (2%)
    all_gather x1, blocking collectives, on_device(): weight_low = lax.all_gather(group_low, 'dp', axis=0, tiled=True)  30.4 us
    all_gather x1, blocking collectives, on_device(): every_group = lax.all_gather(group_grad, 'dp', axis=0, tiled=False)  19.5 us
    all_to_all x1, starting transfers between devices, on_device(): group_grad = lax.all_to_all(grad_tiles, 'dom', 0, 0, tiled=True)  14.1 us
    all_to_all x1, starting transfers between devices, copy_for_each(): return lax.all_to_all(copies, axis, split_axis=0, concat_axis=0, tiled=True)  12.6 us
    all_to_all x1, waiting for transfers between devices, on_device(): group_grad = lax.all_to_all(grad_tiles, 'dom', 0, 0, tiled=True)  10 us
    unnamed x23, local copies, waits for them, and re-layouts  8.9 us
    all_to_all x1, starting transfers between devices, on_device(): lax.all_to_all(grad_lines, 'dom', split_axis=2, concat_axis=3, tiled=True)  6.01 us
    all_to_all x1, waiting for transfers between devices, copy_for_each(): return lax.all_to_all(copies, axis, split_axis=0, concat_axis=0, tiled=True)  5.09 us
  transfers between devices with their start and end apart: 4, of which 2 were waited for; matrix products, arithmetic and copies ran while one was open for 5% of the time, Pallas kernels for 0%

profile of v5, /device:TPU:1, one launch (start us, length us, event | category | flops | bytes accessed | tf_op | source)
XLA Modules:
  0.0 124.5 jit_solution(14504457825139044125)
XLA Ops:
  0.6 0.0 copy-start
  0.6 0.7 convert_element_type.170
  1.3 0.7 copy-done.5
  2.0 0.6 dynamic_slice.7
  2.6 0.6 compare_convert_fusion
  3.3 0.7 reshape.175
  4.0 12.6 %all-to-all-start.1 = ((bf16[64,2,128]{2,1,0:T(2,128)(2,1)}), bf16[64,2,128]{2,1,0:T(2,128)(2,1)S(1)}, u32[]{:S(2)}, u32[]{:S(2)}) async-start(bf16[64,2,128]{2,1,0:T(2,128)(2,1)} %reshape.175), calls=%async_computation.1 | async-start | bytes 65536 | tf_op jit(solution)/shard_map/all_to_all | solution.py:27
  16.5 0.0 copy-start.1
  16.5 1.5 %copy.68 = bf16[1,64,8,256]{1,2,0,3:T(8,128)(2,1)S(1)} copy(bf16[1,64,8,256]{3,2,1,0:T(8,128)(2,1)} %param.9) | data formatting | bytes 524288 | tf_op args[1]
  18.0 0.4 copy.67
  18.4 0.2 fusion.145
  18.7 1.6 %reshape.173 = bf16[64,2,2048]{2,1,0:T(2,128)(2,1)} reshape(bf16[256,2,8,64]{3,2,1,0:T(8,128)(2,1)S(1)} %fusion.145) | data formatting | bytes 1048576
  20.2 5.1 %all-to-all-done.1 = bf16[64,2,128]{2,1,0:T(2,128)(2,1)S(1)} async-done(((bf16[64,2,128]{2,1,0:T(2,128)(2,1)}), bf16[64,2,128]{2,1,0:T(2,128)(2,1)S(1)}, u32[]{:S(2)}, u32[]{:S(2)}) %all-to-all-start.1) | async-done | bytes 32800 | tf_op jit(solution)/shard_map/all_to_all | solution.py:27
  25.3 5.0 %all-to-all-start = ((bf16[64,2,2048]{2,1,0:T(2,128)(2,1)}), bf16[64,2,2048]{2,1,0:T(2,128)(2,1)S(1)}, u32[]{:S(2)}, u32[]{:S(2)}) async-start(bf16[64,2,2048]{2,1,0:T(2,128)(2,1)} %reshape.173), calls=%async_computation | async-start | bytes 1048576 | tf_op jit(solution)/shard_map/all_to_all | solution.py:37
  30.4 0.1 reshape.176
  30.5 30.4 %all_gather.9 = bf16[2048,64]{1,0:T(8,128)(2,1)S(1)} all-gather(bf16[256,64]{1,0:T(8,128)(2,1)S(1)} %bitcast.195), channel_id=1, replica_groups=mesh['dp'=8,'dom'=64] {'dp'}, dimensions={0}, use_global_device_ids=true | all-gather | bytes 294912 | tf_op jit(solution)/shard_map/all_gather | solution.py:118
  60.9 0.7 reshape.174
  61.6 0.1 copy.69
  61.6 0.2 fusion.143
  61.8 0.3 fusion.34
  62.1 0.3 fusion.35
  62.4 0.1 copy.162
  62.5 0.3 copy.81
  62.8 0.2 fusion.97
  63.0 0.2 fusion.91
  63.2 0.2 fusion.33
  63.3 0.3 fusion.67
  63.7 0.2 fusion.32
  63.9 0.0 copy-start.6
  63.9 0.3 fusion.11
  64.2 0.3 copy-done.6
  64.5 0.5 fusion.47
  65.0 0.3 fusion.29
  65.3 0.3 fusion.28
  65.5 0.2 fusion.87
  65.8 0.3 fusion.84
  66.1 0.3 fusion.77
  66.4 0.2 fusion.27
  66.6 0.3 fusion.8
  66.9 0.3 fusion.9
  67.2 0.1 pad_maximum_fusion.1
  67.3 0.2 copy.164
  67.5 1.0 reshape.177
  68.5 14.1 %all-to-all-start.2 = ((bf16[64,2,1024]{2,1,0:T(2,128)(2,1)}), bf16[64,2,1024]{2,1,0:T(2,128)(2,1)S(1)}, u32[]{:S(2)}, u32[]{:S(2)}) async-start(bf16[64,2,1024]{2,1,0:T(2,128)(2,1)} %reshape.177), calls=%async_computation.2 | async-start | bytes 524288 | tf_op jit(solution)/shard_map/all_to_all | solution.py:173
  82.6 0.2 fusion.80
  82.8 0.3 fusion.26
  83.1 0.4 fusion.64
  83.4 0.3 fusion.10
  83.8 0.3 fusion.3
  84.1 10.0 %all-to-all-done.2 = bf16[64,2,1024]{2,1,0:T(2,128)(2,1)S(1)} async-done(((bf16[64,2,1024]{2,1,0:T(2,128)(2,1)}), bf16[64,2,1024]{2,1,0:T(2,128)(2,1)S(1)}, u32[]{:S(2)}, u32[]{:S(2)}) %all-to-all-start.2) | async-done | bytes 262176 | tf_op jit(solution)/shard_map/all_to_all | solution.py:173
  94.1 0.3 reshape.178
  94.4 0.3 copy.98
  94.7 1.0 reshape.179
  95.7 6.0 %all-to-all-start.3 = ((bf16[64,2,1024]{2,1,0:T(2,128)(2,1)}), bf16[64,2,1024]{2,1,0:T(2,128)(2,1)S(1)}, u32[]{:S(2)}, u32[]{:S(2)}) async-start(bf16[64,2,1024]{2,1,0:T(2,128)(2,1)} %reshape.179), calls=%async_computation.3 | async-start | bytes 524288 | tf_op jit(solution)/shard_map/all_to_all | solution.py:175
  101.8 0.3 convert_reduce_fusion
  102.1 19.5 %all-gather = f32[64,4,64]{2,1,0:T(4,128)S(1)} all-gather(f32[8,4,64]{2,1,0:T(4,128)S(1)} %convert_reduce_fusion), channel_id=2, replica_groups=mesh['dp'=8,'dom'=64] {'dp'}, dimensions={0}, use_global_device_ids=true | all-gather | bytes 73728 | tf_op jit(solution)/shard_map/all_gather | solution.py:177
  121.6 0.7 copy-done.2
  122.2 0.0 copy-done.3
  122.3 0.0 copy-done.4
  122.3 0.6 multiply_subtract_fusion
  122.9 0.3 reshape.180
  123.2 0.1 copy.163
  123.3 0.1 copy.100
  123.4 1.1 copy.101
  (13 shorter events, 0.1 us)
Async XLA Ops:
  0.6 63.6 %copy-start = (bf16[64,64]{1,0:T(8,128)(2,1)S(1)}, bf16[64,64]{1,0:T(8,128)(2,1)}, u32[]{:S(2)}) copy-start(bf16[64,64]{1,0:T(8,128)(2,1)} %param.13) | copy-start | bytes 24580
  1.3 0.7 copy-start.5
  4.0 21.4 %all-to-all-start.1 = ((bf16[64,2,128]{2,1,0:T(2,128)(2,1)}), bf16[64,2,128]{2,1,0:T(2,128)(2,1)S(1)}, u32[]{:S(2)}, u32[]{:S(2)}) async-start(bf16[64,2,128]{2,1,0:T(2,128)(2,1)} %reshape.175), calls=%async_computation.1 | async-start | bytes 65536 | tf_op jit(solution)/shard_map/all_to_all | solution.py:27
  16.5 1.5 %copy-start.1 = (bf16[1,64,8,256]{3,2,1,0:T(8,128)(2,1)S(1)}, bf16[1,64,8,256]{3,2,1,0:T(8,128)(2,1)}, u32[]{:S(2)}) copy-start(bf16[1,64,8,256]{3,2,1,0:T(8,128)(2,1)} %param.8) | copy-start | bytes 786436
  25.3 35.6 %all-to-all-start = ((bf16[64,2,2048]{2,1,0:T(2,128)(2,1)}), bf16[64,2,2048]{2,1,0:T(2,128)(2,1)S(1)}, u32[]{:S(2)}, u32[]{:S(2)}) async-start(bf16[64,2,2048]{2,1,0:T(2,128)(2,1)} %reshape.173), calls=%async_computation | async-start | bytes 1048576 | tf_op jit(solution)/shard_map/all_to_all | solution.py:37
  63.9 0.7 copy-start.6
  68.5 25.6 %all-to-all-start.2 = ((bf16[64,2,1024]{2,1,0:T(2,128)(2,1)}), bf16[64,2,1024]{2,1,0:T(2,128)(2,1)S(1)}, u32[]{:S(2)}, u32[]{:S(2)}) async-start(bf16[64,2,1024]{2,1,0:T(2,128)(2,1)} %reshape.177), calls=%async_computation.2 | async-start | bytes 524288 | tf_op jit(solution)/shard_map/all_to_all | solution.py:173
  95.7 27.1 %all-to-all-start.3 = ((bf16[64,2,1024]{2,1,0:T(2,128)(2,1)}), bf16[64,2,1024]{2,1,0:T(2,128)(2,1)S(1)}, u32[]{:S(2)}, u32[]{:S(2)}) async-start(bf16[64,2,1024]{2,1,0:T(2,128)(2,1)} %reshape.179), calls=%async_computation.3 | async-start | bytes 524288 | tf_op jit(solution)/shard_map/all_to_all | solution.py:175
  121.6 0.7 copy-start.2
  121.6 0.7 copy-start.3
  121.6 0.7 copy-start.4

commit v6 on v0

--- a/solution.py
+++ b/solution.py
@@ -142,16 +142,6 @@
     scale = keep_wide * doubling
     grad_real = (grad_real * scale).astype(jnp.bfloat16)
     grad_imag = (grad_imag * scale).astype(jnp.bfloat16)
-    outer = "slof,slcf->fco"
-    part_real = jnp.einsum(
-        outer, grad_real, spec_real, preferred_element_type=jnp.float32
-    ) + jnp.einsum(outer, grad_imag, spec_imag, preferred_element_type=jnp.float32)
-    part_imag = jnp.einsum(
-        outer, grad_imag, spec_real, preferred_element_type=jnp.float32
-    ) - jnp.einsum(outer, grad_real, spec_imag, preferred_element_type=jnp.float32)
-    grad_local = jnp.stack([part_real, part_imag], 0).reshape(2 * MODES * channels, channels)
-    group_grad = sum_at_owner(grad_local.astype(jnp.bfloat16), "dp", 0)
-    weight_grad = summed_on_arrival(group_grad, "dom", 0)
     inner = "fco,slof->slcf"
     input_real = jnp.einsum(
         inner, weight_real, grad_real, preferred_element_type=jnp.float32
@@ -167,7 +157,26 @@
         "oc,soxl->scxl", skip_weight, gate_lines, preferred_element_type=jnp.float32
     )
     grad_lines = (input_rows.astype(jnp.float32) + skip_back).astype(jnp.bfloat16)
+    groups = lax.axis_size("dp")
+    slabs = lax.axis_size("dom")
+    rows_here = spectral_weight.shape[0]
     input_grad = lax.all_to_all(grad_lines, "dom", split_axis=2, concat_axis=3, tiled=True)
+    packed = jnp.stack([grad_real, grad_imag, spec_real, spec_imag], 0)
+    every_group = lax.all_gather(packed, "dp", axis=1, tiled=True)
+    input_grad, every_group = lax.optimization_barrier((input_grad, every_group))
+    group_real, group_imag, group_spec_real, group_spec_imag = (every_group[i] for i in range(4))
+    outer = "slof,slcf->fco"
+    part_real = jnp.einsum(
+        outer, group_real, group_spec_real, preferred_element_type=jnp.float32
+    ) + jnp.einsum(outer, group_imag, group_spec_imag, preferred_element_type=jnp.float32)
+    part_imag = jnp.einsum(
+        outer, group_imag, group_spec_real, preferred_element_type=jnp.float32
+    ) - jnp.einsum(outer, group_real, group_spec_imag, preferred_element_type=jnp.float32)
+    group_rows = jnp.stack([part_real, part_imag], 0).reshape(groups, slabs, rows_here, channels)
+    own_rows = lax.dynamic_index_in_dim(group_rows, lax.axis_index("dp"), 0, keepdims=False)
+    weight_grad = lax.all_to_all(own_rows, "dom", 0, 0, tiled=True).reshape(
+        slabs, rows_here, channels
+    ).sum(axis=0)
     new_moment_one = beta_first * moment_one + (1.0 - beta_first) * weight_grad
     new_moment_two = beta_second * moment_two + (1.0 - beta_second) * weight_grad * weight_grad
     first_hat = new_moment_one / (1.0 - beta_first**STEP)

time: 136 us -> 128 us (0.941)
  waiting for transfers between devices: 35.7 us -> 13 us
  blocking collectives: 27.5 us -> 47.5 us
  starting transfers between devices: 47.5 us -> 43.4 us
    all_gather x0 -> x1, blocking collectives: none -> 20 us  [on_device(): every_group = lax.all_gather(packed, 'dp', axis=1, tiled=True)]
    all_to_all x2 -> x1, waiting for transfers between devices: 20.5 us -> 7.94 us  [on_device(): lax.all_to_all(own_rows, 'dom', 0, 0, tiled=True)]
    all_to_all x1, waiting for transfers between devices: 10.1 us -> 0.01 us  [on_device(): lax.all_to_all(grad_lines, 'dom', split_axis=2, concat_axis=3, tiled=True)]
    all_to_all x1, starting transfers between devices: 17.7 us -> 14.6 us  [on_device(): lax.all_to_all(grad_lines, 'dom', split_axis=2, concat_axis=3, tiled=True)]
    all_to_all x2 -> x1, starting transfers between devices: 12.3 us -> 11.3 us  [on_device(): lax.all_to_all(own_rows, 'dom', 0, 0, tiled=True)]
  transfers between devices with their start and end apart: 5 -> 4, of which waited for: 4 -> 2; matrix products, arithmetic and copies ran while one was open for 8% -> 5% of each run, Pallas kernels for 0% -> 0%
where the time goes in v6:
time: 128 us; the launch traced here: 127 us
  blocking collectives  47.5 us (37%)
  starting transfers between devices  43.4 us (34%)
  waiting for transfers between devices  13 us (10%)
  local copies, waits for them, and re-layouts  11.9 us (9%)
  matrix products  6.12 us (5%)
  other arithmetic  4.03 us (3%)
    all_gather x1, blocking collectives, on_device(): weight_low = lax.all_gather(group_low, 'dp', axis=0, tiled=True)  27.5 us
    all_gather x1, blocking collectives, on_device(): every_group = lax.all_gather(packed, 'dp', axis=1, tiled=True)  20 us
    all_to_all x1, starting transfers between devices, on_device(): lax.all_to_all(grad_lines, 'dom', split_axis=2, concat_axis=3, tiled=True)  14.6 us
    all_to_all x1, starting transfers between devices, copy_for_each(): return lax.all_to_all(copies, axis, split_axis=0, concat_axis=0, tiled=True)  12.6 us
    all_to_all x1, starting transfers between devices, on_device(): lax.all_to_all(own_rows, 'dom', 0, 0, tiled=True)  11.3 us
    unnamed x25, local copies, waits for them, and re-layouts  9.82 us
    all_to_all x1, waiting for transfers between devices, on_device(): lax.all_to_all(own_rows, 'dom', 0, 0, tiled=True)  7.94 us
    all_to_all x1, waiting for transfers between devices, copy_for_each(): return lax.all_to_all(copies, axis, split_axis=0, concat_axis=0, tiled=True)  5.1 us
  transfers between devices with their start and end apart: 4, of which 2 were waited for; matrix products, arithmetic and copies ran while one was open for 5% of the time, Pallas kernels for 0%

profile of v6, /device:TPU:1, one launch (start us, length us, event | category | flops | bytes accessed | tf_op | source)
XLA Modules:
  0.0 127.1 jit_solution(7593993842376711868)
XLA Ops:
  0.6 0.0 copy-start
  0.6 0.7 convert_element_type.165
  1.4 0.7 reshape.165
  2.1 12.6 %all-to-all-start.1 = ((bf16[64,2,128]{2,1,0:T(2,128)(2,1)}), bf16[64,2,128]{2,1,0:T(2,128)(2,1)S(1)}, u32[]{:S(2)}, u32[]{:S(2)}) async-start(bf16[64,2,128]{2,1,0:T(2,128)(2,1)} %reshape.165), calls=%async_computation.1 | async-start | bytes 65536 | tf_op jit(solution)/shard_map/all_to_all | solution.py:27
  14.6 1.5 %copy.68 = bf16[1,64,8,256]{1,2,0,3:T(8,128)(2,1)S(1)} copy(bf16[1,64,8,256]{3,2,1,0:T(8,128)(2,1)} %param.9) | data formatting | bytes 524288 | tf_op args[1]
  16.1 0.4 copy.67
  16.5 0.2 fusion.138
  16.8 1.5 %reshape.163 = bf16[64,2,2048]{2,1,0:T(2,128)(2,1)} reshape(bf16[256,2,8,64]{3,2,1,0:T(8,128)(2,1)S(1)} %fusion.138) | data formatting | bytes 1048576
  18.3 5.1 %all-to-all-done.1 = bf16[64,2,128]{2,1,0:T(2,128)(2,1)S(1)} async-done(((bf16[64,2,128]{2,1,0:T(2,128)(2,1)}), bf16[64,2,128]{2,1,0:T(2,128)(2,1)S(1)}, u32[]{:S(2)}, u32[]{:S(2)}) %all-to-all-start.1) | async-done | bytes 32800 | tf_op jit(solution)/shard_map/all_to_all | solution.py:27
  23.4 5.0 %all-to-all-start = ((bf16[64,2,2048]{2,1,0:T(2,128)(2,1)}), bf16[64,2,2048]{2,1,0:T(2,128)(2,1)S(1)}, u32[]{:S(2)}, u32[]{:S(2)}) async-start(bf16[64,2,2048]{2,1,0:T(2,128)(2,1)} %reshape.163), calls=%async_computation | async-start | bytes 1048576 | tf_op jit(solution)/shard_map/all_to_all | solution.py:37
  28.5 0.6 copy-done.5
  29.1 0.6 dynamic_slice.7
  29.7 0.6 compare_convert_fusion
  30.4 0.7 compare_select_fusion.1
  31.0 0.1 reshape.166
  31.1 27.5 %all_gather.6 = bf16[2048,64]{1,0:T(8,128)(2,1)S(1)} all-gather(bf16[256,64]{1,0:T(8,128)(2,1)S(1)} %bitcast.222), channel_id=1, replica_groups=mesh['dp'=8,'dom'=64] {'dp'}, dimensions={0}, use_global_device_ids=true | all-gather | bytes 294912 | tf_op jit(solution)/shard_map/all_gather | solution.py:117
  58.6 0.7 reshape.164
  59.3 0.1 copy.69
  59.4 0.2 fusion.136
  59.6 0.3 convolution_convert_fusion
  59.8 0.3 fusion.25
  60.1 0.1 copy.164
  60.2 0.3 copy.81
  60.5 0.2 fusion.91
  60.7 0.2 fusion.87
  60.9 0.2 fusion.30
  61.1 0.3 fusion.71
  61.4 0.2 fusion.31
  61.6 0.3 fusion.11
  62.0 0.3 copy-done.6
  62.3 0.5 fusion.43
  62.7 0.3 fusion.21
  63.0 0.3 fusion.22
  63.3 0.2 fusion.85
  63.5 0.3 fusion.81
  63.7 0.3 fusion.27
  64.0 0.4 fusion.68
  64.4 0.2 fusion.26
  64.6 0.4 fusion.10
  65.0 0.3 fusion.7
  65.2 0.3 copy.89
  65.6 1.0 reshape.167
  66.6 14.6 %all-to-all-start.2 = ((bf16[64,2,1024]{2,1,0:T(2,128)(2,1)}), bf16[64,2,1024]{2,1,0:T(2,128)(2,1)S(1)}, u32[]{:S(2)}, u32[]{:S(2)}) async-start(bf16[64,2,1024]{2,1,0:T(2,128)(2,1)} %reshape.167), calls=%async_computation.2 | async-start | bytes 524288 | tf_op jit(solution)/shard_map/all_to_all | solution.py:163
  81.2 20.0 %all_gather.7 = bf16[4,8,4,64,16]{3,4,2,1,0:T(8,128)(2,1)S(1)} all-gather(bf16[4,1,4,64,16]{3,4,2,1,0:T(8,128)(2,1)S(1)} %pad_maximum_fusion.2), channel_id=1, replica_groups=mesh['dp'=8,'dom'=64] {'dp'}, dimensions={1}, use_global_device_ids=true | all-gather | bytes 294912 | tf_op jit(solution)/shard_map/all_gather | solution.py:165
  101.2 0.3 reshape.168
  101.6 0.1 copy.165
  101.7 0.1 copy.91
  101.8 0.3 convolution_bitcast_fusion
  102.1 0.3 convolution_bitcast_fusion.2
  102.4 0.3 fusion.6
  102.7 0.3 fusion.4
  103.0 0.1 pad_maximum_fusion.1
  103.2 0.8 reshape.169
  103.9 11.3 %all-to-all-start.3 = ((f32[64,1,256]{2,1,0:T(1,128)}), f32[64,1,256]{2,1,0:T(1,128)S(1)}, u32[]{:S(2)}, u32[]{:S(2)}) async-start(f32[64,1,256]{2,1,0:T(1,128)} %reshape.169), calls=%async_computation.3 | async-start | bytes 131072 | tf_op jit(solution)/shard_map/all_to_all | solution.py:177
  115.2 1.1 copy.100
  116.4 7.9 %all-to-all-done.3 = f32[64,1,256]{2,1,0:T(1,128)S(1)} async-done(((f32[64,1,256]{2,1,0:T(1,128)}), f32[64,1,256]{2,1,0:T(1,128)S(1)}, u32[]{:S(2)}, u32[]{:S(2)}) %all-to-all-start.3) | async-done | bytes 65568 | tf_op jit(solution)/shard_map/all_to_all | solution.py:177
  124.3 0.5 broadcast.102
  124.8 0.8 reduce
  125.6 0.1 reshape.170
  125.8 0.1 reduce_sum.9
  125.9 0.6 copy-done.2
  126.4 0.0 copy-done.3
  126.5 0.0 copy-done.4
  126.5 0.6 multiply_subtract_fusion
  (16 shorter events, 0.2 us)
Async XLA Ops:
  0.6 61.3 %copy-start = (bf16[64,64]{1,0:T(8,128)(2,1)S(1)}, bf16[64,64]{1,0:T(8,128)(2,1)}, u32[]{:S(2)}) copy-start(bf16[64,64]{1,0:T(8,128)(2,1)} %param.13) | copy-start | bytes 24580
  2.1 21.4 %all-to-all-start.1 = ((bf16[64,2,128]{2,1,0:T(2,128)(2,1)}), bf16[64,2,128]{2,1,0:T(2,128)(2,1)S(1)}, u32[]{:S(2)}, u32[]{:S(2)}) async-start(bf16[64,2,128]{2,1,0:T(2,128)(2,1)} %reshape.165), calls=%async_computation.1 | async-start | bytes 65536 | tf_op jit(solution)/shard_map/all_to_all | solution.py:27
  14.6 1.5 %copy-start.1 = (bf16[1,64,8,256]{3,2,1,0:T(8,128)(2,1)S(1)}, bf16[1,64,8,256]{3,2,1,0:T(8,128)(2,1)}, u32[]{:S(2)}) copy-start(bf16[1,64,8,256]{3,2,1,0:T(8,128)(2,1)} %param.8) | copy-start | bytes 786436
  23.4 35.2 %all-to-all-start = ((bf16[64,2,2048]{2,1,0:T(2,128)(2,1)}), bf16[64,2,2048]{2,1,0:T(2,128)(2,1)S(1)}, u32[]{:S(2)}, u32[]{:S(2)}) async-start(bf16[64,2,2048]{2,1,0:T(2,128)(2,1)} %reshape.163), calls=%async_computation | async-start | bytes 1048576 | tf_op jit(solution)/shard_map/all_to_all | solution.py:37
  28.5 0.7 copy-start.5
  61.6 0.7 copy-start.6
  66.6 34.7 %all-to-all-start.2 = ((bf16[64,2,1024]{2,1,0:T(2,128)(2,1)}), bf16[64,2,1024]{2,1,0:T(2,128)(2,1)S(1)}, u32[]{:S(2)}, u32[]{:S(2)}) async-start(bf16[64,2,1024]{2,1,0:T(2,128)(2,1)} %reshape.167), calls=%async_computation.2 | async-start | bytes 524288 | tf_op jit(solution)/shard_map/all_to_all | solution.py:163
  103.9 20.4 %all-to-all-start.3 = ((f32[64,1,256]{2,1,0:T(1,128)}), f32[64,1,256]{2,1,0:T(1,128)S(1)}, u32[]{:S(2)}, u32[]{:S(2)}) async-start(f32[64,1,256]{2,1,0:T(1,128)} %reshape.169), calls=%async_computation.3 | async-start | bytes 131072 | tf_op jit(solution)/shard_map/all_to_all | solution.py:177
  125.8 0.7 copy-start.2
  125.8 0.7 copy-start.3
  125.8 0.7 copy-start.4

commit v7 on v5

--- a/solution.py
+++ b/solution.py
@@ -88,15 +88,17 @@
 
 
 def forward_parts(field, cosines, sines):
-    real_part = jnp.einsum("scxl,fx->slcf", field, cosines, preferred_element_type=jnp.float32)
-    imag_part = -jnp.einsum("scxl,fx->slcf", field, sines, preferred_element_type=jnp.float32)
-    return (real_part, imag_part)
+    basis = jnp.concatenate([cosines, -sines], axis=0)
+    both = jnp.einsum("scxl,gx->slcg", field, basis, preferred_element_type=jnp.float32)
+    return (both[..., :MODES], both[..., MODES:])
 
 
 def inverse_cells(values_real, values_imag, cosines, sines):
-    first = jnp.einsum("slcf,fx->scxl", values_real, cosines, preferred_element_type=jnp.float32)
-    second = jnp.einsum("slcf,fx->scxl", values_imag, sines, preferred_element_type=jnp.float32)
-    return (first - second).astype(jnp.bfloat16)
+    basis = jnp.concatenate([cosines, -sines], axis=0)
+    both = jnp.concatenate([values_real, values_imag], axis=3)
+    return jnp.einsum("slcg,gx->scxl", both, basis, preferred_element_type=jnp.float32).astype(
+        jnp.bfloat16
+    )
 
 
 def on_device(
@@ -111,9 +113,8 @@
     keep_modes = (jnp.arange(MODES, dtype=jnp.int32)[None, :] < counts_here[:, None]).astype(
         jnp.float32
     )
+    keep_wide = keep_modes[:, None, None, :]
     weight_short = spectral_weight.astype(jnp.bfloat16)
-    weight_short, keep_modes = lax.optimization_barrier((weight_short, keep_modes))
-    keep_wide = keep_modes[:, None, None, :]
     group_low = collect(weight_short, "dom", 0)
     weight_low = lax.all_gather(group_low, "dp", axis=0, tiled=True)
     weight_low = weight_low.reshape(2, MODES, channels, channels)

time: 125 us -> 122 us (0.976)
  blocking collectives: 49.9 us -> 46.7 us
  matrix products: 6.01 us -> 4.47 us
    all_gather x1, blocking collectives: 30.4 us -> 27.1 us  [on_device(): weight_low = lax.all_gather(group_low, 'dp', axis=0, tiled=True)]
    dot_general x8 -> x4, matrix products: 2.46 us -> 0.92 us  [the longest x2 0.52 us: inverse_cells(): jnp.einsum('slcg,gx->scxl', both, basis, preferred_element_type=jnp.float32)]
  transfers between devices with their start and end apart: 4 -> 4, of which waited for: 2 -> 2; matrix products, arithmetic and copies ran while one was open for 5% -> 7% of each run, Pallas kernels for 0% -> 0%
where the time goes in v7:
time: 122 us; the launch traced here: 121 us
  blocking collectives  46.7 us (38%)
  starting transfers between devices  38.1 us (31%)
  waiting for transfers between devices  15 us (12%)
  local copies, waits for them, and re-layouts  12.2 us (10%)
  matrix products  4.47 us (4%)
  other arithmetic  3.92 us (3%)
    all_gather x1, blocking collectives, on_device(): weight_low = lax.all_gather(group_low, 'dp', axis=0, tiled=True)  27.1 us
    all_gather x1, blocking collectives, on_device(): every_group = lax.all_gather(group_grad, 'dp', axis=0, tiled=False)  19.6 us
    all_to_all x1, starting transfers between devices, on_device(): group_grad = lax.all_to_all(grad_tiles, 'dom', 0, 0, tiled=True)  14.7 us
    all_to_all x1, starting transfers between devices, copy_for_each(): return lax.all_to_all(copies, axis, split_axis=0, concat_axis=0, tiled=True)  12.6 us
    all_to_all x1, waiting for transfers between devices, on_device(): group_grad = lax.all_to_all(grad_tiles, 'dom', 0, 0, tiled=True)  9.9 us
    unnamed x23, local copies, waits for them, and re-layouts  8.96 us
    all_to_all x1, starting transfers between devices, on_device(): lax.all_to_all(grad_lines, 'dom', split_axis=2, concat_axis=3, tiled=True)  5.82 us
    all_to_all x1, waiting for transfers between devices, copy_for_each(): return lax.all_to_all(copies, axis, split_axis=0, concat_axis=0, tiled=True)  5.11 us
  transfers between devices with their start and end apart: 4, of which 2 were waited for; matrix products, arithmetic and copies ran while one was open for 7% of the time, Pallas kernels for 0%

profile of v7, /device:TPU:1, one launch (start us, length us, event | category | flops | bytes accessed | tf_op | source)
XLA Modules:
  0.0 121.4 jit_solution(7235048655321989136)
XLA Ops:
  0.6 0.0 copy-start
  0.6 0.7 convert_element_type.125
  1.4 0.7 reshape.148
  2.1 12.6 %all-to-all-start.1 = ((bf16[64,2,128]{2,1,0:T(2,128)(2,1)}), bf16[64,2,128]{2,1,0:T(2,128)(2,1)S(1)}, u32[]{:S(2)}, u32[]{:S(2)}) async-start(bf16[64,2,128]{2,1,0:T(2,128)(2,1)} %reshape.148), calls=%async_computation.1 | async-start | bytes 65536 | tf_op jit(solution)/shard_map/all_to_all | solution.py:27
  14.6 0.0 copy-start.1
  14.6 1.5 %copy.63 = bf16[1,64,8,256]{1,2,0,3:T(8,128)(2,1)S(1)} copy(bf16[1,64,8,256]{3,2,1,0:T(8,128)(2,1)} %param.9) | data formatting | bytes 524288 | tf_op args[1]
  16.1 0.4 copy.62
  16.5 0.2 fusion.82
  16.8 1.5 %reshape.146 = bf16[64,2,2048]{2,1,0:T(2,128)(2,1)} reshape(bf16[256,2,8,64]{3,2,1,0:T(8,128)(2,1)S(1)} %fusion.82) | data formatting | bytes 1048576
  18.3 5.1 %all-to-all-done.1 = bf16[64,2,128]{2,1,0:T(2,128)(2,1)S(1)} async-done(((bf16[64,2,128]{2,1,0:T(2,128)(2,1)}), bf16[64,2,128]{2,1,0:T(2,128)(2,1)S(1)}, u32[]{:S(2)}, u32[]{:S(2)}) %all-to-all-start.1) | async-done | bytes 32800 | tf_op jit(solution)/shard_map/all_to_all | solution.py:27
  23.4 5.0 %all-to-all-start = ((bf16[64,2,2048]{2,1,0:T(2,128)(2,1)}), bf16[64,2,2048]{2,1,0:T(2,128)(2,1)S(1)}, u32[]{:S(2)}, u32[]{:S(2)}) async-start(bf16[64,2,2048]{2,1,0:T(2,128)(2,1)} %reshape.146), calls=%async_computation | async-start | bytes 1048576 | tf_op jit(solution)/shard_map/all_to_all | solution.py:37
  28.5 0.6 copy-done.5
  29.1 0.6 dynamic_slice.7
  29.7 0.6 compare_convert_fusion
  30.3 0.7 compare_select_fusion.1
  31.0 0.1 fusion.50
  31.2 0.1 multiply_convert_fusion.1
  31.3 0.1 reshape.149
  31.4 27.1 %all_gather.9 = bf16[2048,64]{1,0:T(8,128)(2,1)S(1)} all-gather(bf16[256,64]{1,0:T(8,128)(2,1)S(1)} %bitcast.164), channel_id=1, replica_groups=mesh['dp'=8,'dom'=64] {'dp'}, dimensions={0}, use_global_device_ids=true | all-gather | bytes 294912 | tf_op jit(solution)/shard_map/all_gather | solution.py:119
  58.6 0.7 reshape.147
  59.2 0.1 copy.64
  59.3 0.2 fusion.80
  59.5 0.1 copy.145
  59.6 0.3 copy.74
  59.9 0.2 fusion.14
  60.1 0.2 fusion.69
  60.3 0.2 fusion.75
  60.5 0.2 fusion.24
  60.7 0.2 fusion.23
  60.9 0.3 fusion.8
  61.2 0.4 copy-done.6
  61.6 0.5 fusion.35
  62.0 0.2 convolution_bitcast_fusion.2
  62.2 0.1 fusion.51
  62.3 0.3 fusion.55
  62.6 0.3 fusion.62
  62.9 0.3 fusion.6
  63.2 0.3 fusion.7
  63.5 0.1 pad_maximum_fusion.1
  63.6 0.2 copy.147
  63.8 1.0 reshape.150
  64.8 14.7 %all-to-all-start.2 = ((bf16[64,2,1024]{2,1,0:T(2,128)(2,1)}), bf16[64,2,1024]{2,1,0:T(2,128)(2,1)S(1)}, u32[]{:S(2)}, u32[]{:S(2)}) async-start(bf16[64,2,1024]{2,1,0:T(2,128)(2,1)} %reshape.150), calls=%async_computation.2 | async-start | bytes 524288 | tf_op jit(solution)/shard_map/all_to_all | solution.py:174
  79.6 0.2 fusion.58
  79.8 0.3 fusion.19
  80.0 0.2 fusion.65
  80.3 0.3 fusion.20
  80.5 0.1 maximum_bitcast_fusion.2
  80.6 0.3 fusion.9
  80.9 0.3 fusion.3
  81.1 9.9 %all-to-all-done.2 = bf16[64,2,1024]{2,1,0:T(2,128)(2,1)S(1)} async-done(((bf16[64,2,1024]{2,1,0:T(2,128)(2,1)}), bf16[64,2,1024]{2,1,0:T(2,128)(2,1)S(1)}, u32[]{:S(2)}, u32[]{:S(2)}) %all-to-all-start.2) | async-done | bytes 262176 | tf_op jit(solution)/shard_map/all_to_all | solution.py:174
  91.0 0.3 reshape.151
  91.4 0.3 copy.90
  91.7 1.0 reshape.152
  92.7 5.8 %all-to-all-start.3 = ((bf16[64,2,1024]{2,1,0:T(2,128)(2,1)}), bf16[64,2,1024]{2,1,0:T(2,128)(2,1)S(1)}, u32[]{:S(2)}, u32[]{:S(2)}) async-start(bf16[64,2,1024]{2,1,0:T(2,128)(2,1)} %reshape.152), calls=%async_computation.3 | async-start | bytes 524288 | tf_op jit(solution)/shard_map/all_to_all | solution.py:176
  98.5 0.3 convert_reduce_fusion
  98.8 19.6 %all-gather = f32[64,4,64]{2,1,0:T(4,128)S(1)} all-gather(f32[8,4,64]{2,1,0:T(4,128)S(1)} %convert_reduce_fusion), channel_id=2, replica_groups=mesh['dp'=8,'dom'=64] {'dp'}, dimensions={0}, use_global_device_ids=true | all-gather | bytes 73728 | tf_op jit(solution)/shard_map/all_gather | solution.py:178
  118.4 0.7 copy-done.2
  119.1 0.0 copy-done.3
  119.1 0.0 copy-done.4
  119.1 0.6 multiply_subtract_fusion
  119.7 0.3 reshape.153
  120.1 0.1 copy.146
  120.1 0.1 copy.92
  120.2 1.1 copy.93
  (15 shorter events, 0.1 us)
Async XLA Ops:
  0.6 60.6 %copy-start = (bf16[64,64]{1,0:T(8,128)(2,1)S(1)}, bf16[64,64]{1,0:T(8,128)(2,1)}, u32[]{:S(2)}) copy-start(bf16[64,64]{1,0:T(8,128)(2,1)} %param.13) | copy-start | bytes 24580
  2.1 21.4 %all-to-all-start.1 = ((bf16[64,2,128]{2,1,0:T(2,128)(2,1)}), bf16[64,2,128]{2,1,0:T(2,128)(2,1)S(1)}, u32[]{:S(2)}, u32[]{:S(2)}) async-start(bf16[64,2,128]{2,1,0:T(2,128)(2,1)} %reshape.148), calls=%async_computation.1 | async-start | bytes 65536 | tf_op jit(solution)/shard_map/all_to_all | solution.py:27
  14.6 1.5 %copy-start.1 = (bf16[1,64,8,256]{3,2,1,0:T(8,128)(2,1)S(1)}, bf16[1,64,8,256]{3,2,1,0:T(8,128)(2,1)}, u32[]{:S(2)}) copy-start(bf16[1,64,8,256]{3,2,1,0:T(8,128)(2,1)} %param.8) | copy-start | bytes 786436
  23.4 35.1 %all-to-all-start = ((bf16[64,2,2048]{2,1,0:T(2,128)(2,1)}), bf16[64,2,2048]{2,1,0:T(2,128)(2,1)S(1)}, u32[]{:S(2)}, u32[]{:S(2)}) async-start(bf16[64,2,2048]{2,1,0:T(2,128)(2,1)} %reshape.146), calls=%async_computation | async-start | bytes 1048576 | tf_op jit(solution)/shard_map/all_to_all | solution.py:37
  28.4 0.7 copy-start.5
  60.9 0.7 copy-start.6
  64.8 26.2 %all-to-all-start.2 = ((bf16[64,2,1024]{2,1,0:T(2,128)(2,1)}), bf16[64,2,1024]{2,1,0:T(2,128)(2,1)S(1)}, u32[]{:S(2)}, u32[]{:S(2)}) async-start(bf16[64,2,1024]{2,1,0:T(2,128)(2,1)} %reshape.150), calls=%async_computation.2 | async-start | bytes 524288 | tf_op jit(solution)/shard_map/all_to_all | solution.py:174
  92.7 27.0 %all-to-all-start.3 = ((bf16[64,2,1024]{2,1,0:T(2,128)(2,1)}), bf16[64,2,1024]{2,1,0:T(2,128)(2,1)S(1)}, u32[]{:S(2)}, u32[]{:S(2)}) async-start(bf16[64,2,1024]{2,1,0:T(2,128)(2,1)} %reshape.152), calls=%async_computation.3 | async-start | bytes 524288 | tf_op jit(solution)/shard_map/all_to_all | solution.py:176
  118.4 0.7 copy-start.2
  118.4 0.7 copy-start.3
  118.4 0.7 copy-start.4

commit v8 on v7

--- a/solution.py
+++ b/solution.py
@@ -115,12 +115,15 @@
     )
     keep_wide = keep_modes[:, None, None, :]
     weight_short = spectral_weight.astype(jnp.bfloat16)
-    group_low = collect(weight_short, "dom", 0)
-    weight_low = lax.all_gather(group_low, "dp", axis=0, tiled=True)
-    weight_low = weight_low.reshape(2, MODES, channels, channels)
+    density_lines, upstream_lines = in_one_piece((density, upstream), "dom", 3, 2, 0)
+    column_low = lax.all_gather(weight_short, "dp", axis=0, tiled=False)
+    column_low, density_lines, upstream_lines = lax.optimization_barrier(
+        (column_low, density_lines, upstream_lines)
+    )
+    every_low = copy_for_each(column_low, "dom")
+    weight_low = jnp.moveaxis(every_low, 0, 1).reshape(2, MODES, channels, channels)
     weight_real = weight_low[0]
     weight_imag = weight_low[1]
-    density_lines, upstream_lines = in_one_piece((density, upstream), "dom", 3, 2, 0)
     real_part, imag_part = forward_parts(density_lines, cosines, sines)
     spec_real = real_part.astype(jnp.bfloat16)
     spec_imag = imag_part.astype(jnp.bfloat16)

time: 122 us -> 120 us (0.984)
  blocking collectives: 46.7 us -> 44.1 us
  waiting for transfers between devices: 15 us -> 17.1 us
  starting transfers between devices: 38.1 us -> 36.2 us
    all_to_all x1, starting transfers between devices: 14.7 us -> 5.85 us  [on_device(): group_grad = lax.all_to_all(grad_tiles, 'dom', 0, 0, tiled=True)]
    all_to_all x1, starting transfers between devices: 4.99 us -> 12.7 us  [in_one_piece(): lax.all_to_all(both, axis, split_axis=split_dim, concat_axis=concat_dim,...]
    all_gather x1, blocking collectives: 27.1 us -> 23.4 us  [on_device(): column_low = lax.all_gather(weight_short, 'dp', axis=0, tiled=False)]
    all_to_all x1, waiting for transfers between devices: 5.11 us -> 8.18 us  [copy_for_each(): return lax.all_to_all(copies, axis, split_axis=0, concat_axis=0, tiled=True)]
    all_to_all x1, starting transfers between devices: 12.6 us -> 11.2 us  [copy_for_each(): return lax.all_to_all(copies, axis, split_axis=0, concat_axis=0, tiled=True)]
  transfers between devices with their start and end apart: 4 -> 4, of which waited for: 2 -> 2; matrix products, arithmetic and copies ran while one was open for 7% -> 4% of each run, Pallas kernels for 0% -> 0%
where the time goes in v8:
time: 120 us; the launch traced here: 119 us
  blocking collectives  44.1 us (37%)
  starting transfers between devices  36.2 us (30%)
  waiting for transfers between devices  17.1 us (14%)
  local copies, waits for them, and re-layouts  13.2 us (11%)
  matrix products  4.49 us (4%)
  other arithmetic  3.05 us (3%)
    all_gather x1, blocking collectives, on_device(): column_low = lax.all_gather(weight_short, 'dp', axis=0, tiled=False)  23.4 us
    all_gather x1, blocking collectives, on_device(): every_group = lax.all_gather(group_grad, 'dp', axis=0, tiled=False)  20.7 us
    all_to_all x1, starting transfers between devices, in_one_piece(): lax.all_to_all(both, axis, split_axis=split_dim, concat_axis=concat_dim,...  12.7 us
    all_to_all x1, starting transfers between devices, copy_for_each(): return lax.all_to_all(copies, axis, split_axis=0, concat_axis=0, tiled=True)  11.2 us
    unnamed x23, local copies, waits for them, and re-layouts  9.48 us
    all_to_all x1, waiting for transfers between devices, on_device(): group_grad = lax.all_to_all(grad_tiles, 'dom', 0, 0, tiled=True)  8.9 us
    all_to_all x1, waiting for transfers between devices, copy_for_each(): return lax.all_to_all(copies, axis, split_axis=0, concat_axis=0, tiled=True)  8.18 us
    all_to_all x1, starting transfers between devices, on_device(): lax.all_to_all(grad_lines, 'dom', split_axis=2, concat_axis=3, tiled=True)  6.5 us
  transfers between devices with their start and end apart: 4, of which 2 were waited for; matrix products, arithmetic and copies ran while one was open for 4% of the time, Pallas kernels for 0%

profile of v8, /device:TPU:1, one launch (start us, length us, event | category | flops | bytes accessed | tf_op | source)
XLA Modules:
  0.0 119.2 jit_solution(6219955645086699758)
XLA Ops:
  0.7 1.5 %copy.62 = bf16[1,64,8,256]{1,2,0,3:T(8,128)(2,1)S(1)} copy(bf16[1,64,8,256]{3,2,1,0:T(8,128)(2,1)} %param.8) | data formatting | bytes 524288 | tf_op args[0]
  2.1 0.4 copy.63
  2.6 0.2 fusion.80
  2.8 1.5 %reshape.129 = bf16[64,2,2048]{2,1,0:T(2,128)(2,1)} reshape(bf16[256,2,8,64]{3,2,1,0:T(8,128)(2,1)S(1)} %fusion.80) | data formatting | bytes 1048576
  4.3 12.7 %all-to-all-start = ((bf16[64,2,2048]{2,1,0:T(2,128)(2,1)}), bf16[64,2,2048]{2,1,0:T(2,128)(2,1)S(1)}, u32[]{:S(2)}, u32[]{:S(2)}) async-start(bf16[64,2,2048]{2,1,0:T(2,128)(2,1)} %reshape.129), calls=%async_computation | async-start | bytes 1048576 | tf_op jit(solution)/shard_map/all_to_all | solution.py:37
  17.1 23.4 %all-gather.2 = bf16[8,4,64]{2,1,0:T(4,128)(2,1)S(1)} all-gather(bf16[1,4,64]{2,1,0:T(4,128)(2,1)S(1)} %convert_bitcast_fusion), channel_id=2, replica_groups=mesh['dp'=8,'dom'=64] {'dp'}, dimensions={0}, use_global_device_ids=true | all-gather | bytes 4608 | tf_op jit(solution)/shard_map/all_gather | solution.py:119
  40.5 0.7 reshape.130
  41.1 0.1 copy.64
  41.2 0.1 fusion.78
  41.3 0.2 copy_bitcast_fusion.2
  41.5 0.1 broadcast_in_dim.10
  41.6 1.0 reshape.131
  42.6 11.2 %all-to-all-start.1 = ((bf16[64,2,1024]{2,1,0:T(2,128)(2,1)}), bf16[64,2,1024]{2,1,0:T(2,128)(2,1)S(1)}, u32[]{:S(2)}, u32[]{:S(2)}) async-start(bf16[64,2,1024]{2,1,0:T(2,128)(2,1)} %reshape.131), calls=%async_computation.1 | async-start | bytes 524288 | tf_op jit(solution)/shard_map/all_to_all | solution.py:27
  53.8 0.6 copy-done.5
  54.5 0.6 dynamic_slice.7
  55.1 0.6 compare_convert_fusion
  55.7 0.7 compare_select_fusion.1
  56.4 0.1 fusion.48
  56.5 0.1 multiply_convert_fusion.1
  56.7 0.2 copy.67
  56.9 0.2 fusion.12
  57.1 8.2 %all-to-all-done.1 = bf16[64,2,1024]{2,1,0:T(2,128)(2,1)S(1)} async-done(((bf16[64,2,1024]{2,1,0:T(2,128)(2,1)}), bf16[64,2,1024]{2,1,0:T(2,128)(2,1)S(1)}, u32[]{:S(2)}, u32[]{:S(2)}) %all-to-all-start.1) | async-done | bytes 262176 | tf_op jit(solution)/shard_map/all_to_all | solution.py:27
  65.3 0.3 reshape.132
  65.6 0.2 fusion.79
  65.8 0.1 copy.71
  65.9 0.1 copy.68
  66.0 0.2 fusion.67
  66.2 0.2 fusion.73
  66.4 0.2 fusion.23
  66.6 0.2 fusion.24
  66.8 0.3 fusion.8
  67.1 0.4 copy-done.6
  67.4 0.5 fusion.35
  67.9 0.2 convolution_bitcast_fusion.2
  68.1 0.1 fusion.49
  68.2 0.3 fusion.60
  68.5 0.3 fusion.53
  68.8 0.3 fusion.7
  69.1 0.3 fusion.6
  69.4 0.1 pad_maximum_fusion.1
  69.5 0.2 copy.141
  69.7 1.0 reshape.133
  70.7 5.8 %all-to-all-start.2 = ((bf16[64,2,1024]{2,1,0:T(2,128)(2,1)}), bf16[64,2,1024]{2,1,0:T(2,128)(2,1)S(1)}, u32[]{:S(2)}, u32[]{:S(2)}) async-start(bf16[64,2,1024]{2,1,0:T(2,128)(2,1)} %reshape.133), calls=%async_computation.2 | async-start | bytes 524288 | tf_op jit(solution)/shard_map/all_to_all | solution.py:177
  76.6 0.2 fusion.56
  76.8 0.3 fusion.19
  77.0 0.2 fusion.63
  77.3 0.3 fusion.20
  77.5 0.1 maximum_bitcast_fusion.2
  77.6 0.3 fusion.9
  77.9 0.3 fusion.3
  78.1 8.9 %all-to-all-done.2 = bf16[64,2,1024]{2,1,0:T(2,128)(2,1)S(1)} async-done(((bf16[64,2,1024]{2,1,0:T(2,128)(2,1)}), bf16[64,2,1024]{2,1,0:T(2,128)(2,1)S(1)}, u32[]{:S(2)}, u32[]{:S(2)}) %all-to-all-start.2) | async-done | bytes 262176 | tf_op jit(solution)/shard_map/all_to_all | solution.py:177
  87.1 0.3 reshape.134
  87.4 0.3 copy.92
  87.7 1.0 reshape.135
  88.7 6.5 %all-to-all-start.3 = ((bf16[64,2,1024]{2,1,0:T(2,128)(2,1)}), bf16[64,2,1024]{2,1,0:T(2,128)(2,1)S(1)}, u32[]{:S(2)}, u32[]{:S(2)}) async-start(bf16[64,2,1024]{2,1,0:T(2,128)(2,1)} %reshape.135), calls=%async_computation.3 | async-start | bytes 524288 | tf_op jit(solution)/shard_map/all_to_all | solution.py:179
  95.2 0.3 convert_reduce_fusion
  95.5 20.7 %all-gather.1 = f32[64,4,64]{2,1,0:T(4,128)S(1)} all-gather(f32[8,4,64]{2,1,0:T(4,128)S(1)} %convert_reduce_fusion), channel_id=3, replica_groups=mesh['dp'=8,'dom'=64] {'dp'}, dimensions={0}, use_global_device_ids=true | all-gather | bytes 73728 | tf_op jit(solution)/shard_map/all_gather | solution.py:181
  116.3 0.7 copy-done.3
  116.9 0.0 copy-done.4
  117.0 0.6 multiply_subtract_fusion
  117.6 0.3 reshape.136
  117.9 0.1 copy.140
  118.0 0.1 copy.94
  118.1 1.1 copy.95
  (17 shorter events, 0.1 us)
Async XLA Ops:
  0.6 66.4 %copy-start = (bf16[64,64]{1,0:T(8,128)(2,1)S(1)}, bf16[64,64]{1,0:T(8,128)(2,1)}, u32[]{:S(2)}) copy-start(bf16[64,64]{1,0:T(8,128)(2,1)} %param.13) | copy-start | bytes 24580
  0.6 1.5 %copy-start.1 = (bf16[1,64,8,256]{3,2,1,0:T(8,128)(2,1)S(1)}, bf16[1,64,8,256]{3,2,1,0:T(8,128)(2,1)}, u32[]{:S(2)}) copy-start(bf16[1,64,8,256]{3,2,1,0:T(8,128)(2,1)} %param.9) | copy-start | bytes 786436
  4.3 12.7 %copy-start.2 = (f32[4,64]{1,0:T(4,128)S(1)}, f32[4,64]{1,0:T(4,128)}, u32[]{:S(2)}) copy-start(f32[4,64]{1,0:T(4,128)} %param.10) | copy-start | bytes 3076
  4.3 36.1 %all-to-all-start = ((bf16[64,2,2048]{2,1,0:T(2,128)(2,1)}), bf16[64,2,2048]{2,1,0:T(2,128)(2,1)S(1)}, u32[]{:S(2)}, u32[]{:S(2)}) async-start(bf16[64,2,2048]{2,1,0:T(2,128)(2,1)} %reshape.129), calls=%async_computation | async-start | bytes 1048576 | tf_op jit(solution)/shard_map/all_to_all | solution.py:37
  42.6 22.6 %all-to-all-start.1 = ((bf16[64,2,1024]{2,1,0:T(2,128)(2,1)}), bf16[64,2,1024]{2,1,0:T(2,128)(2,1)S(1)}, u32[]{:S(2)}, u32[]{:S(2)}) async-start(bf16[64,2,1024]{2,1,0:T(2,128)(2,1)} %reshape.131), calls=%async_computation.1 | async-start | bytes 524288 | tf_op jit(solution)/shard_map/all_to_all | solution.py:27
  53.8 0.7 copy-start.5
  66.8 0.7 copy-start.6
  70.7 16.3 %all-to-all-start.2 = ((bf16[64,2,1024]{2,1,0:T(2,128)(2,1)}), bf16[64,2,1024]{2,1,0:T(2,128)(2,1)S(1)}, u32[]{:S(2)}, u32[]{:S(2)}) async-start(bf16[64,2,1024]{2,1,0:T(2,128)(2,1)} %reshape.133), calls=%async_computation.2 | async-start | bytes 524288 | tf_op jit(solution)/shard_map/all_to_all | solution.py:177
  88.7 28.8 %all-to-all-start.3 = ((bf16[64,2,1024]{2,1,0:T(2,128)(2,1)}), bf16[64,2,1024]{2,1,0:T(2,128)(2,1)S(1)}, u32[]{:S(2)}, u32[]{:S(2)}) async-start(bf16[64,2,1024]{2,1,0:T(2,128)(2,1)} %reshape.135), calls=%async_computation.3 | async-start | bytes 524288 | tf_op jit(solution)/shard_map/all_to_all | solution.py:179
  116.3 0.7 copy-start.3
  116.3 0.7 copy-start.4

commit v9 on v8

--- a/solution.py
+++ b/solution.py
@@ -115,12 +115,18 @@
     )
     keep_wide = keep_modes[:, None, None, :]
     weight_short = spectral_weight.astype(jnp.bfloat16)
-    density_lines, upstream_lines = in_one_piece((density, upstream), "dom", 3, 2, 0)
+    rows_here = spectral_weight.shape[0]
     column_low = lax.all_gather(weight_short, "dp", axis=0, tiled=False)
-    column_low, density_lines, upstream_lines = lax.optimization_barrier(
-        (column_low, density_lines, upstream_lines)
-    )
-    every_low = copy_for_each(column_low, "dom")
+    tile_shape = (channels, slab_rows, line_count // lax.axis_size("dom"))
+    column_tiles = jnp.broadcast_to(
+        column_low.reshape(channels, slab_rows, 1, tile_shape[2]),
+        (channels, slab_rows, lax.axis_size("dom"), tile_shape[2]),
+    ).reshape(density.shape)
+    density_lines, upstream_lines, column_lines = in_one_piece(
+        (density, upstream, column_tiles), "dom", 3, 2, 0
+    )
+    every_low = column_lines.reshape(channels, lax.axis_size("dom"), *tile_shape[1:])
+    every_low = jnp.moveaxis(every_low, 1, 0).reshape(lax.axis_size("dom"), -1, rows_here, channels)
     weight_low = jnp.moveaxis(every_low, 0, 1).reshape(2, MODES, channels, channels)
     weight_real = weight_low[0]
     weight_imag = weight_low[1]

time: 120 us -> 117 us (0.975)
  starting transfers between devices: 36.2 us -> 21 us
  waiting for transfers between devices: 17.1 us -> 29.9 us
  blocking collectives: 44.1 us -> 42.4 us
    all_to_all x1, waiting for transfers between devices: 0.01 us -> 20.7 us  [in_one_piece(): lax.all_to_all(both, axis, split_axis=split_dim, concat_axis=concat_dim,...]
    all_to_all x1 -> x0, starting transfers between devices: 11.2 us -> none  [copy_for_each(): return lax.all_to_all(copies, axis, split_axis=0, concat_axis=0, tiled=True)]
    all_to_all x1 -> x0, waiting for transfers between devices: 8.18 us -> none  [copy_for_each(): return lax.all_to_all(copies, axis, split_axis=0, concat_axis=0, tiled=True)]
    all_to_all x1, starting transfers between devices: 12.7 us -> 9.02 us  [in_one_piece(): lax.all_to_all(both, axis, split_axis=split_dim, concat_axis=concat_dim,...]
    unnamed x23 -> x19, local copies, waits for them, and re-layouts: 9.48 us -> 8.1 us
  transfers between devices with their start and end apart: 4 -> 3, of which waited for: 2 -> 2; matrix products, arithmetic and copies ran while one was open for 4% -> 4% of each run, Pallas kernels for 0% -> 0%
where the time goes in v9:
time: 117 us; the launch traced here: 116 us
  blocking collectives  42.4 us (36%)
  waiting for transfers between devices  29.9 us (26%)
  starting transfers between devices  21 us (18%)
  local copies, waits for them, and re-layouts  13.4 us (11%)
  matrix products  4.47 us (4%)
  other arithmetic  4.17 us (4%)
    all_gather x1, blocking collectives, on_device(): column_low = lax.all_gather(weight_short, 'dp', axis=0, tiled=False)  22.6 us
    all_to_all x1, waiting for transfers between devices, in_one_piece(): lax.all_to_all(both, axis, split_axis=split_dim, concat_axis=concat_dim,...  20.7 us
    all_gather x1, blocking collectives, on_device(): every_group = lax.all_gather(group_grad, 'dp', axis=0, tiled=False)  19.8 us
    all_to_all x1, waiting for transfers between devices, on_device(): group_grad = lax.all_to_all(grad_tiles, 'dom', 0, 0, tiled=True)  9.19 us
    all_to_all x1, starting transfers between devices, in_one_piece(): lax.all_to_all(both, axis, split_axis=split_dim, concat_axis=concat_dim,...  9.02 us
    unnamed x19, local copies, waits for them, and re-layouts  8.1 us
    all_to_all x1, starting transfers between devices, on_device(): lax.all_to_all(grad_lines, 'dom', split_axis=2, concat_axis=3, tiled=True)  6.33 us
    all_to_all x1, starting transfers between devices, on_device(): group_grad = lax.all_to_all(grad_tiles, 'dom', 0, 0, tiled=True)  5.62 us
  transfers between devices with their start and end apart: 3, of which 2 were waited for; matrix products, arithmetic and copies ran while one was open for 4% of the time, Pallas kernels for 0%

profile of v9, /device:TPU:1, one launch (start us, length us, event | category | flops | bytes accessed | tf_op | source)
XLA Modules:
  0.0 116.4 jit_solution(993937237455035663)
XLA Ops:
  0.6 0.0 copy-start
  0.6 0.7 convert_bitcast_fusion
  1.3 22.6 %all-gather.2 = bf16[8,4,64]{2,1,0:T(4,128)(2,1)S(1)} all-gather(bf16[1,4,64]{2,1,0:T(4,128)(2,1)S(1)} %convert_bitcast_fusion), channel_id=2, replica_groups=mesh['dp'=8,'dom'=64] {'dp'}, dimensions={0}, use_global_device_ids=true | all-gather | bytes 4608 | tf_op jit(solution)/shard_map/all_gather | solution.py:119
  24.0 0.2 broadcast_in_dim.12
  24.1 0.2 copy.66
  24.3 1.4 %copy.67 = bf16[1,64,8,256]{1,2,3,0:T(8,128)(2,1)S(1)} copy(bf16[1,64,8,256]{3,2,1,0:T(8,128)(2,1)} %param.8) | data formatting | bytes 524288 | tf_op args[0]
  25.7 1.4 %copy.68 = bf16[1,64,8,256]{1,2,3,0:T(8,128)(2,1)S(1)} copy(bf16[1,64,8,256]{3,2,1,0:T(8,128)(2,1)} %param.9) | data formatting | bytes 524288 | tf_op args[1]
  27.2 0.1 broadcast_in_dim.13
  27.3 0.4 copy_bitcast_fusion.3
  27.7 0.0 copy-start.4
  27.7 1.7 %reshape.163 = bf16[64,2,3072]{2,1,0:T(2,128)(2,1)} reshape(bf16[256,3,8,64]{3,2,1,0:T(8,128)(2,1)S(1)} %copy_bitcast_fusion.3) | data formatting | bytes 1572864
  29.3 9.0 %all-to-all-start = ((bf16[64,2,3072]{2,1,0:T(2,128)(2,1)}), bf16[64,2,3072]{2,1,0:T(2,128)(2,1)S(1)}, u32[]{:S(2)}, u32[]{:S(2)}) async-start(bf16[64,2,3072]{2,1,0:T(2,128)(2,1)} %reshape.163), calls=%async_computation | async-start | bytes 1572864 | tf_op jit(solution)/shard_map/all_to_all | solution.py:37
  38.4 0.6 dynamic_slice.7
  39.0 0.6 compare_convert_fusion
  39.6 0.7 compare_select_fusion.1
  40.3 0.1 fusion.50
  40.4 0.1 multiply_convert_fusion.1
  40.6 20.7 %all-to-all-done = bf16[64,2,3072]{2,1,0:T(2,128)(2,1)S(1)} async-done(((bf16[64,2,3072]{2,1,0:T(2,128)(2,1)}), bf16[64,2,3072]{2,1,0:T(2,128)(2,1)S(1)}, u32[]{:S(2)}, u32[]{:S(2)}) %all-to-all-start) | async-done | bytes 786464 | tf_op jit(solution)/shard_map/all_to_all | solution.py:37
  61.3 0.9 reshape.164
  62.2 0.3 copy.70
  62.5 0.3 fusion.80
  62.8 0.2 fusion.12
  63.0 1.1 copy.72
  64.1 0.2 copy.73
  64.3 0.2 copy.77
  64.5 0.2 fusion.75
  64.7 0.2 fusion.69
  64.9 0.2 fusion.24
  65.1 0.2 fusion.23
  65.3 0.3 fusion.8
  65.6 0.0 copy-start.5
  65.6 0.1 copy.155
  65.7 0.3 copy.83
  66.0 0.2 copy-done.5
  66.2 0.5 fusion.35
  66.7 0.2 convolution_bitcast_fusion.2
  66.9 0.1 fusion.51
  67.0 0.3 fusion.62
  67.3 0.3 fusion.55
  67.6 0.3 fusion.7
  67.9 0.3 fusion.6
  68.1 0.1 pad_maximum_fusion.1
  68.3 0.2 copy.157
  68.5 1.0 reshape.165
  69.5 5.6 %all-to-all-start.1 = ((bf16[64,2,1024]{2,1,0:T(2,128)(2,1)}), bf16[64,2,1024]{2,1,0:T(2,128)(2,1)S(1)}, u32[]{:S(2)}, u32[]{:S(2)}) async-start(bf16[64,2,1024]{2,1,0:T(2,128)(2,1)} %reshape.165), calls=%async_computation.1 | async-start | bytes 524288 | tf_op jit(solution)/shard_map/all_to_all | solution.py:183
  75.1 0.2 fusion.65
  75.3 0.3 fusion.20
  75.6 0.2 fusion.58
  75.8 0.3 fusion.19
  76.1 0.1 maximum_bitcast_fusion.2
  76.1 0.3 fusion.9
  76.4 0.3 fusion.3
  76.7 9.2 %all-to-all-done.1 = bf16[64,2,1024]{2,1,0:T(2,128)(2,1)S(1)} async-done(((bf16[64,2,1024]{2,1,0:T(2,128)(2,1)}), bf16[64,2,1024]{2,1,0:T(2,128)(2,1)S(1)}, u32[]{:S(2)}, u32[]{:S(2)}) %all-to-all-start.1) | async-done | bytes 262176 | tf_op jit(solution)/shard_map/all_to_all | solution.py:183
  85.9 0.3 reshape.166
  86.3 0.3 copy.99
  86.6 1.0 reshape.167
  87.6 6.3 %all-to-all-start.2 = ((bf16[64,2,1024]{2,1,0:T(2,128)(2,1)}), bf16[64,2,1024]{2,1,0:T(2,128)(2,1)S(1)}, u32[]{:S(2)}, u32[]{:S(2)}) async-start(bf16[64,2,1024]{2,1,0:T(2,128)(2,1)} %reshape.167), calls=%async_computation.2 | async-start | bytes 524288 | tf_op jit(solution)/shard_map/all_to_all | solution.py:185
  93.9 0.3 convert_reduce_fusion
  94.2 19.8 %all-gather.1 = f32[64,4,64]{2,1,0:T(4,128)S(1)} all-gather(f32[8,4,64]{2,1,0:T(4,128)S(1)} %convert_reduce_fusion), channel_id=3, replica_groups=mesh['dp'=8,'dom'=64] {'dp'}, dimensions={0}, use_global_device_ids=true | all-gather | bytes 73728 | tf_op jit(solution)/shard_map/all_gather | solution.py:187
  114.1 0.6 multiply_subtract_fusion
  114.7 0.3 reshape.168
  115.0 0.1 copy.156
  115.1 0.1 copy.101
  115.2 1.1 copy.102
  (14 shorter events, 0.1 us)
Async XLA Ops:
  0.6 65.4 %copy-start = (bf16[64,64]{1,0:T(8,128)(2,1)S(1)}, bf16[64,64]{1,0:T(8,128)(2,1)}, u32[]{:S(2)}) copy-start(bf16[64,64]{1,0:T(8,128)(2,1)} %param.13) | copy-start | bytes 24580
  27.7 10.7 %copy-start.4 = (s32[8]{0:T(128)S(1)}, s32[8]{0:T(128)}, u32[]{:S(2)}) copy-start(s32[8]{0:T(128)} %param.15) | copy-start | bytes 100
  29.3 31.9 %all-to-all-start = ((bf16[64,2,3072]{2,1,0:T(2,128)(2,1)}), bf16[64,2,3072]{2,1,0:T(2,128)(2,1)S(1)}, u32[]{:S(2)}, u32[]{:S(2)}) async-start(bf16[64,2,3072]{2,1,0:T(2,128)(2,1)} %reshape.163), calls=%async_computation | async-start | bytes 1572864 | tf_op jit(solution)/shard_map/all_to_all | solution.py:37
  65.6 0.7 copy-start.5
  69.5 16.4 %all-to-all-start.1 = ((bf16[64,2,1024]{2,1,0:T(2,128)(2,1)}), bf16[64,2,1024]{2,1,0:T(2,128)(2,1)S(1)}, u32[]{:S(2)}, u32[]{:S(2)}) async-start(bf16[64,2,1024]{2,1,0:T(2,128)(2,1)} %reshape.165), calls=%async_computation.1 | async-start | bytes 524288 | tf_op jit(solution)/shard_map/all_to_all | solution.py:183
  86.2 27.8 %copy-start.1 = (f32[4,64]{1,0:T(4,128)S(1)}, f32[4,64]{1,0:T(4,128)}, u32[]{:S(2)}) copy-start(f32[4,64]{1,0:T(4,128)} %param.10) | copy-start | bytes 3076
  86.2 27.8 %copy-start.2 = (f32[4,64]{1,0:T(4,128)S(1)}, f32[4,64]{1,0:T(4,128)}, u32[]{:S(2)}) copy-start(f32[4,64]{1,0:T(4,128)} %param.11) | copy-start | bytes 3076
  86.3 27.8 %copy-start.3 = (f32[4,64]{1,0:T(4,128)S(1)}, f32[4,64]{1,0:T(4,128)}, u32[]{:S(2)}) copy-start(f32[4,64]{1,0:T(4,128)} %param.12) | copy-start | bytes 3076
  87.6 27.1 %all-to-all-start.2 = ((bf16[64,2,1024]{2,1,0:T(2,128)(2,1)}), bf16[64,2,1024]{2,1,0:T(2,128)(2,1)S(1)}, u32[]{:S(2)}, u32[]{:S(2)}) async-start(bf16[64,2,1024]{2,1,0:T(2,128)(2,1)} %reshape.167), calls=%async_computation.2 | async-start | bytes 524288 | tf_op jit(solution)/shard_map/all_to_all | solution.py:185

commit v10 on v9

--- a/solution.py
+++ b/solution.py
@@ -180,13 +180,11 @@
         "oc,soxl->scxl", skip_weight, gate_lines, preferred_element_type=jnp.float32
     )
     grad_lines = (input_rows.astype(jnp.float32) + skip_back).astype(jnp.bfloat16)
-    group_grad = lax.all_to_all(grad_tiles, "dom", 0, 0, tiled=True)
-    grad_lines, group_grad = lax.optimization_barrier((grad_lines, group_grad))
+    owner_tiles = grad_local.reshape(groups * slabs, rows_here, channels)
+    arrived = lax.all_to_all(owner_tiles, ("dp", "dom"), 0, 0, tiled=True)
+    grad_lines, arrived = lax.optimization_barrier((grad_lines, arrived))
     input_grad = lax.all_to_all(grad_lines, "dom", split_axis=2, concat_axis=3, tiled=True)
-    group_grad = group_grad.astype(jnp.float32).sum(axis=0)
-    every_group = lax.all_gather(group_grad, "dp", axis=0, tiled=False)
-    mine = lax.dynamic_index_in_dim(every_group, lax.axis_index("dp"), 1, keepdims=False)
-    weight_grad = mine.sum(axis=0)
+    weight_grad = arrived.astype(jnp.float32).sum(axis=0)
     new_moment_one = beta_first * moment_one + (1.0 - beta_first) * weight_grad
     new_moment_two = beta_second * moment_two + (1.0 - beta_second) * weight_grad * weight_grad
     first_hat = new_moment_one / (1.0 - beta_first**STEP)

time: 117 us -> 126 us (1.077)
  waiting for transfers between devices: 29.9 us -> 53.3 us
  blocking collectives: 42.4 us -> 22.6 us
  starting transfers between devices: 21 us -> 26.6 us
    all_gather x1 -> x0, blocking collectives: 19.8 us -> none  [on_device(): every_group = lax.all_gather(group_grad, 'dp', axis=0, tiled=False)]
    all_to_all x1, waiting for transfers between devices: 9.19 us -> 22.8 us  [on_device(): arrived = lax.all_to_all(owner_tiles, ('dp', 'dom'), 0, 0, tiled=True)]
    all_to_all x1, waiting for transfers between devices: 0.01 us -> 9.87 us  [on_device(): lax.all_to_all(grad_lines, 'dom', split_axis=2, concat_axis=3, tiled=True)]
    all_to_all x1, starting transfers between devices: 5.62 us -> 12.1 us  [on_device(): arrived = lax.all_to_all(owner_tiles, ('dp', 'dom'), 0, 0, tiled=True)]
  transfers between devices with their start and end apart: 3 -> 3, of which waited for: 2 -> 3; matrix products, arithmetic and copies ran while one was open for 4% -> 4% of each run, Pallas kernels for 0% -> 0%
where the time goes in v10:
time: 126 us
  waiting for transfers between devices  53.3 us (42%)
  starting transfers between devices  26.6 us (21%)
  blocking collectives  22.6 us (18%)
  local copies, waits for them, and re-layouts  13.1 us (10%)
  matrix products  4.47 us (4%)
  other arithmetic  4.4 us (3%)
    all_to_all x1, waiting for transfers between devices, on_device(): arrived = lax.all_to_all(owner_tiles, ('dp', 'dom'), 0, 0, tiled=True)  22.8 us
    all_gather x1, blocking collectives, on_device(): column_low = lax.all_gather(weight_short, 'dp', axis=0, tiled=False)  22.6 us
    all_to_all x1, waiting for transfers between devices, in_one_piece(): lax.all_to_all(both, axis, split_axis=split_dim, concat_axis=concat_dim,...  20.7 us
    all_to_all x1, starting transfers between devices, on_device(): arrived = lax.all_to_all(owner_tiles, ('dp', 'dom'), 0, 0, tiled=True)  12.1 us
    all_to_all x1, waiting for transfers between devices, on_device(): lax.all_to_all(grad_lines, 'dom', split_axis=2, concat_axis=3, tiled=True)  9.87 us
    all_to_all x1, starting transfers between devices, in_one_piece(): lax.all_to_all(both, axis, split_axis=split_dim, concat_axis=concat_dim,...  9.02 us
    unnamed x19, local copies, waits for them, and re-layouts  8.05 us
    all_to_all x1, starting transfers between devices, on_device(): lax.all_to_all(grad_lines, 'dom', split_axis=2, concat_axis=3, tiled=True)  5.52 us
  transfers between devices with their start and end apart: 3, of which 3 were waited for; matrix products, arithmetic and copies ran while one was open for 4% of the time, Pallas kernels for 0%

profile of v10, /device:TPU:1, one launch (start us, length us, event | category | flops | bytes accessed | tf_op | source)
XLA Modules:
  0.0 125.6 jit_solution(2636393653466603201)
XLA Ops:
  0.6 0.0 copy-start
  0.6 0.7 convert_bitcast_fusion
  1.3 22.6 %all-gather.1 = bf16[8,4,64]{2,1,0:T(4,128)(2,1)S(1)} all-gather(bf16[1,4,64]{2,1,0:T(4,128)(2,1)S(1)} %convert_bitcast_fusion), channel_id=2, replica_groups=mesh['dp'=8,'dom'=64] {'dp'}, dimensions={0}, use_global_device_ids=true | all-gather | bytes 4608 | tf_op jit(solution)/shard_map/all_gather | solution.py:119
  24.0 0.2 broadcast_in_dim.12
  24.1 0.2 copy.66
  24.3 1.4 %copy.67 = bf16[1,64,8,256]{1,2,3,0:T(8,128)(2,1)S(1)} copy(bf16[1,64,8,256]{3,2,1,0:T(8,128)(2,1)} %param.8) | data formatting | bytes 524288 | tf_op args[0]
  25.7 1.4 %copy.68 = bf16[1,64,8,256]{1,2,3,0:T(8,128)(2,1)S(1)} copy(bf16[1,64,8,256]{3,2,1,0:T(8,128)(2,1)} %param.9) | data formatting | bytes 524288 | tf_op args[1]
  27.2 0.1 broadcast_in_dim.13
  27.3 0.4 copy_bitcast_fusion.2
  27.7 0.0 copy-start.4
  27.7 1.7 %reshape.162 = bf16[64,2,3072]{2,1,0:T(2,128)(2,1)} reshape(bf16[256,3,8,64]{3,2,1,0:T(8,128)(2,1)S(1)} %copy_bitcast_fusion.2) | data formatting | bytes 1572864
  29.3 9.0 %all-to-all-start = ((bf16[64,2,3072]{2,1,0:T(2,128)(2,1)}), bf16[64,2,3072]{2,1,0:T(2,128)(2,1)S(1)}, u32[]{:S(2)}, u32[]{:S(2)}) async-start(bf16[64,2,3072]{2,1,0:T(2,128)(2,1)} %reshape.162), calls=%async_computation | async-start | bytes 1572864 | tf_op jit(solution)/shard_map/all_to_all | solution.py:37
  38.4 0.6 dynamic_slice.3
  39.0 0.6 compare_convert_fusion
  39.6 0.7 compare_select_fusion.1
  40.3 0.1 fusion.50
  40.4 0.1 multiply_convert_fusion.1
  40.6 20.7 %all-to-all-done = bf16[64,2,3072]{2,1,0:T(2,128)(2,1)S(1)} async-done(((bf16[64,2,3072]{2,1,0:T(2,128)(2,1)}), bf16[64,2,3072]{2,1,0:T(2,128)(2,1)S(1)}, u32[]{:S(2)}, u32[]{:S(2)}) %all-to-all-start) | async-done | bytes 786464 | tf_op jit(solution)/shard_map/all_to_all | solution.py:37
  61.3 0.9 reshape.163
  62.2 0.3 copy.70
  62.5 0.3 fusion.80
  62.8 0.2 fusion.12
  63.0 1.1 copy.72
  64.1 0.2 copy.73
  64.3 0.2 copy.77
  64.5 0.2 fusion.75
  64.7 0.2 fusion.69
  64.9 0.2 fusion.24
  65.1 0.2 fusion.23
  65.3 0.3 fusion.8
  65.6 0.0 copy-start.5
  65.6 0.1 copy.153
  65.7 0.3 copy.83
  66.0 0.2 copy-done.5
  66.2 0.5 fusion.35
  66.7 0.2 convolution_bitcast_fusion.2
  66.9 0.1 fusion.51
  67.0 0.3 fusion.62
  67.3 0.3 fusion.55
  67.6 0.3 fusion.7
  67.9 0.3 fusion.6
  68.2 0.1 pad_maximum_fusion.1
  68.3 1.0 reshape.164
  69.2 12.1 %all-to-all-start.1 = ((bf16[512,2,128]{2,1,0:T(2,128)(2,1)}), bf16[512,2,128]{2,1,0:T(2,128)(2,1)S(1)}, u32[]{:S(2)}, u32[]{:S(2)}) async-start(bf16[512,2,128]{2,1,0:T(2,128)(2,1)} %reshape.164), calls=%async_computation.1 | async-start | bytes 524288 | tf_op jit(solution)/shard_map/all_to_all | solution.py:184
  81.3 0.2 fusion.65
  81.6 0.3 fusion.20
  81.8 0.2 fusion.58
  82.1 0.3 fusion.19
  82.3 0.1 maximum_bitcast_fusion.2
  82.4 0.3 fusion.9
  82.7 0.3 fusion.3
  83.0 0.0 copy-start.3
  83.0 22.8 %all-to-all-done.1 = bf16[512,2,128]{2,1,0:T(2,128)(2,1)S(1)} async-done(((bf16[512,2,128]{2,1,0:T(2,128)(2,1)}), bf16[512,2,128]{2,1,0:T(2,128)(2,1)S(1)}, u32[]{:S(2)}, u32[]{:S(2)}) %all-to-all-start.1) | async-done | bytes 262176 | tf_op jit(solution)/shard_map/all_to_all | solution.py:184
  105.7 0.2 reshape.165
  106.0 0.3 copy.98
  106.3 1.0 reshape.166
  107.3 5.5 %all-to-all-start.2 = ((bf16[64,2,1024]{2,1,0:T(2,128)(2,1)}), bf16[64,2,1024]{2,1,0:T(2,128)(2,1)S(1)}, u32[]{:S(2)}, u32[]{:S(2)}) async-start(bf16[64,2,1024]{2,1,0:T(2,128)(2,1)} %reshape.166), calls=%async_computation.2 | async-start | bytes 524288 | tf_op jit(solution)/shard_map/all_to_all | solution.py:186
  112.9 0.5 convert_reduce_fusion
  113.4 0.6 multiply_subtract_fusion
  114.0 9.9 %all-to-all-done.2 = bf16[64,2,1024]{2,1,0:T(2,128)(2,1)S(1)} async-done(((bf16[64,2,1024]{2,1,0:T(2,128)(2,1)}), bf16[64,2,1024]{2,1,0:T(2,128)(2,1)S(1)}, u32[]{:S(2)}, u32[]{:S(2)}) %all-to-all-start.2) | async-done | bytes 262176 | tf_op jit(solution)/shard_map/all_to_all | solution.py:186
  123.9 0.3 reshape.167
  124.2 0.1 copy.154
  124.3 0.1 copy.100
  124.4 1.1 copy.101
  (11 shorter events, 0.1 us)
Async XLA Ops:
  0.6 65.4 %copy-start = (bf16[64,64]{1,0:T(8,128)(2,1)S(1)}, bf16[64,64]{1,0:T(8,128)(2,1)}, u32[]{:S(2)}) copy-start(bf16[64,64]{1,0:T(8,128)(2,1)} %param.13) | copy-start | bytes 24580
  27.7 10.7 %copy-start.4 = (s32[8]{0:T(128)S(1)}, s32[8]{0:T(128)}, u32[]{:S(2)}) copy-start(s32[8]{0:T(128)} %param.15) | copy-start | bytes 100
  29.3 31.9 %all-to-all-start = ((bf16[64,2,3072]{2,1,0:T(2,128)(2,1)}), bf16[64,2,3072]{2,1,0:T(2,128)(2,1)S(1)}, u32[]{:S(2)}, u32[]{:S(2)}) async-start(bf16[64,2,3072]{2,1,0:T(2,128)(2,1)} %reshape.162), calls=%async_computation | async-start | bytes 1572864 | tf_op jit(solution)/shard_map/all_to_all | solution.py:37
  65.6 0.7 copy-start.5
  69.2 36.5 %all-to-all-start.1 = ((bf16[512,2,128]{2,1,0:T(2,128)(2,1)}), bf16[512,2,128]{2,1,0:T(2,128)(2,1)S(1)}, u32[]{:S(2)}, u32[]{:S(2)}) async-start(bf16[512,2,128]{2,1,0:T(2,128)(2,1)} %reshape.164), calls=%async_computation.1 | async-start | bytes 524288 | tf_op jit(solution)/shard_map/all_to_all | solution.py:184
  82.9 30.5 %copy-start.1 = (f32[4,64]{1,0:T(4,128)S(1)}, f32[4,64]{1,0:T(4,128)}, u32[]{:S(2)}) copy-start(f32[4,64]{1,0:T(4,128)} %param.10) | copy-start | bytes 3076
  82.9 30.5 %copy-start.2 = (f32[4,64]{1,0:T(4,128)S(1)}, f32[4,64]{1,0:T(4,128)}, u32[]{:S(2)}) copy-start(f32[4,64]{1,0:T(4,128)} %param.11) | copy-start | bytes 3076
  83.0 30.5 %copy-start.3 = (f32[4,64]{1,0:T(4,128)S(1)}, f32[4,64]{1,0:T(4,128)}, u32[]{:S(2)}) copy-start(f32[4,64]{1,0:T(4,128)} %param.12) | copy-start | bytes 3076
  107.3 16.6 %all-to-all-start.2 = ((bf16[64,2,1024]{2,1,0:T(2,128)(2,1)}), bf16[64,2,1024]{2,1,0:T(2,128)(2,1)S(1)}, u32[]{:S(2)}, u32[]{:S(2)}) async-start(bf16[64,2,1024]{2,1,0:T(2,128)(2,1)} %reshape.166), calls=%async_computation.2 | async-start | bytes 524288 | tf_op jit(solution)/shard_map/all_to_all | solution.py:186

commit v11 on v9

--- a/solution.py
+++ b/solution.py
@@ -181,8 +181,12 @@
     )
     grad_lines = (input_rows.astype(jnp.float32) + skip_back).astype(jnp.bfloat16)
     group_grad = lax.all_to_all(grad_tiles, "dom", 0, 0, tiled=True)
-    grad_lines, group_grad = lax.optimization_barrier((grad_lines, group_grad))
-    input_grad = lax.all_to_all(grad_lines, "dom", split_axis=2, concat_axis=3, tiled=True)
+    lines_here = grad_lines.shape[3]
+    line_tiles = grad_lines.reshape(samples, channels, slabs, slab_rows, lines_here)
+    line_tiles = jnp.moveaxis(line_tiles, 2, 0)
+    line_tiles, group_grad = lax.optimization_barrier((line_tiles, group_grad))
+    input_grad = lax.all_to_all(line_tiles, "dom", 0, 0, tiled=True)
+    input_grad = jnp.moveaxis(input_grad, 0, 3).reshape(samples, channels, slab_rows, -1)
     group_grad = group_grad.astype(jnp.float32).sum(axis=0)
     every_group = lax.all_gather(group_grad, "dp", axis=0, tiled=False)
     mine = lax.dynamic_index_in_dim(every_group, lax.axis_index("dp"), 1, keepdims=False)

time: 117 us -> 116 us (level)
  no operation moved by 1% of the time
where the time goes in v11:
time: 116 us
  blocking collectives  42.4 us (37%)
  waiting for transfers between devices  29.6 us (26%)
  starting transfers between devices  21 us (18%)
  local copies, waits for them, and re-layouts  13.3 us (11%)
  matrix products  4.47 us (4%)
  other arithmetic  4.17 us (4%)
    all_gather x1, blocking collectives, on_device(): column_low = lax.all_gather(weight_short, 'dp', axis=0, tiled=False)  22.6 us
    all_to_all x1, waiting for transfers between devices, in_one_piece(): lax.all_to_all(both, axis, split_axis=split_dim, concat_axis=concat_dim,...  20.7 us
    all_gather x1, blocking collectives, on_device(): every_group = lax.all_gather(group_grad, 'dp', axis=0, tiled=False)  19.8 us
    all_to_all x1, starting transfers between devices, in_one_piece(): lax.all_to_all(both, axis, split_axis=split_dim, concat_axis=concat_dim,...  9.02 us
    all_to_all x1, waiting for transfers between devices, on_device(): group_grad = lax.all_to_all(grad_tiles, 'dom', 0, 0, tiled=True)  8.92 us
    unnamed x19, local copies, waits for them, and re-layouts  8.1 us
    all_to_all x1, starting transfers between devices, on_device(): input_grad = lax.all_to_all(line_tiles, 'dom', 0, 0, tiled=True)  6.33 us
    all_to_all x1, starting transfers between devices, on_device(): group_grad = lax.all_to_all(grad_tiles, 'dom', 0, 0, tiled=True)  5.62 us
  transfers between devices with their start and end apart: 3, of which 2 were waited for; matrix products, arithmetic and copies ran while one was open for 4% of the time, Pallas kernels for 0%

profile of v11, /device:TPU:1, one launch (start us, length us, event | category | flops | bytes accessed | tf_op | source)
XLA Modules:
  0.0 116.0 jit_solution(6864624884709291904)
XLA Ops:
  0.6 0.0 copy-start
  0.6 0.7 convert_bitcast_fusion
  1.3 22.6 %all-gather.2 = bf16[8,4,64]{2,1,0:T(4,128)(2,1)S(1)} all-gather(bf16[1,4,64]{2,1,0:T(4,128)(2,1)S(1)} %convert_bitcast_fusion), channel_id=2, replica_groups=mesh['dp'=8,'dom'=64] {'dp'}, dimensions={0}, use_global_device_ids=true | all-gather | bytes 4608 | tf_op jit(solution)/shard_map/all_gather | solution.py:119
  24.0 0.2 broadcast_in_dim.12
  24.1 0.2 copy.66
  24.3 1.4 %copy.67 = bf16[1,64,8,256]{1,2,3,0:T(8,128)(2,1)S(1)} copy(bf16[1,64,8,256]{3,2,1,0:T(8,128)(2,1)} %param.8) | data formatting | bytes 524288 | tf_op args[0]
  25.7 1.4 %copy.68 = bf16[1,64,8,256]{1,2,3,0:T(8,128)(2,1)S(1)} copy(bf16[1,64,8,256]{3,2,1,0:T(8,128)(2,1)} %param.9) | data formatting | bytes 524288 | tf_op args[1]
  27.2 0.1 broadcast_in_dim.13
  27.3 0.4 copy_bitcast_fusion.2
  27.7 0.0 copy-start.4
  27.7 1.7 %reshape.171 = bf16[64,2,3072]{2,1,0:T(2,128)(2,1)} reshape(bf16[256,3,8,64]{3,2,1,0:T(8,128)(2,1)S(1)} %copy_bitcast_fusion.2) | data formatting | bytes 1572864
  29.3 9.0 %all-to-all-start = ((bf16[64,2,3072]{2,1,0:T(2,128)(2,1)}), bf16[64,2,3072]{2,1,0:T(2,128)(2,1)S(1)}, u32[]{:S(2)}, u32[]{:S(2)}) async-start(bf16[64,2,3072]{2,1,0:T(2,128)(2,1)} %reshape.171), calls=%async_computation | async-start | bytes 1572864 | tf_op jit(solution)/shard_map/all_to_all | solution.py:37
  38.4 0.6 dynamic_slice.7
  39.0 0.6 compare_convert_fusion
  39.6 0.7 compare_select_fusion.1
  40.3 0.1 fusion.50
  40.4 0.1 multiply_convert_fusion.1
  40.6 20.7 %all-to-all-done = bf16[64,2,3072]{2,1,0:T(2,128)(2,1)S(1)} async-done(((bf16[64,2,3072]{2,1,0:T(2,128)(2,1)}), bf16[64,2,3072]{2,1,0:T(2,128)(2,1)S(1)}, u32[]{:S(2)}, u32[]{:S(2)}) %all-to-all-start) | async-done | bytes 786464 | tf_op jit(solution)/shard_map/all_to_all | solution.py:37
  61.3 0.9 reshape.172
  62.2 0.3 copy.70
  62.5 0.3 fusion.80
  62.8 0.2 fusion.12
  63.0 1.1 copy.72
  64.1 0.2 copy.73
  64.3 0.2 copy.77
  64.5 0.2 fusion.75
  64.7 0.2 fusion.69
  64.9 0.2 fusion.24
  65.1 0.2 fusion.23
  65.3 0.3 fusion.8
  65.6 0.0 copy-start.5
  65.6 0.1 copy.154
  65.7 0.3 copy.83
  66.0 0.2 copy-done.5
  66.2 0.5 fusion.35
  66.7 0.2 convolution_bitcast_fusion.2
  66.9 0.1 fusion.51
  67.0 0.3 fusion.62
  67.3 0.3 fusion.55
  67.6 0.3 fusion.7
  67.9 0.3 fusion.6
  68.1 0.1 pad_maximum_fusion.1
  68.3 0.2 copy.155
  68.5 1.0 reshape.173
  69.5 5.6 %all-to-all-start.1 = ((bf16[64,2,1024]{2,1,0:T(2,128)(2,1)}), bf16[64,2,1024]{2,1,0:T(2,128)(2,1)S(1)}, u32[]{:S(2)}, u32[]{:S(2)}) async-start(bf16[64,2,1024]{2,1,0:T(2,128)(2,1)} %reshape.173), calls=%async_computation.1 | async-start | bytes 524288 | tf_op jit(solution)/shard_map/all_to_all | solution.py:183
  75.1 0.2 fusion.65
  75.3 0.3 fusion.20
  75.6 0.2 fusion.58
  75.8 0.3 fusion.19
  76.1 0.1 maximum_bitcast_fusion.2
  76.1 0.3 fusion.9
  76.4 0.3 fusion.3
  76.7 0.3 copy.90
  77.0 8.9 %all-to-all-done.1 = bf16[64,2,1024]{2,1,0:T(2,128)(2,1)S(1)} async-done(((bf16[64,2,1024]{2,1,0:T(2,128)(2,1)}), bf16[64,2,1024]{2,1,0:T(2,128)(2,1)S(1)}, u32[]{:S(2)}, u32[]{:S(2)}) %all-to-all-start.1) | async-done | bytes 262176 | tf_op jit(solution)/shard_map/all_to_all | solution.py:183
  85.9 0.3 reshape.174
  86.2 0.0 copy-start.2
  86.3 0.1 copy.156
  86.4 1.0 reshape.175
  87.4 6.3 %all-to-all-start.2 = ((bf16[64,2,1024]{2,1,0:T(2,128)(2,1)}), bf16[64,2,1024]{2,1,0:T(2,128)(2,1)S(1)}, u32[]{:S(2)}, u32[]{:S(2)}) async-start(bf16[64,2,1024]{2,1,0:T(2,128)(2,1)} %reshape.175), calls=%async_computation.2 | async-start | bytes 524288 | tf_op jit(solution)/shard_map/all_to_all | solution.py:188
  93.7 0.3 convert_reduce_fusion
  94.0 19.8 %all-gather.1 = f32[64,4,64]{2,1,0:T(4,128)S(1)} all-gather(f32[8,4,64]{2,1,0:T(4,128)S(1)} %convert_reduce_fusion), channel_id=3, replica_groups=mesh['dp'=8,'dom'=64] {'dp'}, dimensions={0}, use_global_device_ids=true | all-gather | bytes 73728 | tf_op jit(solution)/shard_map/all_gather | solution.py:191
  113.9 0.6 multiply_subtract_fusion
  114.5 0.3 reshape.176
  114.8 1.1 copy.101
  (13 shorter events, 0.1 us)
Async XLA Ops:
  0.6 65.4 %copy-start = (bf16[64,64]{1,0:T(8,128)(2,1)S(1)}, bf16[64,64]{1,0:T(8,128)(2,1)}, u32[]{:S(2)}) copy-start(bf16[64,64]{1,0:T(8,128)(2,1)} %param.13) | copy-start | bytes 24580
  27.7 10.7 %copy-start.4 = (s32[8]{0:T(128)S(1)}, s32[8]{0:T(128)}, u32[]{:S(2)}) copy-start(s32[8]{0:T(128)} %param.15) | copy-start | bytes 100
  29.3 31.9 %all-to-all-start = ((bf16[64,2,3072]{2,1,0:T(2,128)(2,1)}), bf16[64,2,3072]{2,1,0:T(2,128)(2,1)S(1)}, u32[]{:S(2)}, u32[]{:S(2)}) async-start(bf16[64,2,3072]{2,1,0:T(2,128)(2,1)} %reshape.171), calls=%async_computation | async-start | bytes 1572864 | tf_op jit(solution)/shard_map/all_to_all | solution.py:37
  65.6 0.7 copy-start.5
  69.5 16.4 %all-to-all-start.1 = ((bf16[64,2,1024]{2,1,0:T(2,128)(2,1)}), bf16[64,2,1024]{2,1,0:T(2,128)(2,1)S(1)}, u32[]{:S(2)}, u32[]{:S(2)}) async-start(bf16[64,2,1024]{2,1,0:T(2,128)(2,1)} %reshape.173), calls=%async_computation.1 | async-start | bytes 524288 | tf_op jit(solution)/shard_map/all_to_all | solution.py:183
  86.2 27.6 %copy-start.1 = (f32[4,64]{1,0:T(4,128)S(1)}, f32[4,64]{1,0:T(4,128)}, u32[]{:S(2)}) copy-start(f32[4,64]{1,0:T(4,128)} %param.10) | copy-start | bytes 3076
  86.2 27.6 %copy-start.2 = (f32[4,64]{1,0:T(4,128)S(1)}, f32[4,64]{1,0:T(4,128)}, u32[]{:S(2)}) copy-start(f32[4,64]{1,0:T(4,128)} %param.11) | copy-start | bytes 3076
  86.3 27.6 %copy-start.3 = (f32[4,64]{1,0:T(4,128)S(1)}, f32[4,64]{1,0:T(4,128)}, u32[]{:S(2)}) copy-start(f32[4,64]{1,0:T(4,128)} %param.12) | copy-start | bytes 3076
  87.4 27.1 %all-to-all-start.2 = ((bf16[64,2,1024]{2,1,0:T(2,128)(2,1)}), bf16[64,2,1024]{2,1,0:T(2,128)(2,1)S(1)}, u32[]{:S(2)}, u32[]{:S(2)}) async-start(bf16[64,2,1024]{2,1,0:T(2,128)(2,1)} %reshape.175), calls=%async_computation.2 | async-start | bytes 524288 | tf_op jit(solution)/shard_map/all_to_all | solution.py:188

commit v12 on v9

--- a/solution.py
+++ b/solution.py
@@ -184,9 +184,9 @@
     grad_lines, group_grad = lax.optimization_barrier((grad_lines, group_grad))
     input_grad = lax.all_to_all(grad_lines, "dom", split_axis=2, concat_axis=3, tiled=True)
     group_grad = group_grad.astype(jnp.float32).sum(axis=0)
-    every_group = lax.all_gather(group_grad, "dp", axis=0, tiled=False)
+    every_group = lax.all_gather(group_grad.astype(jnp.bfloat16), "dp", axis=0, tiled=False)
     mine = lax.dynamic_index_in_dim(every_group, lax.axis_index("dp"), 1, keepdims=False)
-    weight_grad = mine.sum(axis=0)
+    weight_grad = mine.astype(jnp.float32).sum(axis=0)
     new_moment_one = beta_first * moment_one + (1.0 - beta_first) * weight_grad
     new_moment_two = beta_second * moment_two + (1.0 - beta_second) * weight_grad * weight_grad
     first_hat = new_moment_one / (1.0 - beta_first**STEP)

time: 117 us -> 117 us (level)
  no operation moved by 1% of the time
where the time goes in v12:
time: 117 us; the launch traced here: 116 us
  blocking collectives  42.3 us (36%)
  waiting for transfers between devices  29.9 us (26%)
  starting transfers between devices  21 us (18%)
  local copies, waits for them, and re-layouts  13.4 us (11%)
  matrix products  4.47 us (4%)
  other arithmetic  4.17 us (4%)
    all_gather x1, blocking collectives, on_device(): column_low = lax.all_gather(weight_short, 'dp', axis=0, tiled=False)  22.6 us
    all_to_all x1, waiting for transfers between devices, in_one_piece(): lax.all_to_all(both, axis, split_axis=split_dim, concat_axis=concat_dim,...  20.7 us
    all_gather x1, blocking collectives, on_device(): lax.all_gather(group_grad.astype(jnp.bfloat16), 'dp', axis=0, tiled=False)  19.7 us
    all_to_all x1, waiting for transfers between devices, on_device(): group_grad = lax.all_to_all(grad_tiles, 'dom', 0, 0, tiled=True)  9.16 us
    all_to_all x1, starting transfers between devices, in_one_piece(): lax.all_to_all(both, axis, split_axis=split_dim, concat_axis=concat_dim,...  9.02 us
    unnamed x19, local copies, waits for them, and re-layouts  8.1 us
    all_to_all x1, starting transfers between devices, on_device(): lax.all_to_all(grad_lines, 'dom', split_axis=2, concat_axis=3, tiled=True)  6.33 us
    all_to_all x1, starting transfers between devices, on_device(): group_grad = lax.all_to_all(grad_tiles, 'dom', 0, 0, tiled=True)  5.62 us
  transfers between devices with their start and end apart: 3, of which 2 were waited for; matrix products, arithmetic and copies ran while one was open for 4% of the time, Pallas kernels for 0%

profile of v12, /device:TPU:1, one launch (start us, length us, event | category | flops | bytes accessed | tf_op | source)
XLA Modules:
  0.0 116.2 jit_solution(6353980044907060438)
XLA Ops:
  0.6 0.0 copy-start
  0.6 0.7 convert_bitcast_fusion
  1.3 22.6 %all-gather.2 = bf16[8,4,64]{2,1,0:T(4,128)(2,1)S(1)} all-gather(bf16[1,4,64]{2,1,0:T(4,128)(2,1)S(1)} %convert_bitcast_fusion), channel_id=2, replica_groups=mesh['dp'=8,'dom'=64] {'dp'}, dimensions={0}, use_global_device_ids=true | all-gather | bytes 4608 | tf_op jit(solution)/shard_map/all_gather | solution.py:119
  24.0 0.2 broadcast_in_dim.12
  24.1 0.2 copy.66
  24.3 1.4 %copy.67 = bf16[1,64,8,256]{1,2,3,0:T(8,128)(2,1)S(1)} copy(bf16[1,64,8,256]{3,2,1,0:T(8,128)(2,1)} %param.8) | data formatting | bytes 524288 | tf_op args[0]
  25.7 1.4 %copy.68 = bf16[1,64,8,256]{1,2,3,0:T(8,128)(2,1)S(1)} copy(bf16[1,64,8,256]{3,2,1,0:T(8,128)(2,1)} %param.9) | data formatting | bytes 524288 | tf_op args[1]
  27.2 0.1 broadcast_in_dim.13
  27.3 0.4 copy_bitcast_fusion.3
  27.7 1.7 %reshape.164 = bf16[64,2,3072]{2,1,0:T(2,128)(2,1)} reshape(bf16[256,3,8,64]{3,2,1,0:T(8,128)(2,1)S(1)} %copy_bitcast_fusion.3) | data formatting | bytes 1572864
  29.3 9.0 %all-to-all-start = ((bf16[64,2,3072]{2,1,0:T(2,128)(2,1)}), bf16[64,2,3072]{2,1,0:T(2,128)(2,1)S(1)}, u32[]{:S(2)}, u32[]{:S(2)}) async-start(bf16[64,2,3072]{2,1,0:T(2,128)(2,1)} %reshape.164), calls=%async_computation | async-start | bytes 1572864 | tf_op jit(solution)/shard_map/all_to_all | solution.py:37
  38.4 0.6 dynamic_slice.7
  39.0 0.6 compare_convert_fusion
  39.6 0.7 compare_select_fusion.1
  40.3 0.1 fusion.50
  40.4 0.1 multiply_convert_fusion.1
  40.6 20.7 %all-to-all-done = bf16[64,2,3072]{2,1,0:T(2,128)(2,1)S(1)} async-done(((bf16[64,2,3072]{2,1,0:T(2,128)(2,1)}), bf16[64,2,3072]{2,1,0:T(2,128)(2,1)S(1)}, u32[]{:S(2)}, u32[]{:S(2)}) %all-to-all-start) | async-done | bytes 786464 | tf_op jit(solution)/shard_map/all_to_all | solution.py:37
  61.3 0.9 reshape.165
  62.2 0.3 copy.70
  62.5 0.3 fusion.80
  62.8 0.2 fusion.12
  63.0 1.1 copy.72
  64.1 0.2 copy.73
  64.3 0.2 copy.77
  64.5 0.2 fusion.75
  64.7 0.2 fusion.69
  64.9 0.2 fusion.24
  65.1 0.2 fusion.23
  65.3 0.3 fusion.8
  65.6 0.1 copy.155
  65.7 0.3 copy.83
  66.0 0.2 copy-done.5
  66.2 0.5 fusion.35
  66.7 0.2 convolution_bitcast_fusion.2
  66.9 0.1 fusion.51
  67.0 0.3 fusion.62
  67.3 0.3 fusion.55
  67.6 0.3 fusion.7
  67.9 0.3 fusion.6
  68.1 0.1 pad_maximum_fusion.1
  68.3 0.2 copy.157
  68.5 1.0 reshape.166
  69.5 5.6 %all-to-all-start.1 = ((bf16[64,2,1024]{2,1,0:T(2,128)(2,1)}), bf16[64,2,1024]{2,1,0:T(2,128)(2,1)S(1)}, u32[]{:S(2)}, u32[]{:S(2)}) async-start(bf16[64,2,1024]{2,1,0:T(2,128)(2,1)} %reshape.166), calls=%async_computation.1 | async-start | bytes 524288 | tf_op jit(solution)/shard_map/all_to_all | solution.py:183
  75.1 0.2 fusion.65
  75.3 0.3 fusion.20
  75.6 0.2 fusion.58
  75.8 0.3 fusion.19
  76.1 0.1 maximum_bitcast_fusion.2
  76.1 0.3 fusion.9
  76.4 0.3 fusion.3
  76.7 0.0 copy-start.2
  76.7 0.0 copy-start.3
  76.7 9.2 %all-to-all-done.1 = bf16[64,2,1024]{2,1,0:T(2,128)(2,1)S(1)} async-done(((bf16[64,2,1024]{2,1,0:T(2,128)(2,1)}), bf16[64,2,1024]{2,1,0:T(2,128)(2,1)S(1)}, u32[]{:S(2)}, u32[]{:S(2)}) %all-to-all-start.1) | async-done | bytes 262176 | tf_op jit(solution)/shard_map/all_to_all | solution.py:183
  85.9 0.3 reshape.167
  86.2 0.3 copy.99
  86.5 1.0 reshape.168
  87.6 6.3 %all-to-all-start.2 = ((bf16[64,2,1024]{2,1,0:T(2,128)(2,1)}), bf16[64,2,1024]{2,1,0:T(2,128)(2,1)S(1)}, u32[]{:S(2)}, u32[]{:S(2)}) async-start(bf16[64,2,1024]{2,1,0:T(2,128)(2,1)} %reshape.168), calls=%async_computation.2 | async-start | bytes 524288 | tf_op jit(solution)/shard_map/all_to_all | solution.py:185
  93.9 0.3 reduce_sum.21
  94.2 19.7 %all-gather.1 = bf16[64,4,64]{2,1,0:T(4,128)(2,1)S(1)} all-gather(bf16[8,4,64]{2,1,0:T(4,128)(2,1)S(1)} %reduce_sum.21), channel_id=3, replica_groups=mesh['dp'=8,'dom'=64] {'dp'}, dimensions={0}, use_global_device_ids=true | all-gather | bytes 36864 | tf_op jit(solution)/shard_map/all_gather | solution.py:187
  113.9 0.6 multiply_subtract_fusion
  114.5 0.3 reshape.169
  114.9 0.1 copy.156
  115.0 0.1 copy.101
  115.0 1.1 copy.102
  (14 shorter events, 0.1 us)
Async XLA Ops:
  0.6 65.4 %copy-start = (bf16[64,64]{1,0:T(8,128)(2,1)S(1)}, bf16[64,64]{1,0:T(8,128)(2,1)}, u32[]{:S(2)}) copy-start(bf16[64,64]{1,0:T(8,128)(2,1)} %param.13) | copy-start | bytes 24580
  27.7 10.7 %copy-start.4 = (s32[8]{0:T(128)S(1)}, s32[8]{0:T(128)}, u32[]{:S(2)}) copy-start(s32[8]{0:T(128)} %param.15) | copy-start | bytes 100
  29.3 31.9 %all-to-all-start = ((bf16[64,2,3072]{2,1,0:T(2,128)(2,1)}), bf16[64,2,3072]{2,1,0:T(2,128)(2,1)S(1)}, u32[]{:S(2)}, u32[]{:S(2)}) async-start(bf16[64,2,3072]{2,1,0:T(2,128)(2,1)} %reshape.164), calls=%async_computation | async-start | bytes 1572864 | tf_op jit(solution)/shard_map/all_to_all | solution.py:37
  65.6 0.7 copy-start.5
  69.5 16.4 %all-to-all-start.1 = ((bf16[64,2,1024]{2,1,0:T(2,128)(2,1)}), bf16[64,2,1024]{2,1,0:T(2,128)(2,1)S(1)}, u32[]{:S(2)}, u32[]{:S(2)}) async-start(bf16[64,2,1024]{2,1,0:T(2,128)(2,1)} %reshape.166), calls=%async_computation.1 | async-start | bytes 524288 | tf_op jit(solution)/shard_map/all_to_all | solution.py:183
  76.7 37.2 %copy-start.1 = (f32[4,64]{1,0:T(4,128)S(1)}, f32[4,64]{1,0:T(4,128)}, u32[]{:S(2)}) copy-start(f32[4,64]{1,0:T(4,128)} %param.10) | copy-start | bytes 3076
  76.7 37.2 %copy-start.2 = (f32[4,64]{1,0:T(4,128)S(1)}, f32[4,64]{1,0:T(4,128)}, u32[]{:S(2)}) copy-start(f32[4,64]{1,0:T(4,128)} %param.11) | copy-start | bytes 3076
  76.7 37.2 %copy-start.3 = (f32[4,64]{1,0:T(4,128)S(1)}, f32[4,64]{1,0:T(4,128)}, u32[]{:S(2)}) copy-start(f32[4,64]{1,0:T(4,128)} %param.12) | copy-start | bytes 3076
  87.6 27.0 %all-to-all-start.2 = ((bf16[64,2,1024]{2,1,0:T(2,128)(2,1)}), bf16[64,2,1024]{2,1,0:T(2,128)(2,1)S(1)}, u32[]{:S(2)}, u32[]{:S(2)}) async-start(bf16[64,2,1024]{2,1,0:T(2,128)(2,1)} %reshape.168), calls=%async_computation.2 | async-start | bytes 524288 | tf_op jit(solution)/shard_map/all_to_all | solution.py:185
